TPU v7x, 32 devices: a whole 2x2x4 slice. The times are simulated.
32 devices in a mesh: rows: 16 (over z, y, x), rep: 2 (over core).
Axes of the slice: x: 2, y: 2, z: 4, core: 2. Of those that a mesh axis runs over, the one named last changes fastest.
Arguments:
- features: bfloat16 [4096, 256], P(('rows', 'rep')), may hold values from -6 to 6
- cotangent: bfloat16 [4096, 256], P('rows'), may hold values from -6 to 6
- weight: bfloat16 [256, 256], replicated, may hold values from -0.375 to 0.375
- tile_vals: bfloat16 [32, 2, 16, 128, 128], P('rows', 'rep'), may hold values from -0.1875 to 0.1875
- tile_cols: int32 [32, 2, 16], P('rows', 'rep'), may hold values from 0 to 15, as said below
- tile_count: int32 [32, 2], P('rows', 'rep'), may hold values from 1 to 16
Outputs:
- output: bfloat16 [4096, 256], P(('rows', 'rep'))
- weight_grad: float32 [256, 256], replicated
- feature_grad: bfloat16 [4096, 256], P(('rows', 'rep'))
Inputs may be any that keep to these rules, and one draw needn't show every extreme that they name: `tile_cols`: for each row tile and replica index the 16 entries are distinct.
All inputs are finite; a program needn't handle non-finite values.
Results may differ from a plain program's by a relative error of at most 0.0063.
Values may be sent and summed in bfloat16 or wider, within the bound.
No kernel may reach another device: no remote copies, remote signals or barrier semaphores. Data moves between devices by JAX's collectives and lax.ppermute only.
A program may use at most 64 MiB of HBM per device.

v0:
```python
import jax
import jax.numpy as jnp
from jax import lax
from jax.sharding import PartitionSpec as P

slot_group = 4


def add_sources(received):
    return jnp.sum(received, axis=0)


def local(features, cotangent, weight, tile_vals, tile_cols, tile_count):
    tile_size = tile_vals.shape[-1]
    slot_total = tile_vals.shape[2]
    panel_tiles = tile_vals.shape[0]
    block_rows = features.shape[0]
    feat_width = features.shape[1]
    values = tile_vals[:, 0]
    columns = tile_cols[:, 0]
    filled = tile_count[:, 0]
    gathered = lax.all_gather(features, "rows", axis=0, tiled=True)
    gathered_tiles = gathered.reshape(-1, tile_size, feat_width)

    def group_step(turn_index, running):
        offset = turn_index * slot_group
        part_values = lax.dynamic_slice_in_dim(values, offset, slot_group, 1)
        part_columns = lax.dynamic_slice_in_dim(columns, offset, slot_group, 1)
        is_live = (offset + jnp.arange(slot_group, dtype=jnp.int32))[None, :] < filled[:, None]
        picked = jnp.where(
            is_live[:, :, None, None], gathered_tiles[part_columns], jnp.zeros((), jnp.bfloat16)
        )
        return running + jnp.einsum(
            "tsab,tsbf->taf", part_values, picked, preferred_element_type=jnp.float32
        )

    turn_total = (jnp.max(filled) + slot_group - 1) // slot_group
    initial = jnp.zeros((panel_tiles, tile_size, feat_width), jnp.float32)
    partial_value = lax.fori_loop(0, turn_total, group_step, initial)
    partial_value = partial_value.reshape(panel_tiles * tile_size, feat_width)
    replica = lax.axis_index("rep")
    aggregated = lax.psum_scatter(partial_value, "rep", scatter_dimension=0, tiled=True).astype(
        jnp.bfloat16
    )
    upstream = lax.dynamic_slice_in_dim(cotangent, replica * block_rows, block_rows, 0)
    preact = jnp.dot(aggregated, weight, preferred_element_type=jnp.float32)
    sigmoid_part = jax.nn.sigmoid(preact)
    output = (preact * sigmoid_part).astype(jnp.bfloat16)
    grad_pre = (
        upstream.astype(jnp.float32) * sigmoid_part * (1.0 + preact * (1.0 - sigmoid_part))
    ).astype(jnp.bfloat16)
    pulled = lax.dot_general(
        grad_pre, weight, (((1,), (1,)), ((), ())), preferred_element_type=jnp.float32
    )
    output, grad_pre, pulled = (output, grad_pre, pulled.astype(jnp.bfloat16))
    pulled_panel = lax.all_gather(pulled, "rep", axis=0, tiled=True)
    local_weight = lax.dot_general(
        aggregated, grad_pre, (((0,), (0,)), ((), ())), preferred_element_type=jnp.float32
    )
    weight_grad = lax.psum(local_weight, ("rows", "rep"))
    pulled_tiles = pulled_panel.reshape(panel_tiles, tile_size, feat_width)
    is_filled = jnp.arange(slot_total, dtype=jnp.int32)[None, :] < filled[:, None]
    products = jnp.einsum(
        "tsab,taf->tsbf", values, pulled_tiles, preferred_element_type=jnp.float32
    )
    products = products.reshape(panel_tiles * slot_total, tile_size, feat_width)
    flat_columns = columns.reshape(-1)
    flat_filled = is_filled.reshape(-1)
    row_groups = lax.axis_size("rows")
    amount = row_groups * block_rows
    first_tile = 0 // tile_size
    tile_span = amount // tile_size
    relative = flat_columns - first_tile
    in_range = flat_filled & (relative >= 0) & (relative < tile_span)
    segment_ids = jnp.where(in_range, relative, tile_span)
    summed = jax.ops.segment_sum(products, segment_ids, num_segments=tile_span)
    every_term = summed.reshape(amount, feat_width).reshape(row_groups, block_rows, feat_width)
    feature_grad = add_sources(
        lax.all_to_all(every_term, "rows", split_axis=0, concat_axis=0, tiled=True)
    )
    return (output, weight_grad, feature_grad.astype(jnp.bfloat16))


def solution(mesh):
    return jax.shard_map(
        local,
        mesh=mesh,
        in_specs=(
            P(("rows", "rep"), None),
            P("rows", None),
            P(),
            P("rows", "rep", None, None, None),
            P("rows", "rep", None),
            P("rows", "rep"),
        ),
        out_specs=(P(("rows", "rep"), None), P(), P(("rows", "rep"), None)),
        check_vma=False,
    )
```

profile of v0, /device:TPU:0, one launch (start us, length us, event | category | flops | bytes accessed | tf_op | source)
XLA Modules:
  0.0 282.1 jit_solution(4228823531810199843)
XLA Ops:
  7.2 0.0 copy-start
  7.2 0.0 all-gather.2.cloned.1.call-start
  7.2 0.7 all-gather.2.cloned.1.call-update
  7.9 0.0 reduce-scatter.2.cloned.1.call-start
  8.0 1.3 reduce_max.9
  9.9 58.9 %all-gather.2.cloned.1.call-done = bf16[2048,256]{1,0:T(8,128)(2,1)} async-done(((bf16[128,256]{1,0:T(8,128)(2,1)}), bf16[2048,256]{1,0:T(8,128)(2,1)}) %all-gather.2.cloned.1.call-update) | async-done | bytes 1048592 | tf_op jit(solution)/shard_map/all_gather | solution.py:22
  68.8 0.0 copy-start.3
  68.8 14.2 %while.10 = (s32[]{:T(128)}, f32[2,128,256]{2,1,0:T(8,128)S(1)}, s32[]{:T(128)}, bf16[2,16,128,128]{3,2,1,0:T(8,128)(2,1)}, s32[2,1]{0,1:T(1,128)}, /*index=5*/s...) while((s32[]{:T(128)}, f32[2,128,256]{2,1,0:T(8,128)S(1)}, ...), condition=%wide.region_2.3_spmd, body=%wide.region_1.2_spmd.sunk | while | flops 67437608 | bytes 2363807 | solution.py:39
  68.8 0.8 compare_select_fusion.2
  69.6 0.1 reshape.144
  69.7 1.8 gather_fusion
  71.5 0.7 broadcast_compare_fusion.2
  72.3 1.3 fusion.24
  73.6 0.8 compare_select_fusion.2
  74.4 0.1 reshape.144
  74.5 1.8 gather_fusion
  76.3 0.7 broadcast_compare_fusion.2
  77.0 1.3 fusion.24
  78.3 0.8 compare_select_fusion.2
  79.1 0.1 reshape.144
  79.2 1.8 gather_fusion
  81.0 0.7 broadcast_compare_fusion.2
  81.7 1.3 fusion.24
  83.0 0.0 copy-start.1
  83.1 0.7 copy-done.1
  83.7 0.0 reduce-scatter.2.cloned.1.call-update
  83.8 0.5 broadcast.68
  84.3 1.3 reduce.4
  85.6 0.1 reshape_squeeze.3
  85.7 0.7 iota_compare_fusion
  86.4 0.1 lt.76
  86.5 8.6 %reduce-scatter.2.cloned.1.call-done = f32[128,256]{1,0:T(8,128)} async-done(((f32[256,256]{1,0:T(8,128)}), f32[128,256]{1,0:T(8,128)}) %reduce-scatter.2.cloned.1.call-update) | async-done | bytes 131088 | tf_op jit(solution)/shard_map/reduce_scatter | solution.py:42
  95.1 0.0 copy-done
  95.1 0.0 copy-done.3
  95.1 1.8 multiply_convert_fusion
  96.9 0.2 convolution_convert_fusion
  97.1 1.9 all_gather.7
  99.0 3.9 %fusion.12 = f32[2,256,16,128]{3,1,2,0:T(8,128)} fusion(bf16[2,128,256,1]{2,1,3,0:T(8,128)(2,1)S(1)} %bitcast.41, bf16[2,1,16,128,128]{4,3,2,1,0:T(8,128)(2,1)} %bitcast.40), kind=kOutput, calls=%fused_computation.25 | convolution fusion | flops 268435456 | bytes 5373952 | tf_op jit(solution)/shard_map/tsab,taf->tsbf/dot_general | solution.py:63
  102.9 5.6 %copy.11 = f32[32,128,256]{2,1,0:T(8,128)} copy(f32[32,128,256]{1,2,0:T(8,128)} %bitcast.36) | data formatting | bytes 8388608 | tf_op jit(solution)/shard_map/reshape | solution.py:66
  108.5 1.5 broadcast_in_dim.28
  110.1 9.7 %scatter_fusion = f32[16,128,256]{2,1,0:T(8,128)} fusion(f32[16,128,256]{2,1,0:T(8,128)} %broadcast_in_dim.28, s32[32]{0:T(128)S(1)} %fusion.11, f32[32,128,256]{2,1,0:T(8,128)} %copy.11), kind=kCustom, calls=%fused_computation.1 | custom fusion | flops 1048576 | bytes 12583040 | tf_op jit(solution)/shard_map/scatter-add | solution.py:76
  119.7 0.0 copy-start.2
  119.7 7.3 %all-to-all-start = ((f32[16,128,256]{2,1,0:T(8,128)}), f32[16,128,256]{2,1,0:T(8,128)S(1)}, u32[]{:S(2)}, u32[]{:S(2)}) async-start(f32[16,128,256]{2,1,0:T(8,128)} %scatter_fusion), calls=%async_computation.1 | async-start | bytes 4194304 | tf_op jit(solution)/shard_map/all_to_all | solution.py:79
  127.1 0.0 all-reduce.2.cloned.1.call-start
  127.1 0.0 copy-done.2
  127.2 0.9 fusion.7
  128.1 0.0 all-reduce.2.cloned.1.call-update
  128.1 43.0 %all-to-all-done = f32[16,128,256]{2,1,0:T(8,128)S(1)} async-done(((f32[16,128,256]{2,1,0:T(8,128)}), f32[16,128,256]{2,1,0:T(8,128)S(1)}, u32[]{:S(2)}, u32[]{:S(2)}) %all-to-all-start) | async-done | bytes 2097184 | tf_op jit(solution)/shard_map/all_to_all | solution.py:79
  171.1 0.8 reduce_sum.9
  171.8 102.0 %all-reduce.2.cloned.1.call-done = f32[256,256]{1,0:T(8,128)} async-done(((f32[256,256]{1,0:T(8,128)}), f32[256,256]{1,0:T(8,128)}) %all-reduce.2.cloned.1.call-update) | async-done | bytes 262160 | tf_op jit(solution)/shard_map/psum | solution.py:60
  273.9 1.7 copy.24
  (8 shorter events, 0.1 us)
Async XLA Ops:
  7.2 88.0 %copy-start = (bf16[256,256]{1,0:T(8,128)(2,1)S(1)}, bf16[256,256]{1,0:T(8,128)(2,1)}, u32[]{:S(2)}) copy-start(bf16[256,256]{1,0:T(8,128)(2,1)} %param.10) | copy-start | bytes 393220
  7.2 61.6 %all-gather.2.cloned.1.call-start = ((), (), s32[]{:S(2)}) async-start(), calls=%async_computation.2 | async-start | bytes 1114112 | tf_op jit(solution)/shard_map/all_gather | solution.py:22
  7.9 87.2 %reduce-scatter.2.cloned.1.call-start = ((), (), s32[]{:S(2)}) async-start(), calls=%async_computation.3 | async-start | bytes 393216 | tf_op jit(solution)/shard_map/reduce_scatter | solution.py:42
  68.8 26.3 %copy-start.3 = (bf16[256,256]{1,0:T(8,128)(2,1)S(1)}, bf16[256,256]{1,0:T(8,128)(2,1)}, u32[]{:S(2)}) copy-start(bf16[256,256]{1,0:T(8,128)(2,1)} %param.9) | copy-start | bytes 393220
  83.0 0.7 copy-start.1
  119.7 7.4 %copy-start.2 = (f32[128,256]{1,0:T(8,128)S(1)}, f32[128,256]{1,0:T(8,128)}, u32[]{:S(2)}) copy-start(f32[128,256]{1,0:T(8,128)} %reduce-scatter.2.cloned.1.call-done) | copy-start | bytes 393220
  119.7 51.3 %all-to-all-start = ((f32[16,128,256]{2,1,0:T(8,128)}), f32[16,128,256]{2,1,0:T(8,128)S(1)}, u32[]{:S(2)}, u32[]{:S(2)}) async-start(f32[16,128,256]{2,1,0:T(8,128)} %scatter_fusion), calls=%async_computation.1 | async-start | bytes 4194304 | tf_op jit(solution)/shard_map/all_to_all | solution.py:79
  127.1 146.8 %all-reduce.2.cloned.1.call-start = ((), (), s32[]{:S(2)}) async-start(), calls=%async_computation.4 | async-start | bytes 524288 | tf_op jit(solution)/shard_map/psum | solution.py:60
Sparse Core Ops, SparseCore 0:
  10.8 57.9 all-gather.1
  83.9 11.1 reduce-scatter.1
  134.9 138.8 all-reduce.1
where the time goes:
time: 284 us; the launch traced here: 282 us
  waiting for transfers between devices  213 us (75%)
  other arithmetic  18.3 us (6%)
  local copies, waits for them, and re-layouts  15.9 us (6%)
  between operations  14.5 us (5%)
  matrix products  10.7 us (4%)
  starting transfers between devices  7.45 us (3%)
    psum x1, waiting for transfers between devices, local(): weight_grad = lax.psum(local_weight, ('rows', 'rep'))  102 us
    all_gather x1, waiting for transfers between devices, local(): gathered = lax.all_gather(features, 'rows', axis=0, tiled=True)  58.9 us
    all_to_all x1, waiting for transfers between devices, local(): lax.all_to_all(every_term, 'rows', split_axis=0, concat_axis=0, tiled=True)  43 us
    scatter-add x1, other arithmetic, local(): summed = jax.ops.segment_sum(products, segment_ids, num_segments=tile_span)  9.67 us
    reduce_scatter x1, waiting for transfers between devices, local(): lax.psum_scatter(partial_value, 'rep', scatter_dimension=0, tiled=True)  8.59 us
    all_to_all x1, starting transfers between devices, local(): lax.all_to_all(every_term, 'rows', split_axis=0, concat_axis=0, tiled=True)  7.34 us
  transfers between devices with their start and end apart: 4, of which 4 were waited for; matrix products, arithmetic and copies ran while one was open for 2% of the time, Pallas kernels for 0%

commit v1 on v0

v1 whole, which is shorter than its diff:
```python
import jax
import jax.numpy as jnp
from jax import lax
from jax.sharding import PartitionSpec as P


def bit_count(n):
    return n.bit_length() - 1


def position_of(j, order):
    pos = 0
    for k, b in enumerate(order):
        pos = pos + (((j >> b) & 1) << k)
    return pos


def doubling_gather(x, axis, n, order):
    me = lax.axis_index(axis)
    buf = x[None]
    for b in order:
        pairs = [(j, j ^ (1 << b)) for j in range(n)]
        got = lax.ppermute(buf, axis, pairs)
        low = ((me >> b) & 1) == 0
        buf = jnp.where(low, jnp.concatenate([buf, got]), jnp.concatenate([got, buf]))
    return buf


def halving_scatter(buf, axis, n, order, send_dtype):
    me = lax.axis_index(axis)
    nb = bit_count(n)
    cur = buf.reshape((2,) * nb + buf.shape[1:]).astype(jnp.float32)
    axes_bits = list(range(nb - 1, -1, -1))
    for b in order:
        ax = axes_bits.index(b)
        mine = (me >> b) & 1
        keep = lax.dynamic_index_in_dim(cur, mine, ax, keepdims=False)
        send = lax.dynamic_index_in_dim(cur, 1 - mine, ax, keepdims=False)
        pairs = [(j, j ^ (1 << b)) for j in range(n)]
        got = lax.ppermute(send.astype(send_dtype), axis, pairs)
        cur = keep + got.astype(jnp.float32)
        axes_bits.pop(ax)
    return cur.reshape(buf.shape[1:])


def local(features, cotangent, weight, tile_vals, tile_cols, tile_count):
    n_rows = lax.axis_size("rows")
    n_rep = lax.axis_size("rep")
    tile = tile_vals.shape[-1]
    slots = tile_vals.shape[2]
    panel_tiles = tile_vals.shape[0]
    block_rows = features.shape[0]
    feat_width = features.shape[1]
    rep_bits = list(range(bit_count(n_rep)))
    row_bits = list(range(bit_count(n_rows)))
    me_rep = lax.axis_index("rep")

    values = tile_vals[:, 0]
    columns = tile_cols[:, 0]
    filled = tile_count[:, 0]
    col_tiles = n_rows * (block_rows // tile)

    is_live = jnp.arange(slots, dtype=jnp.int32)[None, :] < filled[:, None]
    picks = (columns[:, :, None] == jnp.arange(col_tiles, dtype=jnp.int32)[None, None, :]) & is_live[:, :, None]
    sorted_vals = jnp.einsum(
        "tsq,tsab->tqab", picks.astype(jnp.bfloat16), values, preferred_element_type=jnp.bfloat16
    )

    gather_order = row_bits[::-1]
    gathered = doubling_gather(features, "rows", n_rows, gather_order)
    natural = jnp.array([position_of(j, gather_order) for j in range(n_rows)], jnp.int32)
    gathered = jnp.take(gathered, natural, axis=0)
    partial_value = jnp.einsum(
        "tqab,qbf->taf", sorted_vals, gathered, preferred_element_type=jnp.float32
    )
    aggregated = halving_scatter(partial_value, "rep", n_rep, rep_bits, jnp.float32).astype(jnp.bfloat16)

    upstream = lax.dynamic_slice_in_dim(cotangent, me_rep * block_rows, block_rows, 0)
    preact = jnp.dot(aggregated, weight, preferred_element_type=jnp.float32)
    sigmoid_part = jax.nn.sigmoid(preact)
    output = (preact * sigmoid_part).astype(jnp.bfloat16)
    grad_pre = (
        upstream.astype(jnp.float32) * sigmoid_part * (1.0 + preact * (1.0 - sigmoid_part))
    ).astype(jnp.bfloat16)
    pulled = lax.dot_general(
        grad_pre, weight, (((1,), (1,)), ((), ())), preferred_element_type=jnp.float32
    ).astype(jnp.bfloat16)
    pulled_panel = doubling_gather(pulled, "rep", n_rep, rep_bits)
    local_weight = lax.dot_general(
        aggregated, grad_pre, (((0,), (0,)), ((), ())), preferred_element_type=jnp.float32
    )

    w_half = halving_scatter(
        local_weight.reshape(n_rep, feat_width // n_rep, feat_width), "rep", n_rep, rep_bits, jnp.float32
    )
    w_rows = w_half.shape[0] // n_rows
    w_pieces = w_half.reshape(n_rows, w_rows, feat_width)

    products = jnp.einsum(
        "tqab,taf->qbf", sorted_vals, pulled_panel, preferred_element_type=jnp.float32
    )
    products = products.reshape(n_rows, block_rows, feat_width)
    packed = jnp.concatenate([products, w_pieces], axis=1).astype(jnp.bfloat16)
    received = lax.all_to_all(packed, "rows", 0, 0, tiled=True)
    summed = jnp.sum(received.astype(jnp.float32), axis=0)
    feature_grad = summed[:block_rows].astype(jnp.bfloat16)
    w_mine = summed[block_rows:]

    w_rows_all = doubling_gather(w_mine, "rows", n_rows, row_bits)
    w_rep_all = doubling_gather(w_rows_all.reshape(-1, feat_width), "rep", n_rep, rep_bits)
    weight_grad = w_rep_all.reshape(feat_width, feat_width)
    return (output, weight_grad, feature_grad)


def solution(mesh):
    return jax.shard_map(
        local,
        mesh=mesh,
        in_specs=(
            P(("rows", "rep"), None),
            P("rows", None),
            P(),
            P("rows", "rep", None, None, None),
            P("rows", "rep", None),
            P("rows", "rep"),
        ),
        out_specs=(P(("rows", "rep"), None), P(), P(("rows", "rep"), None)),
        check_vma=False,
    )
```

time: 284 us -> 99 us (0.35)
  waiting for transfers between devices: 213 us -> 38.3 us
  blocking collectives: 1.9 us -> 37.9 us
  other arithmetic: 18.3 us -> 3.91 us
  between operations: 14.5 us -> 0.85 us
  local copies, waits for them, and re-layouts: 15.9 us -> 2.31 us
  matrix products: 10.7 us -> 4.22 us
  starting transfers between devices: 7.45 us -> 11.3 us
    psum x1 -> x0, waiting for transfers between devices: 102 us -> none  [local(): weight_grad = lax.psum(local_weight, ('rows', 'rep'))]
    all_gather x1 -> x0, waiting for transfers between devices: 58.9 us -> none  [local(): gathered = lax.all_gather(features, 'rows', axis=0, tiled=True)]
    all_to_all x1 -> x0, waiting for transfers between devices: 43 us -> none  [local(): lax.all_to_all(every_term, 'rows', split_axis=0, concat_axis=0, tiled=True)]
    ppermute x0 -> x12, waiting for transfers between devices: none -> 38.3 us  [the longest x10 36.9 us: doubling_gather(): got = lax.ppermute(buf, axis, pairs)]
    all_to_all x0 -> x1, blocking collectives: none -> 37.9 us  [local(): received = lax.all_to_all(packed, 'rows', 0, 0, tiled=True)]
    ppermute x0 -> x12, starting transfers between devices: none -> 11.3 us  [the longest x10 10.8 us: doubling_gather(): got = lax.ppermute(buf, axis, pairs)]
    scatter-add x1 -> x0, other arithmetic: 9.67 us -> none  [local(): summed = jax.ops.segment_sum(products, segment_ids, num_segments=tile_span)]
    reduce_scatter x1 -> x0, waiting for transfers between devices: 8.59 us -> none  [local(): lax.psum_scatter(partial_value, 'rep', scatter_dimension=0, tiled=True)]
  transfers between devices with their start and end apart: 4 -> 12, of which waited for: 4 -> 11; matrix products, arithmetic and copies ran while one was open for 2% -> 2% of each run, Pallas kernels for 0% -> 0%
where the time goes in v1:
time: 99 us; the launch traced here: 98.8 us
  waiting for transfers between devices  38.3 us (39%)
  blocking collectives  37.9 us (38%)
  starting transfers between devices  11.3 us (11%)
  matrix products  4.22 us (4%)
  other arithmetic  3.91 us (4%)
  local copies, waits for them, and re-layouts  2.31 us (2%)
    all_to_all x1, blocking collectives, local(): received = lax.all_to_all(packed, 'rows', 0, 0, tiled=True)  37.9 us
    ppermute x10, waiting for transfers between devices, doubling_gather(): got = lax.ppermute(buf, axis, pairs)  36.9 us
    ppermute x10, starting transfers between devices, doubling_gather(): got = lax.ppermute(buf, axis, pairs)  10.8 us
    select_n x9, other arithmetic, doubling_gather(): jnp.where(low, jnp.concatenate([buf, got]), jnp.concatenate([got, buf]))  3.57 us
  transfers between devices with their start and end apart: 12, of which 11 were waited for; matrix products, arithmetic and copies ran while one was open for 2% of the time, Pallas kernels for 0%

profile of v1, /device:TPU:0, one launch (start us, length us, event | category | flops | bytes accessed | tf_op | source)
XLA Modules:
  0.0 98.8 jit_solution(16558247839359897814)
XLA Ops:
  0.6 0.0 copy-start
  0.6 0.0 copy-start.4
  0.7 0.0 copy-start.6
  0.7 0.0 copy-start.3
  0.7 4.1 %collective-permute-start = (bf16[1,128,256]{2,1,0:T(8,128)(2,1)}, bf16[1,128,256]{2,1,0:T(8,128)(2,1)S(1)}, u32[]{:S(2)}, u32[]{:S(2)}) collective-permute-start(bf16[1,128,256]{2,1,0:T(8,128)(2,1)} %bitcast.55), channel_id=1, source_target_pairs={{0,16},{2,18},{4,20},{6,22},{8,24},{10,26},{12,28},{14,30},{16,0},... | collective-permute-start | bytes 196616 | tf_op jit(solution)/shard_map/ppermute | solution.py:23
  4.8 3.9 %collective-permute-done = bf16[1,128,256]{2,1,0:T(8,128)(2,1)S(1)} collective-permute-done((bf16[1,128,256]{2,1,0:T(8,128)(2,1)}, bf16[1,128,256]{2,1,0:T(8,128)(2,1)S(1)}, u32[]{:S(2)}, u32[]{:S(2)}) %collective-permute-start) | collective-permute-done | bytes 65568 | tf_op jit(solution)/shard_map/ppermute | solution.py:23
  8.6 0.9 maximum_select_fusion.4
  9.6 0.7 collective-permute-start.1
  10.3 4.3 %collective-permute-done.1 = bf16[2,128,256]{2,1,0:T(8,128)(2,1)S(1)} collective-permute-done((bf16[2,128,256]{2,1,0:T(8,128)(2,1)S(1)}, bf16[2,128,256]{2,1,0:T(8,128)(2,1)S(1)}, u32[]{:S(2)}, u32[]{:S(2)}) %collective-permute-start.1) | collective-permute-done | bytes 131104 | tf_op jit(solution)/shard_map/ppermute | solution.py:23
  14.6 1.8 %collective-permute-start.2 = (bf16[4,128,256]{2,1,0:T(8,128)(2,1)S(1)}, bf16[4,128,256]{2,1,0:T(8,128)(2,1)S(1)}, u32[]{:S(2)}, u32[]{:S(2)}) collective-permute-start(bf16[4,128,256]{2,1,0:T(8,128)(2,1)S(1)} %maximum_select_fusion.2), channel_id=1, source_target_pairs={{0,4},{2,6},{4,0},{6,2},{8,12},{10,14},{12,8},{14,10},{16,20},{18,... | collective-permute-start | bytes 786440 | tf_op jit(solution)/shard_map/ppermute | solution.py:23
  16.4 4.6 %collective-permute-done.2 = bf16[4,128,256]{2,1,0:T(8,128)(2,1)S(1)} collective-permute-done((bf16[4,128,256]{2,1,0:T(8,128)(2,1)S(1)}, bf16[4,128,256]{2,1,0:T(8,128)(2,1)S(1)}, u32[]{:S(2)}, u32[]{:S(2)}) %collective-permute-start.2) | collective-permute-done | bytes 262176 | tf_op jit(solution)/shard_map/ppermute | solution.py:23
  21.1 0.1 maximum_select_fusion.1
  21.2 0.0 copy-start.1
  21.2 1.8 %collective-permute-start.3 = (bf16[8,128,256]{2,1,0:T(8,128)(2,1)S(1)}, bf16[8,128,256]{2,1,0:T(8,128)(2,1)}, u32[]{:S(2)}, u32[]{:S(2)}) collective-permute-start(bf16[8,128,256]{2,1,0:T(8,128)(2,1)S(1)} %maximum_select_fusion.1), channel_id=1, source_target_pairs={{0,2},{2,0},{4,6},{6,4},{8,10},{10,8},{12,14},{14,12},{16,18},{18,... | collective-permute-start | bytes 1572872 | tf_op jit(solution)/shard_map/ppermute | solution.py:23
  22.9 0.0 copy-done.4
  23.0 0.0 copy-done.6
  23.0 0.1 iota_compare_fusion.1
  23.0 0.0 copy-done
  23.0 0.0 copy-done.3
  23.0 0.7 fusion.4
  23.8 0.0 copy-done.1
  23.8 7.5 %collective-permute-done.3 = bf16[8,128,256]{2,1,0:T(8,128)(2,1)} collective-permute-done((bf16[8,128,256]{2,1,0:T(8,128)(2,1)S(1)}, bf16[8,128,256]{2,1,0:T(8,128)(2,1)}, u32[]{:S(2)}, u32[]{:S(2)}) %collective-permute-start.3) | collective-permute-done | bytes 524320 | tf_op jit(solution)/shard_map/ppermute | solution.py:23
  31.3 1.8 %maximum_select_fusion = bf16[16,128,256]{2,1,0:T(8,128)(2,1)S(1)} fusion(bf16[8,128,256]{2,1,0:T(8,128)(2,1)} %collective-permute-done.3, bf16[8,128,256]{2,1,0:T(8,128)(2,1)} %copy-done.1, pred[]{:T(512)S(6)} %eq.39), kind=kLoop, calls=%fused_computation.7 | loop fusion | flops 1572864 | bytes 2097153 | tf_op jit(solution)/shard_map/jit(_where)/select_n | solution.py:25
  33.1 1.6 %gather_fusion = bf16[16,128,256]{2,1,0:T(8,128)(2,1)} fusion(bf16[16,128,256]{2,1,0:T(8,128)(2,1)S(1)} %maximum_select_fusion, s32[1024]{0:T(1024)S(1)} %pad_clamp_fusion), kind=kCustom, calls=%fused_computation | custom fusion | bytes 2097216 | tf_op jit(solution)/shard_map/jit(_take)/gather | solution.py:72
  34.7 0.0 copy-start.2
  34.7 0.0 copy-start.5
  34.7 1.7 %convolution_bitcast_fusion = f32[2,128,256]{2,1,0:T(8,128)S(1)} fusion(bf16[16,128,256]{2,1,0:T(8,128)(2,1)} %gather_fusion, bf16[2,16,128,128]{3,1,2,0:T(8,128)(2,1)S(1)} %fusion.4), kind=kOutput, calls=%fused_computation.3 | convolution fusion | flops 268435456 | bytes 2359296 | tf_op jit(solution)/shard_map/tqab,qbf->taf/dot_general | solution.py:73
  36.5 0.1 collective-permute-start.4
  36.5 1.3 %collective-permute-done.4 = f32[128,256]{1,0:T(8,128)S(1)} collective-permute-done((f32[128,256]{1,0:T(8,128)S(1)}, f32[128,256]{1,0:T(8,128)S(1)}, u32[]{:S(2)}, u32[]{:S(2)}) %collective-permute-start.4) | collective-permute-done | bytes 131104 | tf_op jit(solution)/shard_map/ppermute | solution.py:40
  37.9 0.0 copy-done.2
  37.9 0.0 copy-done.5
  37.9 0.9 multiply_convert_fusion
  38.8 0.2 fusion.24
  39.0 0.2 fusion
  39.2 0.2 collective-permute-start.5
  39.4 0.4 collective-permute-start.6
  39.8 0.7 collective-permute-done.5
  40.5 0.5 bitcast_convert_fusion
  41.0 0.0 collective-permute-done.6
  41.1 0.1 pad_maximum_fusion
  41.1 37.9 %all_to_all.5 = bf16[16,136,256]{2,1,0:T(8,128)(2,1)S(1)} all-to-all(bf16[16,136,256]{2,1,0:T(8,128)(2,1)S(1)} %pad_maximum_fusion), channel_id=1, replica_groups=mesh['rows'=16,'rep'=2] {'rows'}, dimensions={0} | all-to-all | bytes 2228224 | tf_op jit(solution)/shard_map/all_to_all | solution.py:104
  79.0 0.1 convert_reduce_fusion
  79.2 0.6 collective-permute-start.7
  79.8 3.1 %collective-permute-done.7 = f32[1,8,256]{2,1,0:T(8,128)S(1)} collective-permute-done((f32[1,8,256]{2,1,0:T(8,128)S(1)}, f32[1,8,256]{2,1,0:T(8,128)S(1)}, u32[]{:S(2)}, u32[]{:S(2)}) %collective-permute-start.7) | collective-permute-done | bytes 8224 | tf_op jit(solution)/shard_map/ppermute | solution.py:23
  82.9 0.6 collective-permute-start.8
  83.5 3.1 %collective-permute-done.8 = f32[2,8,256]{2,1,0:T(8,128)S(1)} collective-permute-done((f32[2,8,256]{2,1,0:T(8,128)S(1)}, f32[2,8,256]{2,1,0:T(8,128)S(1)}, u32[]{:S(2)}, u32[]{:S(2)}) %collective-permute-start.8) | collective-permute-done | bytes 16416 | tf_op jit(solution)/shard_map/ppermute | solution.py:23
  86.7 0.7 collective-permute-start.9
  87.3 3.7 %collective-permute-done.9 = f32[4,8,256]{2,1,0:T(8,128)S(1)} collective-permute-done((f32[4,8,256]{2,1,0:T(8,128)S(1)}, f32[4,8,256]{2,1,0:T(8,128)S(1)}, u32[]{:S(2)}, u32[]{:S(2)}) %collective-permute-start.9) | collective-permute-done | bytes 32800 | tf_op jit(solution)/shard_map/ppermute | solution.py:23
  91.0 0.3 collective-permute-start.10
  91.2 5.4 %collective-permute-done.10 = f32[8,8,256]{2,1,0:T(8,128)S(1)} collective-permute-done((f32[8,8,256]{2,1,0:T(8,128)S(1)}, f32[8,8,256]{2,1,0:T(8,128)S(1)}, u32[]{:S(2)}, u32[]{:S(2)}) %collective-permute-start.10) | collective-permute-done | bytes 65568 | tf_op jit(solution)/shard_map/ppermute | solution.py:23
  96.6 0.1 collective-permute-start.11
  96.7 0.6 slice.15
  97.3 0.7 collective-permute-done.11
  98.0 0.7 maximum_select_fusion.3
  (11 shorter events, 0.1 us)
Async XLA Ops:
  0.6 22.4 %copy-start = (bf16[2,1,16,128,128]{4,3,2,1,0:T(8,128)(2,1)S(1)}, bf16[2,1,16,128,128]{4,3,2,1,0:T(8,128)(2,1)}, u32[]{:S(2)}) copy-start(bf16[2,1,16,128,128]{4,3,2,1,0:T(8,128)(2,1)} %param.10) | copy-start | bytes 3145732
  0.6 22.3 %copy-start.4 = (s32[16]{0:T(128)S(1)}, s32[16]{0:T(128)}, u32[]{:S(2)}) copy-start(s32[16]{0:T(128)} %constant.64) | copy-start | bytes 196
  0.7 22.3 %copy-start.6 = (s32[2,1]{0,1:T(1,128)S(1)}, s32[2,1]{0,1:T(1,128)}, u32[]{:S(2)}) copy-start(s32[2,1]{0,1:T(1,128)} %param.12) | copy-start | bytes 28
  0.7 22.4 %copy-start.3 = (s32[2,1,16]{2,1,0:T(1,128)S(1)}, s32[2,1,16]{2,1,0:T(1,128)}, u32[]{:S(2)}) copy-start(s32[2,1,16]{2,1,0:T(1,128)} %param.11) | copy-start | bytes 388
  0.7 8.0 %collective-permute-start = (bf16[1,128,256]{2,1,0:T(8,128)(2,1)}, bf16[1,128,256]{2,1,0:T(8,128)(2,1)S(1)}, u32[]{:S(2)}, u32[]{:S(2)}) collective-permute-start(bf16[1,128,256]{2,1,0:T(8,128)(2,1)} %bitcast.55), channel_id=1, source_target_pairs={{0,16},{2,18},{4,20},{6,22},{8,24},{10,26},{12,28},{14,30},{16,0},... | collective-permute-start | bytes 196616 | tf_op jit(solution)/shard_map/ppermute | solution.py:23
  9.6 5.0 %collective-permute-start.1 = (bf16[2,128,256]{2,1,0:T(8,128)(2,1)S(1)}, bf16[2,128,256]{2,1,0:T(8,128)(2,1)S(1)}, u32[]{:S(2)}, u32[]{:S(2)}) collective-permute-start(bf16[2,128,256]{2,1,0:T(8,128)(2,1)S(1)} %maximum_select_fusion.4), channel_id=1, source_target_pairs={{0,8},{2,10},{4,12},{6,14},{8,0},{10,2},{12,4},{14,6},{16,24},{18,... | collective-permute-start | bytes 393224 | tf_op jit(solution)/shard_map/ppermute | solution.py:23
  14.6 6.4 %collective-permute-start.2 = (bf16[4,128,256]{2,1,0:T(8,128)(2,1)S(1)}, bf16[4,128,256]{2,1,0:T(8,128)(2,1)S(1)}, u32[]{:S(2)}, u32[]{:S(2)}) collective-permute-start(bf16[4,128,256]{2,1,0:T(8,128)(2,1)S(1)} %maximum_select_fusion.2), channel_id=1, source_target_pairs={{0,4},{2,6},{4,0},{6,2},{8,12},{10,14},{12,8},{14,10},{16,20},{18,... | collective-permute-start | bytes 786440 | tf_op jit(solution)/shard_map/ppermute | solution.py:23
  21.2 2.6 %copy-start.1 = (bf16[8,128,256]{2,1,0:T(8,128)(2,1)}, bf16[8,128,256]{2,1,0:T(8,128)(2,1)S(1)}, u32[]{:S(2)}) copy-start(bf16[8,128,256]{2,1,0:T(8,128)(2,1)S(1)} %maximum_select_fusion.1) | copy-start | bytes 1572868
  21.2 10.2 %collective-permute-start.3 = (bf16[8,128,256]{2,1,0:T(8,128)(2,1)S(1)}, bf16[8,128,256]{2,1,0:T(8,128)(2,1)}, u32[]{:S(2)}, u32[]{:S(2)}) collective-permute-start(bf16[8,128,256]{2,1,0:T(8,128)(2,1)S(1)} %maximum_select_fusion.1), channel_id=1, source_target_pairs={{0,2},{2,0},{4,6},{6,4},{8,10},{10,8},{12,14},{14,12},{16,18},{18,... | collective-permute-start | bytes 1572872 | tf_op jit(solution)/shard_map/ppermute | solution.py:23
  34.7 3.2 %copy-start.2 = (bf16[256,256]{1,0:T(8,128)(2,1)S(1)}, bf16[256,256]{1,0:T(8,128)(2,1)}, u32[]{:S(2)}) copy-start(bf16[256,256]{1,0:T(8,128)(2,1)} %param.9) | copy-start | bytes 393220
  34.7 3.2 %copy-start.5 = (bf16[256,256]{1,0:T(8,128)(2,1)S(1)}, bf16[256,256]{1,0:T(8,128)(2,1)}, u32[]{:S(2)}) copy-start(bf16[256,256]{1,0:T(8,128)(2,1)} %param.8) | copy-start | bytes 393220
  36.5 1.4 %collective-permute-start.4 = (f32[128,256]{1,0:T(8,128)S(1)}, f32[128,256]{1,0:T(8,128)S(1)}, u32[]{:S(2)}, u32[]{:S(2)}) collective-permute-start(f32[128,256]{1,0:T(8,128)S(1)} %dynamic-slice_bitcast_fusion.1), channel_id=1, source_target_pairs={{0,1},{1,0},{2,3},{3,2},{4,5},{5,4},{6,7},{7,6},{8,9},{9,8},{10,11... | collective-permute-start | bytes 393224 | tf_op jit(solution)/shard_map/ppermute | solution.py:40
  39.2 1.3 %collective-permute-start.5 = (bf16[1,128,256]{2,1,0:T(8,128)(2,1)S(1)}, bf16[1,128,256]{2,1,0:T(8,128)(2,1)S(1)}, u32[]{:S(2)}, u32[]{:S(2)}) collective-permute-start(bf16[1,128,256]{2,1,0:T(8,128)(2,1)S(1)} %fusion), channel_id=1, source_target_pairs={{0,1},{1,0},{2,3},{3,2},{4,5},{5,4},{6,7},{7,6},{8,9},{9,8},{10,11... | collective-permute-start | bytes 196616 | tf_op jit(solution)/shard_map/ppermute | solution.py:23
  39.4 1.6 %collective-permute-start.6 = (f32[128,256]{1,0:T(8,128)S(1)}, f32[128,256]{1,0:T(8,128)S(1)}, u32[]{:S(2)}, u32[]{:S(2)}) collective-permute-start(f32[128,256]{1,0:T(8,128)S(1)} %dynamic-slice_bitcast_fusion), channel_id=1, source_target_pairs={{0,1},{1,0},{2,3},{3,2},{4,5},{5,4},{6,7},{7,6},{8,9},{9,8},{10,11... | collective-permute-start | bytes 393224 | tf_op jit(solution)/shard_map/ppermute | solution.py:40
  79.2 3.7 %collective-permute-start.7 = (f32[1,8,256]{2,1,0:T(8,128)S(1)}, f32[1,8,256]{2,1,0:T(8,128)S(1)}, u32[]{:S(2)}, u32[]{:S(2)}) collective-permute-start(f32[1,8,256]{2,1,0:T(8,128)S(1)} %slice_bitcast_fusion), channel_id=1, source_target_pairs={{0,2},{2,0},{4,6},{6,4},{8,10},{10,8},{12,14},{14,12},{16,18},{18,... | collective-permute-start | bytes 24584 | tf_op jit(solution)/shard_map/ppermute | solution.py:23
  82.9 3.7 %collective-permute-start.8 = (f32[2,8,256]{2,1,0:T(8,128)S(1)}, f32[2,8,256]{2,1,0:T(8,128)S(1)}, u32[]{:S(2)}, u32[]{:S(2)}) collective-permute-start(f32[2,8,256]{2,1,0:T(8,128)S(1)} %maximum_select_fusion.9), channel_id=1, source_target_pairs={{0,4},{2,6},{4,0},{6,2},{8,12},{10,14},{12,8},{14,10},{16,20},{18,... | collective-permute-start | bytes 49160 | tf_op jit(solution)/shard_map/ppermute | solution.py:23
  86.7 4.3 %collective-permute-start.9 = (f32[4,8,256]{2,1,0:T(8,128)S(1)}, f32[4,8,256]{2,1,0:T(8,128)S(1)}, u32[]{:S(2)}, u32[]{:S(2)}) collective-permute-start(f32[4,8,256]{2,1,0:T(8,128)S(1)} %maximum_select_fusion.8), channel_id=1, source_target_pairs={{0,8},{2,10},{4,12},{6,14},{8,0},{10,2},{12,4},{14,6},{16,24},{18,... | collective-permute-start | bytes 98312 | tf_op jit(solution)/shard_map/ppermute | solution.py:23
  91.0 5.6 %collective-permute-start.10 = (f32[8,8,256]{2,1,0:T(8,128)S(1)}, f32[8,8,256]{2,1,0:T(8,128)S(1)}, u32[]{:S(2)}, u32[]{:S(2)}) collective-permute-start(f32[8,8,256]{2,1,0:T(8,128)S(1)} %maximum_select_fusion.7), channel_id=1, source_target_pairs={{0,16},{2,18},{4,20},{6,22},{8,24},{10,26},{12,28},{14,30},{16,0},... | collective-permute-start | bytes 196616 | tf_op jit(solution)/shard_map/ppermute | solution.py:23
  96.6 1.4 %collective-permute-start.11 = (f32[1,128,256]{2,1,0:T(8,128)S(1)}, f32[1,128,256]{2,1,0:T(8,128)S(1)}, u32[]{:S(2)}, u32[]{:S(2)}) collective-permute-start(f32[1,128,256]{2,1,0:T(8,128)S(1)} %fusion.13), channel_id=1, source_target_pairs={{0,1},{1,0},{2,3},{3,2},{4,5},{5,4},{6,7},{7,6},{8,9},{9,8},{10,11... | collective-permute-start | bytes 393224 | tf_op jit(solution)/shard_map/ppermute | solution.py:23

commit v2 on v1

v2 whole, which is shorter than its diff:
```python
import jax
import jax.numpy as jnp
from jax import lax
from jax.sharding import PartitionSpec as P


def bit_count(n):
    return n.bit_length() - 1


def pairs_of(n, b):
    return [(j, j ^ (1 << b)) for j in range(n)]


def bit_slices(shape_bits, fixed):
    nb = len(shape_bits)
    return tuple(slice(*fixed.get(nb - 1 - k, (0, 2))) for k in range(nb))


def gather_contract(x_part, sorted_rel, order, n):
    nb = bit_count(n)
    t_count, a_size = sorted_rel.shape[0], sorted_rel.shape[-2]
    held = x_part.reshape((1,) * nb + x_part.shape)
    own = sorted_rel[(slice(None),) + (0,) * nb]
    acc = jnp.einsum("tab,bf->taf", own, x_part, preferred_element_type=jnp.float32)
    done = []
    for step, b in enumerate(order):
        got = lax.ppermute(held, "rows", pairs_of(n, b))
        fixed = {bb: (0, 1) for bb in range(nb) if bb not in done}
        fixed[b] = (1, 2)
        tiles = sorted_rel[(slice(None),) + bit_slices(range(nb), fixed)]
        tiles = tiles.reshape(t_count, -1, a_size, tiles.shape[-1])
        acc = acc + jnp.einsum(
            "tmab,mbf->taf", tiles, got.reshape((-1,) + x_part.shape), preferred_element_type=jnp.float32
        )
        done.append(b)
        if step + 1 < len(order):
            held = jnp.concatenate([held, got], axis=nb - 1 - b)
    return acc


def halving_scatter(rel, order, n, send_dtype):
    nb = bit_count(n)
    cur = rel
    axes_bits = list(range(nb - 1, -1, -1))
    for b in order:
        ax = axes_bits.index(b)
        keep = lax.index_in_dim(cur, 0, ax, keepdims=False)
        send = lax.index_in_dim(cur, 1, ax, keepdims=False)
        got = lax.ppermute(send.astype(send_dtype), "rows", pairs_of(n, b))
        cur = keep + got.astype(jnp.float32)
        axes_bits.pop(ax)
    return cur


def doubling_sum(x, axis, n, order):
    for b in order:
        x = x + lax.ppermute(x, axis, pairs_of(n, b))
    return x


def doubling_gather(x, axis, n):
    me = lax.axis_index(axis)
    buf = x[None]
    for b in range(bit_count(n)):
        got = lax.ppermute(buf, axis, pairs_of(n, b))
        low = ((me >> b) & 1) == 0
        buf = jnp.where(low, jnp.concatenate([buf, got]), jnp.concatenate([got, buf]))
    return buf


def local(features, cotangent, weight, tile_vals, tile_cols, tile_count):
    n_rows = lax.axis_size("rows")
    n_rep = lax.axis_size("rep")
    tile = tile_vals.shape[-1]
    slots = tile_vals.shape[2]
    panel_tiles = tile_vals.shape[0]
    block_rows = features.shape[0]
    feat_width = features.shape[1]
    nb = bit_count(n_rows)
    rep_bits = list(range(bit_count(n_rep)))
    me_rep = lax.axis_index("rep")
    me_rows = lax.axis_index("rows")

    values = tile_vals[:, 0]
    columns = tile_cols[:, 0]
    filled = tile_count[:, 0]

    is_live = jnp.arange(slots, dtype=jnp.int32)[None, :] < filled[:, None]
    relative = jnp.bitwise_xor(columns, me_rows)
    picks = (relative[:, :, None] == jnp.arange(n_rows, dtype=jnp.int32)[None, None, :]) & is_live[:, :, None]
    sorted_rel = jnp.einsum(
        "tsq,tsab->tqab", picks.astype(jnp.bfloat16), values, preferred_element_type=jnp.bfloat16
    )
    sorted_rel = sorted_rel.reshape((panel_tiles,) + (2,) * nb + (tile, tile))

    down = list(range(nb - 1, -1, -1))
    gather_orders = [down, down[:-2] + [down[-1], down[-2]]]
    width = feat_width // len(gather_orders)
    partial_value = jnp.concatenate(
        [
            gather_contract(features[:, k * width:(k + 1) * width], sorted_rel, order, n_rows)
            for k, order in enumerate(gather_orders)
        ],
        axis=-1,
    )
    panel_sum = doubling_sum(partial_value, "rep", n_rep, rep_bits)
    aggregated = panel_sum.reshape(panel_tiles * tile, feat_width).astype(jnp.bfloat16)

    preact = jnp.dot(aggregated, weight, preferred_element_type=jnp.float32)
    sigmoid_part = jax.nn.sigmoid(preact)
    output = (preact * sigmoid_part).astype(jnp.bfloat16)
    output = lax.dynamic_slice_in_dim(output, me_rep * block_rows, block_rows, 0)
    grad_pre = (
        cotangent.astype(jnp.float32) * sigmoid_part * (1.0 + preact * (1.0 - sigmoid_part))
    ).astype(jnp.bfloat16)
    pulled = lax.dot_general(
        grad_pre, weight, (((1,), (1,)), ((), ())), preferred_element_type=jnp.float32
    ).astype(jnp.bfloat16)
    local_weight = lax.dot_general(
        aggregated, grad_pre, (((0,), (0,)), ((), ())), preferred_element_type=jnp.float32
    )

    slice_rows = feat_width // n_rep
    w_slice = lax.dynamic_slice_in_dim(local_weight, me_rep * slice_rows, slice_rows, 0)
    w_order = list(range(2, nb)) + [0, 1] if nb >= 2 else list(range(nb))
    w_slice = doubling_sum(w_slice, "rows", n_rows, w_order)
    weight_grad = doubling_gather(w_slice, "rep", n_rep).reshape(feat_width, feat_width)

    pulled_tiles = pulled.reshape(panel_tiles, tile, feat_width)
    flat_rel = sorted_rel.reshape(panel_tiles, n_rows, tile, tile)
    up = list(range(nb))
    scatter_orders = [up, [up[1], up[0]] + up[2:]] if nb >= 2 else [up]
    width = feat_width // len(scatter_orders)
    pieces = []
    for k, order in enumerate(scatter_orders):
        products = jnp.einsum(
            "tqab,taf->qbf",
            flat_rel,
            pulled_tiles[:, :, k * width:(k + 1) * width],
            preferred_element_type=jnp.float32,
        )
        products = products.reshape((2,) * nb + (block_rows, width))
        pieces.append(halving_scatter(products, order, n_rows, jnp.bfloat16))
    feature_grad = jnp.concatenate(pieces, axis=-1).astype(jnp.bfloat16)
    return (output, weight_grad, feature_grad)


def solution(mesh):
    return jax.shard_map(
        local,
        mesh=mesh,
        in_specs=(
            P(("rows", "rep"), None),
            P("rows", None),
            P(),
            P("rows", "rep", None, None, None),
            P("rows", "rep", None),
            P("rows", "rep"),
        ),
        out_specs=(P(("rows", "rep"), None), P(), P(("rows", "rep"), None)),
        check_vma=False,
    )
```

time: 99 us -> 75.5 us (0.76)
  blocking collectives: 37.9 us -> 0 us
  starting transfers between devices: 11.3 us -> 30.1 us
  waiting for transfers between devices: 38.3 us -> 21.9 us
  local copies, waits for them, and re-layouts: 2.31 us -> 11.1 us
  other arithmetic: 3.91 us -> 5.99 us
    all_to_all x1 -> x0, blocking collectives: 37.9 us -> none  [local(): received = lax.all_to_all(packed, 'rows', 0, 0, tiled=True)]
    ppermute x12 -> x22, starting transfers between devices: 11.3 us -> 30.1 us  [the longest x8 12.3 us: gather_contract(): got = lax.ppermute(held, 'rows', pairs_of(n, b))]
    ppermute x12 -> x22, waiting for transfers between devices: 38.3 us -> 21.9 us  [the longest x8 10.1 us: gather_contract(): got = lax.ppermute(held, 'rows', pairs_of(n, b))]
    unnamed x14 -> x22, local copies, waits for them, and re-layouts: 0.04 us -> 5.33 us
    slice x1 -> x14, local copies, waits for them, and re-layouts: 0.64 us -> 4.91 us  [the longest x9 3.17 us: gather_contract(): tiles = sorted_rel[(slice(None),) + bit_slices(range(nb), fixed)]]
    add x0 -> x9, other arithmetic: none -> 3.71 us  [the longest x3 2.57 us: doubling_sum(): x = x + lax.ppermute(x, axis, pairs_of(n, b))]
    select_n x9 -> x1, other arithmetic: 3.57 us -> 0.72 us  [doubling_gather(): jnp.where(low, jnp.concatenate([buf, got]), jnp.concatenate([got, buf]))]
    gather x1 -> x0, local copies, waits for them, and re-layouts: 1.6 us -> none  [local(): gathered = jnp.take(gathered, natural, axis=0)]
  transfers between devices with their start and end apart: 12 -> 22, of which waited for: 11 -> 14; matrix products, arithmetic and copies ran while one was open for 2% -> 20% of each run, Pallas kernels for 0% -> 0%
where the time goes in v2:
time: 75.5 us; the launch traced here: 75.2 us
  starting transfers between devices  30.1 us (40%)
  waiting for transfers between devices  21.9 us (29%)
  local copies, waits for them, and re-layouts  11.1 us (15%)
  other arithmetic  5.99 us (8%)
  matrix products  5.05 us (7%)
  between operations  1.11 us (1%)
    ppermute x8, starting transfers between devices, gather_contract(): got = lax.ppermute(held, 'rows', pairs_of(n, b))  12.3 us
    ppermute x8, starting transfers between devices, halving_scatter(): got = lax.ppermute(send.astype(send_dtype), 'rows', pairs_of(n, b))  11.1 us
    ppermute x8, waiting for transfers between devices, gather_contract(): got = lax.ppermute(held, 'rows', pairs_of(n, b))  10.1 us
    ppermute x5, starting transfers between devices, doubling_sum(): x = x + lax.ppermute(x, axis, pairs_of(n, b))  6.6 us
    ppermute x5, waiting for transfers between devices, doubling_sum(): x = x + lax.ppermute(x, axis, pairs_of(n, b))  5.94 us
    ppermute x8, waiting for transfers between devices, halving_scatter(): got = lax.ppermute(send.astype(send_dtype), 'rows', pairs_of(n, b))  5.8 us
    unnamed x22, local copies, waits for them, and re-layouts  5.33 us
    slice x9, local copies, waits for them, and re-layouts, gather_contract(): tiles = sorted_rel[(slice(None),) + bit_slices(range(nb), fixed)]  3.17 us
  transfers between devices with their start and end apart: 22, of which 14 were waited for; matrix products, arithmetic and copies ran while one was open for 20% of the time, Pallas kernels for 0%

profile of v2, /device:TPU:0, one launch (start us, length us, event | category | flops | bytes accessed | tf_op | source)
XLA Modules:
  0.0 75.2 jit_solution(16735329440215338090)
XLA Ops:
  0.6 0.9 %fusion.44 = (bf16[128,128]{1,0:T(8,128)(2,1)S(1)}, bf16[128,128]{1,0:T(8,128)(2,1)S(1)}) fusion(bf16[128,256]{1,0:T(8,128)(2,1)} %param.6), kind=kLoop, calls=%fused_computation.91 | loop fusion | bytes 131072 | tf_op jit(solution)/shard_map/slice | solution.py:102
  1.6 4.1 %collective-permute-start.4 = (bf16[1,1,1,1,128,128]{4,5,3,2,1,0:T(8,128)(2,1)S(1)}, bf16[1,1,1,1,128,128]{4,5,3,2,1,0:T(8,128)(2,1)S(1)}, u32[]{:S(2)}, u32[]{:S(2)}) collective-permute-start(bf16[1,1,1,1,128,128]{4,5,3,2,1,0:T(8,128)(2,1)S(1)} %bitcast.194), channel_id=1, source_target_pairs={{0,16},{2,18},{4,20},{6,22},{8,24},{10,26},{12,28},{14,30},{16,0},... | collective-permute-start | bytes 98312 | tf_op jit(solution)/shard_map/ppermute | solution.py:28
  5.9 0.6 copy-done.7
  6.7 0.6 copy-done.5
  7.3 0.7 fusion.6
  8.0 0.9 %fusion.42 = (bf16[2,2,2,1,1,128,128]{6,4,3,2,1,5,0:T(2,128)(2,1)S(1)}, bf16[2,2,2,1,1,128,128]{6,4,3,2,1,5,0:T(2,128)(2,1)S(1)}) fusion(bf16[2,2,2,2,2,128,128]{6,4,3,2,1,5,0:T(2,128)(2,1)S(1)} %bitcast.171), kind=kLoop, calls=%fused_computation.89 | loop fusion | bytes 1048576 | tf_op jit(solution)/shard_map/slice | solution.py:31
  9.1 0.6 copy-done.1
  9.8 0.2 fusion.29
  10.0 0.2 fusion.31
  10.2 0.4 slice.125
  10.8 1.1 %slice.123 = bf16[2,2,2,2,1,128,128]{6,4,3,2,1,5,0:T(2,128)(2,1)S(1)} slice(bf16[2,2,2,2,2,128,128]{6,4,3,2,1,5,0:T(2,128)(2,1)S(1)} %bitcast.175), slice={[0:2], [0:2], [0:2], [0:2], [1:2], [0:128], [0:128]} | slice | bytes 1048576 | tf_op jit(solution)/shard_map/slice | solution.py:31
  12.1 0.2 copy.33
  12.4 2.0 %collective-permute-start.5 = (bf16[2,1,1,1,128,128]{4,5,3,2,1,0:T(8,128)(2,1)S(1)}, bf16[2,1,1,1,128,128]{4,5,3,2,1,0:T(8,128)(2,1)S(1)}, u32[]{:S(2)}, u32[]{:S(2)}) collective-permute-start(bf16[2,1,1,1,128,128]{4,5,3,2,1,0:T(8,128)(2,1)S(1)} %pad_maximum_fusion.6), channel_id=1, source_target_pairs={{0,8},{2,10},{4,12},{6,14},{8,0},{10,2},{12,4},{14,6},{16,24},{18,... | collective-permute-start | bytes 196616 | tf_op jit(solution)/shard_map/ppermute | solution.py:28
  14.3 0.2 collective-permute-start.1
  14.5 2.9 %collective-permute-done.5 = bf16[2,1,1,1,128,128]{4,5,3,2,1,0:T(8,128)(2,1)S(1)} collective-permute-done((bf16[2,1,1,1,128,128]{4,5,3,2,1,0:T(8,128)(2,1)S(1)}, bf16[2,1,1,1,128,128]{4,5,3,2,1,0:T(8,128)(2,1)S(1)}, u32[]{:S(2)}, u32[]{:S(2)}) %collective-permute-start.5) | collective-permute-done | bytes 65568 | tf_op jit(solution)/shard_map/ppermute | solution.py:28
  17.4 1.6 %collective-permute-start.6 = (bf16[2,2,1,1,128,128]{4,5,3,2,1,0:T(8,128)(2,1)S(1)}, bf16[2,2,1,1,128,128]{4,5,3,2,1,0:T(8,128)(2,1)S(1)}, u32[]{:S(2)}, u32[]{:S(2)}) collective-permute-start(bf16[2,2,1,1,128,128]{4,5,3,2,1,0:T(8,128)(2,1)S(1)} %pad_maximum_fusion.4), channel_id=1, source_target_pairs={{0,2},{2,0},{4,6},{6,4},{8,10},{10,8},{12,14},{14,12},{16,18},{18,... | collective-permute-start | bytes 393224 | tf_op jit(solution)/shard_map/ppermute | solution.py:28
  19.0 1.6 %collective-permute-start.2 = (bf16[2,2,1,1,128,128]{4,5,3,2,1,0:T(8,128)(2,1)S(1)}, bf16[2,2,1,1,128,128]{4,5,3,2,1,0:T(8,128)(2,1)S(1)}, u32[]{:S(2)}, u32[]{:S(2)}) collective-permute-start(bf16[2,2,1,1,128,128]{4,5,3,2,1,0:T(8,128)(2,1)S(1)} %pad_maximum_fusion.3), channel_id=1, source_target_pairs={{0,4},{2,6},{4,0},{6,2},{8,12},{10,14},{12,8},{14,10},{16,20},{18,... | collective-permute-start | bytes 393224 | tf_op jit(solution)/shard_map/ppermute | solution.py:28
  20.8 0.2 convolution_bitcast_fusion.5
  21.0 1.5 %collective-permute-done.6 = bf16[2,2,1,1,128,128]{4,5,3,2,1,0:T(8,128)(2,1)S(1)} collective-permute-done((bf16[2,2,1,1,128,128]{4,5,3,2,1,0:T(8,128)(2,1)S(1)}, bf16[2,2,1,1,128,128]{4,5,3,2,1,0:T(8,128)(2,1)S(1)}, u32[]{:S(2)}, u32[]{:S(2)}) %collective-permute-start.6) | collective-permute-done | bytes 131104 | tf_op jit(solution)/shard_map/ppermute | solution.py:28
  22.5 1.6 %collective-permute-start.7 = (bf16[2,2,1,2,128,128]{4,5,3,2,1,0:T(8,128)(2,1)S(1)}, bf16[2,2,1,2,128,128]{4,5,3,2,1,0:T(8,128)(2,1)S(1)}, u32[]{:S(2)}, u32[]{:S(2)}) collective-permute-start(bf16[2,2,1,2,128,128]{4,5,3,2,1,0:T(8,128)(2,1)S(1)} %pad_maximum_fusion.1), channel_id=1, source_target_pairs={{0,4},{2,6},{4,0},{6,2},{8,12},{10,14},{12,8},{14,10},{16,20},{18,... | collective-permute-start | bytes 786440 | tf_op jit(solution)/shard_map/ppermute | solution.py:28
  24.1 1.4 %collective-permute-done.2 = bf16[2,2,1,1,128,128]{4,5,3,2,1,0:T(8,128)(2,1)S(1)} collective-permute-done((bf16[2,2,1,1,128,128]{4,5,3,2,1,0:T(8,128)(2,1)S(1)}, bf16[2,2,1,1,128,128]{4,5,3,2,1,0:T(8,128)(2,1)S(1)}, u32[]{:S(2)}, u32[]{:S(2)}) %collective-permute-start.2) | collective-permute-done | bytes 131104 | tf_op jit(solution)/shard_map/ppermute | solution.py:28
  25.5 1.2 %collective-permute-start.3 = (bf16[2,2,2,1,128,128]{4,5,3,2,1,0:T(8,128)(2,1)S(1)}, bf16[2,2,2,1,128,128]{4,5,3,2,1,0:T(8,128)(2,1)S(1)}, u32[]{:S(2)}, u32[]{:S(2)}) collective-permute-start(bf16[2,2,2,1,128,128]{4,5,3,2,1,0:T(8,128)(2,1)S(1)} %pad_maximum_fusion), channel_id=1, source_target_pairs={{0,2},{2,0},{4,6},{6,4},{8,10},{10,8},{12,14},{14,12},{16,18},{18,... | collective-permute-start | bytes 786440 | tf_op jit(solution)/shard_map/ppermute | solution.py:28
  26.7 0.2 convolution_bitcast_fusion.1
  26.9 0.2 convolution_bitcast_fusion.3
  27.1 1.8 %collective-permute-done.7 = bf16[2,2,1,2,128,128]{4,5,3,2,1,0:T(8,128)(2,1)S(1)} collective-permute-done((bf16[2,2,1,2,128,128]{4,5,3,2,1,0:T(8,128)(2,1)S(1)}, bf16[2,2,1,2,128,128]{4,5,3,2,1,0:T(8,128)(2,1)S(1)}, u32[]{:S(2)}, u32[]{:S(2)}) %collective-permute-start.7) | collective-permute-done | bytes 262176 | tf_op jit(solution)/shard_map/ppermute | solution.py:28
  28.9 0.3 convolution_bitcast_fusion
  29.2 2.7 %collective-permute-done.3 = bf16[2,2,2,1,128,128]{4,5,3,2,1,0:T(8,128)(2,1)S(1)} collective-permute-done((bf16[2,2,2,1,128,128]{4,5,3,2,1,0:T(8,128)(2,1)S(1)}, bf16[2,2,2,1,128,128]{4,5,3,2,1,0:T(8,128)(2,1)S(1)}, u32[]{:S(2)}, u32[]{:S(2)}) %collective-permute-start.3) | collective-permute-done | bytes 262176 | tf_op jit(solution)/shard_map/ppermute | solution.py:28
  31.9 0.3 convolution_bitcast_fusion.2
  32.7 1.5 %collective-permute-done.8 = f32[2,128,256]{1,2,0:T(8,128)S(1)} collective-permute-done((f32[2,128,256]{1,2,0:T(8,128)S(1)}, f32[2,128,256]{1,2,0:T(8,128)S(1)}, u32[]{:S(2)}, u32[]{:S(2)}) %collective-permute-start.8) | collective-permute-done | bytes 262176 | tf_op jit(solution)/shard_map/ppermute | solution.py:58
  34.4 0.8 %copy-done.2 = bf16[256,256]{1,0:T(8,128)(2,1)S(1)} copy-done((bf16[256,256]{1,0:T(8,128)(2,1)S(1)}, bf16[256,256]{1,0:T(8,128)(2,1)}, u32[]{:S(2)}) %copy-start.2) | copy-done | bytes 131096
  35.2 1.0 %multiply_convert_fusion = (bf16[256,256]{1,0:T(8,128)(2,1)S(1)}, f32[256,256]{1,0:T(8,128)}, f32[256,256]{1,0:T(8,128)}) fusion(bf16[256,256]{1,0:T(8,128)(2,1)S(1)} %copy-done.6, bf16[256,256]{1,0:T(8,128)(2,1)S(1)} %bitcast.186, bf16[256,256]{1,0:T(8,128)(2,1)S(1)} %copy-done.2), kind=kOutput, calls=%fused_computation.35 | convolution fusion | flops 34209792 | bytes 1048576 | tf_op jit(solution)/shard_map/dot_general | solution.py:110
  36.2 0.2 fusion.45
  36.4 0.2 convolution_convert_fusion
  36.6 0.7 constant_dynamic-slice_fusion
  37.3 1.1 %collective-permute-start.9 = (f32[128,256]{1,0:T(8,128)}, f32[128,256]{1,0:T(8,128)}, u32[]{:S(2)}, u32[]{:S(2)}) collective-permute-start(f32[128,256]{1,0:T(8,128)} %constant_dynamic-slice_fusion), channel_id=1, source_target_pairs={{0,8},{2,10},{4,12},{6,14},{8,0},{10,2},{12,4},{14,6},{16,24},{18,... | collective-permute-start | bytes 393224 | tf_op jit(solution)/shard_map/ppermute | solution.py:58
  38.5 0.3 fusion.10
  38.8 0.8 %slice.137 = bf16[2,2,1,2,128,128]{4,5,3,2,1,0:T(8,128)(2,1)} slice(f32[2,2,2,2,128,128]{4,5,3,2,1,0:T(8,128)S(1)} %bitcast.176), slice={[0:2], [0:2], [1:2], [0:2], [0:128], [0:128]} | slice | bytes 524288 | tf_op jit(solution)/shard_map/slice | solution.py:49
  39.6 1.8 %copy.65 = bf16[2,2,1,2,128,128]{5,4,0,1,3,2:T(8,128)(2,1)} copy(bf16[2,2,1,2,128,128]{4,5,3,2,1,0:T(8,128)(2,1)} %slice.137) | data formatting | bytes 524288
  41.3 1.5 %collective-permute-start.18 = (bf16[2,2,2,128,128]{4,3,0,1,2:T(8,128)(2,1)}, bf16[2,2,2,128,128]{4,3,0,1,2:T(8,128)(2,1)}, u32[]{:S(2)}, u32[]{:S(2)}) collective-permute-start(bf16[2,2,2,128,128]{4,3,0,1,2:T(8,128)(2,1)} %bitcast.201), channel_id=1, source_target_pairs={{0,4},{2,6},{4,0},{6,2},{8,12},{10,14},{12,8},{14,10},{16,20},{18,... | collective-permute-start | bytes 786440 | tf_op jit(solution)/shard_map/ppermute | solution.py:50
  42.9 0.3 collective-permute-done.9
  43.2 1.6 %fusion.60 = f32[128,256]{1,0:T(8,128)} fusion(f32[128,256]{1,0:T(8,128)} %collective-permute-done.9, f32[256,256]{1,0:T(8,128)S(1)} %fusion.45, s32[]{:T(128)S(6)} %select_n.16), kind=kLoop, calls=%fused_computation.93 | loop fusion | flops 32768 | bytes 393220 | tf_op jit(solution)/shard_map/add | solution.py:58
  44.7 2.6 %collective-permute-start.10 = (f32[128,256]{1,0:T(8,128)}, f32[128,256]{1,0:T(8,128)}, u32[]{:S(2)}, u32[]{:S(2)}) collective-permute-start(f32[128,256]{1,0:T(8,128)} %fusion.60), channel_id=1, source_target_pairs={{0,16},{2,18},{4,20},{6,22},{8,24},{10,26},{12,28},{14,30},{16,0},... | collective-permute-start | bytes 393224 | tf_op jit(solution)/shard_map/ppermute | solution.py:58
  47.3 0.3 fusion.8
  48.4 1.2 %collective-permute-start.14 = (bf16[2,2,2,128,128]{4,3,0,1,2:T(8,128)(2,1)S(1)}, bf16[2,2,2,128,128]{4,3,0,1,2:T(8,128)(2,1)S(1)}, u32[]{:S(2)}, u32[]{:S(2)}) collective-permute-start(bf16[2,2,2,128,128]{4,3,0,1,2:T(8,128)(2,1)S(1)} %bitcast.202), channel_id=1, source_target_pairs={{0,2},{2,0},{4,6},{6,4},{8,10},{10,8},{12,14},{14,12},{16,18},{18,... | collective-permute-start | bytes 786440 | tf_op jit(solution)/shard_map/ppermute | solution.py:50
  49.6 0.6 fusion.18
  50.3 3.2 %collective-permute-done.10 = f32[128,256]{1,0:T(8,128)} collective-permute-done((f32[128,256]{1,0:T(8,128)}, f32[128,256]{1,0:T(8,128)}, u32[]{:S(2)}, u32[]{:S(2)}) %collective-permute-start.10) | collective-permute-done | bytes 131104 | tf_op jit(solution)/shard_map/ppermute | solution.py:58
  53.5 1.0 %add.86 = f32[128,256]{1,0:T(8,128)S(1)} add(f32[128,256]{1,0:T(8,128)} %fusion.60, f32[128,256]{1,0:T(8,128)} %collective-permute-done.10) | non-fusion elementwise | flops 32768 | bytes 393216 | tf_op jit(solution)/shard_map/add | solution.py:58
  54.5 1.2 %collective-permute-start.11 = (f32[128,256]{1,0:T(8,128)S(1)}, f32[128,256]{1,0:T(8,128)S(1)}, u32[]{:S(2)}, u32[]{:S(2)}) collective-permute-start(f32[128,256]{1,0:T(8,128)S(1)} %add.86), channel_id=1, source_target_pairs={{0,2},{2,0},{4,6},{6,4},{8,10},{10,8},{12,14},{14,12},{16,18},{18,... | collective-permute-start | bytes 393224 | tf_op jit(solution)/shard_map/ppermute | solution.py:58
  55.7 1.0 %bitcast_add_fusion = f32[2,2,2,128,128]{4,3,0,1,2:T(8,128)S(1)} fusion(f32[2,2,1,2,128,128]{5,4,0,1,3,2:T(8,128)S(1)} %copy.64, bf16[2,2,2,128,128]{4,3,0,1,2:T(8,128)(2,1)} %collective-permute-done.18), kind=kLoop, calls=%fused_computation.21 | loop fusion | flops 262144 | bytes 1310720 | tf_op jit(solution)/shard_map/add | solution.py:51
  56.7 0.9 %collective-permute-start.19 = (bf16[2,2,128,128]{3,2,0,1:T(8,128)(2,1)S(1)}, bf16[2,2,128,128]{3,2,0,1:T(8,128)(2,1)S(1)}, u32[]{:S(2)}, u32[]{:S(2)}) collective-permute-start(bf16[2,2,128,128]{3,2,0,1:T(8,128)(2,1)S(1)} %fusion.15), channel_id=1, source_target_pairs={{0,2},{2,0},{4,6},{6,4},{8,10},{10,8},{12,14},{14,12},{16,18},{18,... | collective-permute-start | bytes 393224 | tf_op jit(solution)/shard_map/ppermute | solution.py:50
  57.8 1.6 %collective-permute-start.15 = (bf16[2,2,128,128]{3,2,0,1:T(8,128)(2,1)S(1)}, bf16[2,2,128,128]{3,2,0,1:T(8,128)(2,1)S(1)}, u32[]{:S(2)}, u32[]{:S(2)}) collective-permute-start(bf16[2,2,128,128]{3,2,0,1:T(8,128)(2,1)S(1)} %fusion.14), channel_id=1, source_target_pairs={{0,4},{2,6},{4,0},{6,2},{8,12},{10,14},{12,8},{14,10},{16,20},{18,... | collective-permute-start | bytes 393224 | tf_op jit(solution)/shard_map/ppermute | solution.py:50
  59.3 0.9 %collective-permute-done.11 = f32[128,256]{1,0:T(8,128)S(1)} collective-permute-done((f32[128,256]{1,0:T(8,128)S(1)}, f32[128,256]{1,0:T(8,128)S(1)}, u32[]{:S(2)}, u32[]{:S(2)}) %collective-permute-start.11) | collective-permute-done | bytes 131104 | tf_op jit(solution)/shard_map/ppermute | solution.py:58
  60.3 1.6 %collective-permute-start.12 = (f32[128,256]{1,0:T(8,128)S(1)}, f32[128,256]{1,0:T(8,128)S(1)}, u32[]{:S(2)}, u32[]{:S(2)}) collective-permute-start(f32[128,256]{1,0:T(8,128)S(1)} %add.87), channel_id=1, source_target_pairs={{0,4},{2,6},{4,0},{6,2},{8,12},{10,14},{12,8},{14,10},{16,20},{18,... | collective-permute-start | bytes 393224 | tf_op jit(solution)/shard_map/ppermute | solution.py:58
  61.9 0.5 collective-permute-done.19
  62.4 0.7 collective-permute-start.20
  63.0 0.4 collective-permute-done.15
  63.5 1.1 %collective-permute-start.16 = (bf16[2,128,128]{2,1,0:T(8,128)(2,1)S(1)}, bf16[2,128,128]{2,1,0:T(8,128)(2,1)S(1)}, u32[]{:S(2)}, u32[]{:S(2)}) collective-permute-start(bf16[2,128,128]{2,1,0:T(8,128)(2,1)S(1)} %fusion.19), channel_id=1, source_target_pairs={{0,8},{2,10},{4,12},{6,14},{8,0},{10,2},{12,4},{14,6},{16,24},{18,... | collective-permute-start | bytes 196616 | tf_op jit(solution)/shard_map/ppermute | solution.py:50
  64.6 2.1 %collective-permute-done.20 = bf16[2,128,128]{2,1,0:T(8,128)(2,1)S(1)} collective-permute-done((bf16[2,128,128]{2,1,0:T(8,128)(2,1)S(1)}, bf16[2,128,128]{2,1,0:T(8,128)(2,1)S(1)}, u32[]{:S(2)}, u32[]{:S(2)}) %collective-permute-start.20) | collective-permute-done | bytes 65568 | tf_op jit(solution)/shard_map/ppermute | solution.py:50
  66.7 2.2 %collective-permute-start.21 = (bf16[128,128]{1,0:T(8,128)(2,1)S(1)}, bf16[128,128]{1,0:T(8,128)(2,1)S(1)}, u32[]{:S(2)}, u32[]{:S(2)}) collective-permute-start(bf16[128,128]{1,0:T(8,128)(2,1)S(1)} %fusion.28), channel_id=1, source_target_pairs={{0,16},{2,18},{4,20},{6,22},{8,24},{10,26},{12,28},{14,30},{16,0},... | collective-permute-start | bytes 98312 | tf_op jit(solution)/shard_map/ppermute | solution.py:50
  68.9 2.0 %collective-permute-start.17 = (bf16[128,128]{1,0:T(8,128)(2,1)S(1)}, bf16[128,128]{1,0:T(8,128)(2,1)S(1)}, u32[]{:S(2)}, u32[]{:S(2)}) collective-permute-start(bf16[128,128]{1,0:T(8,128)(2,1)S(1)} %fusion.27), channel_id=1, source_target_pairs={{0,16},{2,18},{4,20},{6,22},{8,24},{10,26},{12,28},{14,30},{16,0},... | collective-permute-start | bytes 98312 | tf_op jit(solution)/shard_map/ppermute | solution.py:50
  70.9 0.8 %collective-permute-done.21 = bf16[128,128]{1,0:T(8,128)(2,1)S(1)} collective-permute-done((bf16[128,128]{1,0:T(8,128)(2,1)S(1)}, bf16[128,128]{1,0:T(8,128)(2,1)S(1)}, u32[]{:S(2)}, u32[]{:S(2)}) %collective-permute-start.21) | collective-permute-done | bytes 32800 | tf_op jit(solution)/shard_map/ppermute | solution.py:50
  71.8 2.0 %collective-permute-done.17 = bf16[128,128]{1,0:T(8,128)(2,1)S(1)} collective-permute-done((bf16[128,128]{1,0:T(8,128)(2,1)S(1)}, bf16[128,128]{1,0:T(8,128)(2,1)S(1)}, u32[]{:S(2)}, u32[]{:S(2)}) %collective-permute-start.17) | collective-permute-done | bytes 32800 | tf_op jit(solution)/shard_map/ppermute | solution.py:50
  73.8 0.6 pad_maximum_fusion.7
  74.5 0.7 maximum_select_fusion
  (65 shorter events, 3.0 us)
Async XLA Ops:
  0.6 6.6 %copy-start = (bf16[2,1,16,128,128]{4,3,2,1,0:T(8,128)(2,1)S(1)}, bf16[2,1,16,128,128]{4,3,2,1,0:T(8,128)(2,1)}, u32[]{:S(2)}) copy-start(bf16[2,1,16,128,128]{4,3,2,1,0:T(8,128)(2,1)} %param.9) | copy-start | bytes 3145732
  1.6 10.7 %collective-permute-start.4 = (bf16[1,1,1,1,128,128]{4,5,3,2,1,0:T(8,128)(2,1)S(1)}, bf16[1,1,1,1,128,128]{4,5,3,2,1,0:T(8,128)(2,1)S(1)}, u32[]{:S(2)}, u32[]{:S(2)}) collective-permute-start(bf16[1,1,1,1,128,128]{4,5,3,2,1,0:T(8,128)(2,1)S(1)} %bitcast.194), channel_id=1, source_target_pairs={{0,16},{2,18},{4,20},{6,22},{8,24},{10,26},{12,28},{14,30},{16,0},... | collective-permute-start | bytes 98312 | tf_op jit(solution)/shard_map/ppermute | solution.py:28
  5.8 8.5 %collective-permute-start = (bf16[1,1,1,1,128,128]{4,5,3,2,1,0:T(8,128)(2,1)S(1)}, bf16[1,1,1,1,128,128]{4,5,3,2,1,0:T(8,128)(2,1)S(1)}, u32[]{:S(2)}, u32[]{:S(2)}) collective-permute-start(bf16[1,1,1,1,128,128]{4,5,3,2,1,0:T(8,128)(2,1)S(1)} %bitcast.190), channel_id=1, source_target_pairs={{0,16},{2,18},{4,20},{6,22},{8,24},{10,26},{12,28},{14,30},{16,0},... | collective-permute-start | bytes 98312 | tf_op jit(solution)/shard_map/ppermute | solution.py:28
  5.9 0.7 copy-start.7
  6.6 0.7 copy-start.5
  8.9 0.8 %copy-start.1 = (bf16[128,256]{1,0:T(8,128)(2,1)S(1)}, bf16[128,256]{1,0:T(8,128)(2,1)}, u32[]{:S(2)}) copy-start(bf16[128,256]{1,0:T(8,128)(2,1)} %param.6) | copy-start | bytes 196612
  12.4 5.0 %collective-permute-start.5 = (bf16[2,1,1,1,128,128]{4,5,3,2,1,0:T(8,128)(2,1)S(1)}, bf16[2,1,1,1,128,128]{4,5,3,2,1,0:T(8,128)(2,1)S(1)}, u32[]{:S(2)}, u32[]{:S(2)}) collective-permute-start(bf16[2,1,1,1,128,128]{4,5,3,2,1,0:T(8,128)(2,1)S(1)} %pad_maximum_fusion.6), channel_id=1, source_target_pairs={{0,8},{2,10},{4,12},{6,14},{8,0},{10,2},{12,4},{14,6},{16,24},{18,... | collective-permute-start | bytes 196616 | tf_op jit(solution)/shard_map/ppermute | solution.py:28
  14.3 4.6 %collective-permute-start.1 = (bf16[2,1,1,1,128,128]{4,5,3,2,1,0:T(8,128)(2,1)S(1)}, bf16[2,1,1,1,128,128]{4,5,3,2,1,0:T(8,128)(2,1)S(1)}, u32[]{:S(2)}, u32[]{:S(2)}) collective-permute-start(bf16[2,1,1,1,128,128]{4,5,3,2,1,0:T(8,128)(2,1)S(1)} %pad_maximum_fusion.5), channel_id=1, source_target_pairs={{0,8},{2,10},{4,12},{6,14},{8,0},{10,2},{12,4},{14,6},{16,24},{18,... | collective-permute-start | bytes 196616 | tf_op jit(solution)/shard_map/ppermute | solution.py:28
  17.4 5.0 %collective-permute-start.6 = (bf16[2,2,1,1,128,128]{4,5,3,2,1,0:T(8,128)(2,1)S(1)}, bf16[2,2,1,1,128,128]{4,5,3,2,1,0:T(8,128)(2,1)S(1)}, u32[]{:S(2)}, u32[]{:S(2)}) collective-permute-start(bf16[2,2,1,1,128,128]{4,5,3,2,1,0:T(8,128)(2,1)S(1)} %pad_maximum_fusion.4), channel_id=1, source_target_pairs={{0,2},{2,0},{4,6},{6,4},{8,10},{10,8},{12,14},{14,12},{16,18},{18,... | collective-permute-start | bytes 393224 | tf_op jit(solution)/shard_map/ppermute | solution.py:28
  19.0 6.4 %collective-permute-start.2 = (bf16[2,2,1,1,128,128]{4,5,3,2,1,0:T(8,128)(2,1)S(1)}, bf16[2,2,1,1,128,128]{4,5,3,2,1,0:T(8,128)(2,1)S(1)}, u32[]{:S(2)}, u32[]{:S(2)}) collective-permute-start(bf16[2,2,1,1,128,128]{4,5,3,2,1,0:T(8,128)(2,1)S(1)} %pad_maximum_fusion.3), channel_id=1, source_target_pairs={{0,4},{2,6},{4,0},{6,2},{8,12},{10,14},{12,8},{14,10},{16,20},{18,... | collective-permute-start | bytes 393224 | tf_op jit(solution)/shard_map/ppermute | solution.py:28
  22.5 6.4 %collective-permute-start.7 = (bf16[2,2,1,2,128,128]{4,5,3,2,1,0:T(8,128)(2,1)S(1)}, bf16[2,2,1,2,128,128]{4,5,3,2,1,0:T(8,128)(2,1)S(1)}, u32[]{:S(2)}, u32[]{:S(2)}) collective-permute-start(bf16[2,2,1,2,128,128]{4,5,3,2,1,0:T(8,128)(2,1)S(1)} %pad_maximum_fusion.1), channel_id=1, source_target_pairs={{0,4},{2,6},{4,0},{6,2},{8,12},{10,14},{12,8},{14,10},{16,20},{18,... | collective-permute-start | bytes 786440 | tf_op jit(solution)/shard_map/ppermute | solution.py:28
  25.5 6.4 %collective-permute-start.3 = (bf16[2,2,2,1,128,128]{4,5,3,2,1,0:T(8,128)(2,1)S(1)}, bf16[2,2,2,1,128,128]{4,5,3,2,1,0:T(8,128)(2,1)S(1)}, u32[]{:S(2)}, u32[]{:S(2)}) collective-permute-start(bf16[2,2,2,1,128,128]{4,5,3,2,1,0:T(8,128)(2,1)S(1)} %pad_maximum_fusion), channel_id=1, source_target_pairs={{0,2},{2,0},{4,6},{6,4},{8,10},{10,8},{12,14},{14,12},{16,18},{18,... | collective-permute-start | bytes 786440 | tf_op jit(solution)/shard_map/ppermute | solution.py:28
  32.6 1.6 %collective-permute-start.8 = (f32[2,128,256]{1,2,0:T(8,128)S(1)}, f32[2,128,256]{1,2,0:T(8,128)S(1)}, u32[]{:S(2)}, u32[]{:S(2)}) collective-permute-start(f32[2,128,256]{1,2,0:T(8,128)S(1)} %pad_maximum_fusion.2), channel_id=1, source_target_pairs={{0,1},{1,0},{2,3},{3,2},{4,5},{5,4},{6,7},{7,6},{8,9},{9,8},{10,11... | collective-permute-start | bytes 786440 | tf_op jit(solution)/shard_map/ppermute | solution.py:58
  34.2 0.9 %copy-start.2 = (bf16[256,256]{1,0:T(8,128)(2,1)S(1)}, bf16[256,256]{1,0:T(8,128)(2,1)}, u32[]{:S(2)}) copy-start(bf16[256,256]{1,0:T(8,128)(2,1)} %param.8) | copy-start | bytes 393220
  34.3 1.0 %copy-start.6 = (bf16[256,256]{1,0:T(8,128)(2,1)S(1)}, bf16[256,256]{1,0:T(8,128)(2,1)}, u32[]{:S(2)}) copy-start(bf16[256,256]{1,0:T(8,128)(2,1)} %param.7) | copy-start | bytes 393220
  37.3 5.9 %collective-permute-start.9 = (f32[128,256]{1,0:T(8,128)}, f32[128,256]{1,0:T(8,128)}, u32[]{:S(2)}, u32[]{:S(2)}) collective-permute-start(f32[128,256]{1,0:T(8,128)} %constant_dynamic-slice_fusion), channel_id=1, source_target_pairs={{0,8},{2,10},{4,12},{6,14},{8,0},{10,2},{12,4},{14,6},{16,24},{18,... | collective-permute-start | bytes 393224 | tf_op jit(solution)/shard_map/ppermute | solution.py:58
  41.3 14.4 %collective-permute-start.18 = (bf16[2,2,2,128,128]{4,3,0,1,2:T(8,128)(2,1)}, bf16[2,2,2,128,128]{4,3,0,1,2:T(8,128)(2,1)}, u32[]{:S(2)}, u32[]{:S(2)}) collective-permute-start(bf16[2,2,2,128,128]{4,3,0,1,2:T(8,128)(2,1)} %bitcast.201), channel_id=1, source_target_pairs={{0,4},{2,6},{4,0},{6,2},{8,12},{10,14},{12,8},{14,10},{16,20},{18,... | collective-permute-start | bytes 786440 | tf_op jit(solution)/shard_map/ppermute | solution.py:50
  44.7 8.7 %collective-permute-start.10 = (f32[128,256]{1,0:T(8,128)}, f32[128,256]{1,0:T(8,128)}, u32[]{:S(2)}, u32[]{:S(2)}) collective-permute-start(f32[128,256]{1,0:T(8,128)} %fusion.60), channel_id=1, source_target_pairs={{0,16},{2,18},{4,20},{6,22},{8,24},{10,26},{12,28},{14,30},{16,0},... | collective-permute-start | bytes 393224 | tf_op jit(solution)/shard_map/ppermute | solution.py:58
  48.2 1.4 %copy-start.3 = (f32[256,256]{1,0:T(8,128)S(1)}, f32[256,256]{1,0:T(8,128)}, u32[]{:S(2)}) copy-start(f32[256,256]{1,0:T(8,128)} %get-tuple-element.8) | copy-start | bytes 786436
  48.2 1.4 %copy-start.4 = (f32[256,256]{1,0:T(8,128)S(1)}, f32[256,256]{1,0:T(8,128)}, u32[]{:S(2)}) copy-start(f32[256,256]{1,0:T(8,128)} %get-tuple-element.11) | copy-start | bytes 786436
  48.4 9.2 %collective-permute-start.14 = (bf16[2,2,2,128,128]{4,3,0,1,2:T(8,128)(2,1)S(1)}, bf16[2,2,2,128,128]{4,3,0,1,2:T(8,128)(2,1)S(1)}, u32[]{:S(2)}, u32[]{:S(2)}) collective-permute-start(bf16[2,2,2,128,128]{4,3,0,1,2:T(8,128)(2,1)S(1)} %bitcast.202), channel_id=1, source_target_pairs={{0,2},{2,0},{4,6},{6,4},{8,10},{10,8},{12,14},{14,12},{16,18},{18,... | collective-permute-start | bytes 786440 | tf_op jit(solution)/shard_map/ppermute | solution.py:50
  54.5 5.8 %collective-permute-start.11 = (f32[128,256]{1,0:T(8,128)S(1)}, f32[128,256]{1,0:T(8,128)S(1)}, u32[]{:S(2)}, u32[]{:S(2)}) collective-permute-start(f32[128,256]{1,0:T(8,128)S(1)} %add.86), channel_id=1, source_target_pairs={{0,2},{2,0},{4,6},{6,4},{8,10},{10,8},{12,14},{14,12},{16,18},{18,... | collective-permute-start | bytes 393224 | tf_op jit(solution)/shard_map/ppermute | solution.py:58
  56.7 5.6 %collective-permute-start.19 = (bf16[2,2,128,128]{3,2,0,1:T(8,128)(2,1)S(1)}, bf16[2,2,128,128]{3,2,0,1:T(8,128)(2,1)S(1)}, u32[]{:S(2)}, u32[]{:S(2)}) collective-permute-start(bf16[2,2,128,128]{3,2,0,1:T(8,128)(2,1)S(1)} %fusion.15), channel_id=1, source_target_pairs={{0,2},{2,0},{4,6},{6,4},{8,10},{10,8},{12,14},{14,12},{16,18},{18,... | collective-permute-start | bytes 393224 | tf_op jit(solution)/shard_map/ppermute | solution.py:50
  57.8 5.7 %collective-permute-start.15 = (bf16[2,2,128,128]{3,2,0,1:T(8,128)(2,1)S(1)}, bf16[2,2,128,128]{3,2,0,1:T(8,128)(2,1)S(1)}, u32[]{:S(2)}, u32[]{:S(2)}) collective-permute-start(bf16[2,2,128,128]{3,2,0,1:T(8,128)(2,1)S(1)} %fusion.14), channel_id=1, source_target_pairs={{0,4},{2,6},{4,0},{6,2},{8,12},{10,14},{12,8},{14,10},{16,20},{18,... | collective-permute-start | bytes 393224 | tf_op jit(solution)/shard_map/ppermute | solution.py:50
  60.3 11.4 %collective-permute-start.12 = (f32[128,256]{1,0:T(8,128)S(1)}, f32[128,256]{1,0:T(8,128)S(1)}, u32[]{:S(2)}, u32[]{:S(2)}) collective-permute-start(f32[128,256]{1,0:T(8,128)S(1)} %add.87), channel_id=1, source_target_pairs={{0,4},{2,6},{4,0},{6,2},{8,12},{10,14},{12,8},{14,10},{16,20},{18,... | collective-permute-start | bytes 393224 | tf_op jit(solution)/shard_map/ppermute | solution.py:58
  62.4 4.3 %collective-permute-start.20 = (bf16[2,128,128]{2,1,0:T(8,128)(2,1)S(1)}, bf16[2,128,128]{2,1,0:T(8,128)(2,1)S(1)}, u32[]{:S(2)}, u32[]{:S(2)}) collective-permute-start(bf16[2,128,128]{2,1,0:T(8,128)(2,1)S(1)} %fusion.20), channel_id=1, source_target_pairs={{0,8},{2,10},{4,12},{6,14},{8,0},{10,2},{12,4},{14,6},{16,24},{18,... | collective-permute-start | bytes 196616 | tf_op jit(solution)/shard_map/ppermute | solution.py:50
  63.5 5.4 %collective-permute-start.16 = (bf16[2,128,128]{2,1,0:T(8,128)(2,1)S(1)}, bf16[2,128,128]{2,1,0:T(8,128)(2,1)S(1)}, u32[]{:S(2)}, u32[]{:S(2)}) collective-permute-start(bf16[2,128,128]{2,1,0:T(8,128)(2,1)S(1)} %fusion.19), channel_id=1, source_target_pairs={{0,8},{2,10},{4,12},{6,14},{8,0},{10,2},{12,4},{14,6},{16,24},{18,... | collective-permute-start | bytes 196616 | tf_op jit(solution)/shard_map/ppermute | solution.py:50
  66.7 4.9 %collective-permute-start.21 = (bf16[128,128]{1,0:T(8,128)(2,1)S(1)}, bf16[128,128]{1,0:T(8,128)(2,1)S(1)}, u32[]{:S(2)}, u32[]{:S(2)}) collective-permute-start(bf16[128,128]{1,0:T(8,128)(2,1)S(1)} %fusion.28), channel_id=1, source_target_pairs={{0,16},{2,18},{4,20},{6,22},{8,24},{10,26},{12,28},{14,30},{16,0},... | collective-permute-start | bytes 98312 | tf_op jit(solution)/shard_map/ppermute | solution.py:50
  68.9 4.9 %collective-permute-start.17 = (bf16[128,128]{1,0:T(8,128)(2,1)S(1)}, bf16[128,128]{1,0:T(8,128)(2,1)S(1)}, u32[]{:S(2)}, u32[]{:S(2)}) collective-permute-start(bf16[128,128]{1,0:T(8,128)(2,1)S(1)} %fusion.27), channel_id=1, source_target_pairs={{0,16},{2,18},{4,20},{6,22},{8,24},{10,26},{12,28},{14,30},{16,0},... | collective-permute-start | bytes 98312 | tf_op jit(solution)/shard_map/ppermute | solution.py:50
  71.7 2.8 %collective-permute-start.13 = (f32[1,128,256]{2,1,0:T(8,128)S(1)}, f32[1,128,256]{2,1,0:T(8,128)S(1)}, u32[]{:S(2)}, u32[]{:S(2)}) collective-permute-start(f32[1,128,256]{2,1,0:T(8,128)S(1)} %add_bitcast_fusion), channel_id=1, source_target_pairs={{0,1},{1,0},{2,3},{3,2},{4,5},{5,4},{6,7},{7,6},{8,9},{9,8},{10,11... | collective-permute-start | bytes 393224 | tf_op jit(solution)/shard_map/ppermute | solution.py:66

commit v3 on v2

--- a/solution.py
+++ b/solution.py
@@ -3,6 +3,11 @@
 from jax import lax
 from jax.sharding import PartitionSpec as P
 
+GATHER_PARTS = 2
+SCATTER_PARTS = 1
+W_PACKED = False
+PIPE_FWD = False
+
 
 def bit_count(n):
     return n.bit_length() - 1
@@ -21,11 +26,17 @@
     nb = bit_count(n)
     t_count, a_size = sorted_rel.shape[0], sorted_rel.shape[-2]
     held = x_part.reshape((1,) * nb + x_part.shape)
-    own = sorted_rel[(slice(None),) + (0,) * nb]
-    acc = jnp.einsum("tab,bf->taf", own, x_part, preferred_element_type=jnp.float32)
+    acc = None
+    if PIPE_FWD:
+        own = sorted_rel[(slice(None),) + (0,) * nb]
+        acc = jnp.einsum("tab,bf->taf", own, x_part, preferred_element_type=jnp.float32)
     done = []
     for step, b in enumerate(order):
         got = lax.ppermute(held, "rows", pairs_of(n, b))
+        if not PIPE_FWD:
+            held = jnp.concatenate([held, got], axis=nb - 1 - b)
+            done.append(b)
+            continue
         fixed = {bb: (0, 1) for bb in range(nb) if bb not in done}
         fixed[b] = (1, 2)
         tiles = sorted_rel[(slice(None),) + bit_slices(range(nb), fixed)]
@@ -36,21 +47,48 @@
         done.append(b)
         if step + 1 < len(order):
             held = jnp.concatenate([held, got], axis=nb - 1 - b)
+    if not PIPE_FWD:
+        every = sorted_rel.reshape(t_count, -1, a_size, sorted_rel.shape[-1])
+        return jnp.einsum(
+            "tmab,mbf->taf", every, held.reshape((-1,) + x_part.shape), preferred_element_type=jnp.float32
+        )
     return acc
 
 
-def halving_scatter(rel, order, n, send_dtype):
+def split_words(x):
+    hi = x.astype(jnp.bfloat16)
+    lo = (x - hi.astype(jnp.float32)).astype(jnp.bfloat16)
+    return hi, lo
+
+
+def joined(hi, lo):
+    return hi.astype(jnp.float32) + lo.astype(jnp.float32)
+
+
+def halving_scatter(rel, order, n, send_dtype, extra=None):
     nb = bit_count(n)
     cur = rel
     axes_bits = list(range(nb - 1, -1, -1))
+    width = rel.shape[-1]
     for b in order:
         ax = axes_bits.index(b)
         keep = lax.index_in_dim(cur, 0, ax, keepdims=False)
         send = lax.index_in_dim(cur, 1, ax, keepdims=False)
-        got = lax.ppermute(send.astype(send_dtype), "rows", pairs_of(n, b))
+        if extra is None:
+            got = lax.ppermute(send.astype(send_dtype), "rows", pairs_of(n, b))
+        else:
+            hi, lo = split_words(extra)
+            flat = send.astype(send_dtype).reshape(-1, width)
+            words = jnp.concatenate([flat, hi, lo])
+            got_words = lax.ppermute(words, "rows", pairs_of(n, b))
+            got = got_words[: flat.shape[0]].reshape(send.shape)
+            rows_extra = extra.shape[0]
+            got_hi = got_words[flat.shape[0]: flat.shape[0] + rows_extra]
+            got_lo = got_words[flat.shape[0] + rows_extra:]
+            extra = joined(hi, lo) + joined(got_hi, got_lo)
         cur = keep + got.astype(jnp.float32)
         axes_bits.pop(ax)
-    return cur
+    return cur, extra
 
 
 def doubling_sum(x, axis, n, order):
@@ -95,7 +133,7 @@
     sorted_rel = sorted_rel.reshape((panel_tiles,) + (2,) * nb + (tile, tile))
 
     down = list(range(nb - 1, -1, -1))
-    gather_orders = [down, down[:-2] + [down[-1], down[-2]]]
+    gather_orders = [down, down[:-2] + [down[-1], down[-2]]][:GATHER_PARTS] if nb >= 2 else [down]
     width = feat_width // len(gather_orders)
     partial_value = jnp.concatenate(
         [
@@ -123,14 +161,14 @@
 
     slice_rows = feat_width // n_rep
     w_slice = lax.dynamic_slice_in_dim(local_weight, me_rep * slice_rows, slice_rows, 0)
-    w_order = list(range(2, nb)) + [0, 1] if nb >= 2 else list(range(nb))
-    w_slice = doubling_sum(w_slice, "rows", n_rows, w_order)
-    weight_grad = doubling_gather(w_slice, "rep", n_rep).reshape(feat_width, feat_width)
+    if not W_PACKED:
+        w_order = list(range(2, nb)) + [0, 1] if nb >= 2 else list(range(nb))
+        w_slice = doubling_sum(w_slice, "rows", n_rows, w_order)
 
     pulled_tiles = pulled.reshape(panel_tiles, tile, feat_width)
     flat_rel = sorted_rel.reshape(panel_tiles, n_rows, tile, tile)
     up = list(range(nb))
-    scatter_orders = [up, [up[1], up[0]] + up[2:]] if nb >= 2 else [up]
+    scatter_orders = ([up, [up[1], up[0]] + up[2:]] if nb >= 2 else [up])[:SCATTER_PARTS]
     width = feat_width // len(scatter_orders)
     pieces = []
     for k, order in enumerate(scatter_orders):
@@ -141,8 +179,13 @@
             preferred_element_type=jnp.float32,
         )
         products = products.reshape((2,) * nb + (block_rows, width))
-        pieces.append(halving_scatter(products, order, n_rows, jnp.bfloat16))
+        extra = w_slice.reshape(-1, width) if (W_PACKED and k == 0) else None
+        piece, extra = halving_scatter(products, order, n_rows, jnp.bfloat16, extra)
+        if extra is not None:
+            w_slice = extra.reshape(slice_rows, feat_width)
+        pieces.append(piece)
     feature_grad = jnp.concatenate(pieces, axis=-1).astype(jnp.bfloat16)
+    weight_grad = doubling_gather(w_slice, "rep", n_rep).reshape(feat_width, feat_width)
     return (output, weight_grad, feature_grad)
 
 

time: 75.5 us -> 66.8 us (0.88)
  waiting for transfers between devices: 21.9 us -> 34.8 us
  local copies, waits for them, and re-layouts: 11.1 us -> 1.14 us
  starting transfers between devices: 30.1 us -> 22.3 us
  other arithmetic: 5.99 us -> 3.94 us
  matrix products: 5.05 us -> 3.55 us
    ppermute x8 -> x4, starting transfers between devices: 11.1 us -> 5.69 us  [halving_scatter(): got = lax.ppermute(send.astype(send_dtype), 'rows', pairs_of(n, b))]
    ppermute x5, waiting for transfers between devices: 5.94 us -> 11.3 us  [doubling_sum(): x = x + lax.ppermute(x, axis, pairs_of(n, b))]
    unnamed x22 -> x8, local copies, waits for them, and re-layouts: 5.33 us -> 0.03 us
    slice x14 -> x0, local copies, waits for them, and re-layouts: 4.91 us -> none  [the longest x9 3.17 us: gather_contract(): tiles = sorted_rel[(slice(None),) + bit_slices(range(nb), fixed)]]
    ppermute x8 -> x4, waiting for transfers between devices: 5.8 us -> 10.2 us  [halving_scatter(): got = lax.ppermute(send.astype(send_dtype), 'rows', pairs_of(n, b))]
    ppermute x8, waiting for transfers between devices: 10.1 us -> 13.2 us  [gather_contract(): got = lax.ppermute(held, 'rows', pairs_of(n, b))]
    add x3, other arithmetic: 2.57 us -> 0.05 us  [doubling_sum(): x = x + lax.ppermute(x, axis, pairs_of(n, b))]
    ppermute x5, starting transfers between devices: 6.6 us -> 4.43 us  [doubling_sum(): x = x + lax.ppermute(x, axis, pairs_of(n, b))]
  transfers between devices with their start and end apart: 22 -> 18, of which waited for: 14 -> 14; matrix products, arithmetic and copies ran while one was open for 20% -> 7% of each run, Pallas kernels for 0% -> 0%
where the time goes in v3:
time: 66.8 us; the launch traced here: 66.6 us
  waiting for transfers between devices  34.8 us (52%)
  starting transfers between devices  22.3 us (33%)
  other arithmetic  3.94 us (6%)
  matrix products  3.55 us (5%)
  local copies, waits for them, and re-layouts  1.14 us (2%)
  between operations  0.88 us (1%)
    ppermute x8, waiting for transfers between devices, gather_contract(): got = lax.ppermute(held, 'rows', pairs_of(n, b))  13.2 us
    ppermute x8, starting transfers between devices, gather_contract(): got = lax.ppermute(held, 'rows', pairs_of(n, b))  12.1 us
    ppermute x5, waiting for transfers between devices, doubling_sum(): x = x + lax.ppermute(x, axis, pairs_of(n, b))  11.3 us
    ppermute x4, waiting for transfers between devices, halving_scatter(): got = lax.ppermute(send.astype(send_dtype), 'rows', pairs_of(n, b))  10.2 us
    ppermute x4, starting transfers between devices, halving_scatter(): got = lax.ppermute(send.astype(send_dtype), 'rows', pairs_of(n, b))  5.69 us
    ppermute x5, starting transfers between devices, doubling_sum(): x = x + lax.ppermute(x, axis, pairs_of(n, b))  4.43 us
  transfers between devices with their start and end apart: 18, of which 14 were waited for; matrix products, arithmetic and copies ran while one was open for 7% of the time, Pallas kernels for 0%

profile of v3, /device:TPU:0, one launch (start us, length us, event | category | flops | bytes accessed | tf_op | source)
XLA Modules:
  0.0 66.6 jit_solution(7270775357290881945)
XLA Ops:
  0.6 0.0 copy-start
  0.6 0.9 %slice_bitcast_fusion.5 = (bf16[1,1,1,1,128,128]{5,4,3,2,1,0:T(8,128)(2,1)S(1)}, bf16[1,1,1,1,128,128]{5,4,3,2,1,0:T(8,128)(2,1)S(1)}) fusion(bf16[128,256]{1,0:T(8,128)(2,1)} %param.6), kind=kLoop, calls=%fused_computation.43 | loop fusion | bytes 131072 | tf_op jit(solution)/shard_map/reshape | solution.py:28
  1.5 4.0 %collective-permute-start = (bf16[1,1,1,1,128,128]{5,4,3,2,1,0:T(8,128)(2,1)S(1)}, bf16[1,1,1,1,128,128]{5,4,3,2,1,0:T(8,128)(2,1)S(1)}, u32[]{:S(2)}, u32[]{:S(2)}) collective-permute-start(bf16[1,1,1,1,128,128]{5,4,3,2,1,0:T(8,128)(2,1)S(1)} %get-tuple-element.5), channel_id=1, source_target_pairs={{0,16},{2,18},{4,20},{6,22},{8,24},{10,26},{12,28},{14,30},{16,0},... | collective-permute-start | bytes 98312 | tf_op jit(solution)/shard_map/ppermute | solution.py:35
  5.6 0.1 collective-permute-start.4
  5.6 0.7 %broadcast_xor_fusion = s32[2,1,16]{2,1,0:T(1,128)S(1)} fusion(s32[2,1,16]{2,1,0:T(1,128)} %param.10, s32[]{:T(128)S(6)} %axis_index.27), kind=kLoop, calls=%fused_computation.51 | loop fusion | flops 32 | bytes 260 | tf_op jit(solution)/shard_map/xor | solution.py:128
  6.3 4.1 %collective-permute-done.4 = bf16[1,1,1,1,128,128]{5,4,3,2,1,0:T(8,128)(2,1)S(1)} collective-permute-done((bf16[1,1,1,1,128,128]{5,4,3,2,1,0:T(8,128)(2,1)S(1)}, bf16[1,1,1,1,128,128]{5,4,3,2,1,0:T(8,128)(2,1)S(1)}, u32[]{:S(2)}, u32[]{:S(2)}) %collective-permute-start.4) | collective-permute-done | bytes 32800 | tf_op jit(solution)/shard_map/ppermute | solution.py:35
  10.4 1.6 %collective-permute-start.5 = (bf16[2,1,1,1,128,128]{5,4,3,2,1,0:T(8,128)(2,1)S(1)}, bf16[2,1,1,1,128,128]{5,4,3,2,1,0:T(8,128)(2,1)S(1)}, u32[]{:S(2)}, u32[]{:S(2)}) collective-permute-start(bf16[2,1,1,1,128,128]{5,4,3,2,1,0:T(8,128)(2,1)S(1)} %pad_maximum_fusion.8), channel_id=1, source_target_pairs={{0,8},{2,10},{4,12},{6,14},{8,0},{10,2},{12,4},{14,6},{16,24},{18,... | collective-permute-start | bytes 196616 | tf_op jit(solution)/shard_map/ppermute | solution.py:35
  12.0 0.0 collective-permute-done
  12.0 0.5 collective-permute-start.1
  12.5 2.2 %collective-permute-done.5 = bf16[2,1,1,1,128,128]{5,4,3,2,1,0:T(8,128)(2,1)S(1)} collective-permute-done((bf16[2,1,1,1,128,128]{5,4,3,2,1,0:T(8,128)(2,1)S(1)}, bf16[2,1,1,1,128,128]{5,4,3,2,1,0:T(8,128)(2,1)S(1)}, u32[]{:S(2)}, u32[]{:S(2)}) %collective-permute-start.5) | collective-permute-done | bytes 65568 | tf_op jit(solution)/shard_map/ppermute | solution.py:35
  14.7 1.6 %collective-permute-start.6 = (bf16[2,2,1,1,128,128]{5,4,3,2,1,0:T(8,128)(2,1)S(1)}, bf16[2,2,1,1,128,128]{5,4,3,2,1,0:T(8,128)(2,1)S(1)}, u32[]{:S(2)}, u32[]{:S(2)}) collective-permute-start(bf16[2,2,1,1,128,128]{5,4,3,2,1,0:T(8,128)(2,1)S(1)} %pad_maximum_fusion.6), channel_id=1, source_target_pairs={{0,2},{2,0},{4,6},{6,4},{8,10},{10,8},{12,14},{14,12},{16,18},{18,... | collective-permute-start | bytes 393224 | tf_op jit(solution)/shard_map/ppermute | solution.py:35
  16.3 0.7 %iota_compare_fusion.1 = pred[2,16]{1,0:T(4,128)(4,1)S(1)} fusion(s32[2]{0:T(128)} %bitcast.91), kind=kLoop, calls=%fused_computation.49 | loop fusion | flops 32 | bytes 40 | tf_op jit(solution)/shard_map/lt | solution.py:127
  17.0 0.0 collective-permute-done.1
  17.0 1.6 %collective-permute-start.2 = (bf16[2,2,1,1,128,128]{5,4,3,2,1,0:T(8,128)(2,1)S(1)}, bf16[2,2,1,1,128,128]{5,4,3,2,1,0:T(8,128)(2,1)S(1)}, u32[]{:S(2)}, u32[]{:S(2)}) collective-permute-start(bf16[2,2,1,1,128,128]{5,4,3,2,1,0:T(8,128)(2,1)S(1)} %pad_maximum_fusion.5), channel_id=1, source_target_pairs={{0,4},{2,6},{4,0},{6,2},{8,12},{10,14},{12,8},{14,10},{16,20},{18,... | collective-permute-start | bytes 393224 | tf_op jit(solution)/shard_map/ppermute | solution.py:35
  18.6 1.1 %collective-permute-done.6 = bf16[2,2,1,1,128,128]{5,4,3,2,1,0:T(8,128)(2,1)S(1)} collective-permute-done((bf16[2,2,1,1,128,128]{5,4,3,2,1,0:T(8,128)(2,1)S(1)}, bf16[2,2,1,1,128,128]{5,4,3,2,1,0:T(8,128)(2,1)S(1)}, u32[]{:S(2)}, u32[]{:S(2)}) %collective-permute-start.6) | collective-permute-done | bytes 131104 | tf_op jit(solution)/shard_map/ppermute | solution.py:35
  19.8 1.6 %collective-permute-start.7 = (bf16[2,2,1,2,128,128]{5,4,3,2,1,0:T(8,128)(2,1)S(1)}, bf16[2,2,1,2,128,128]{5,4,3,2,1,0:T(8,128)(2,1)S(1)}, u32[]{:S(2)}, u32[]{:S(2)}) collective-permute-start(bf16[2,2,1,2,128,128]{5,4,3,2,1,0:T(8,128)(2,1)S(1)} %pad_maximum_fusion.3), channel_id=1, source_target_pairs={{0,4},{2,6},{4,0},{6,2},{8,12},{10,14},{12,8},{14,10},{16,20},{18,... | collective-permute-start | bytes 786440 | tf_op jit(solution)/shard_map/ppermute | solution.py:35
  21.4 0.0 copy-done
  21.4 0.7 %fusion.2 = bf16[2,16,128,128]{3,1,2,0:T(8,128)(2,1)S(1)} fusion(bf16[2,16,128,128]{3,2,1,0:T(8,128)(2,1)S(1)} %bitcast.82, s32[2,16]{1,0:T(2,128)S(1)} %bitcast.90, pred[2,16]{1,0:T(4,128)(4,1)S(1)} %iota_compare_fusion.1), kind=kOutput, calls=%fused_computation.8 | convolution fusion | flops 16778240 | bytes 2097312 | tf_op jit(solution)/shard_map/tsq,tsab->tqab/dot_general | solution.py:130
  22.1 1.1 %collective-permute-done.2 = bf16[2,2,1,1,128,128]{5,4,3,2,1,0:T(8,128)(2,1)S(1)} collective-permute-done((bf16[2,2,1,1,128,128]{5,4,3,2,1,0:T(8,128)(2,1)S(1)}, bf16[2,2,1,1,128,128]{5,4,3,2,1,0:T(8,128)(2,1)S(1)}, u32[]{:S(2)}, u32[]{:S(2)}) %collective-permute-start.2) | collective-permute-done | bytes 131104 | tf_op jit(solution)/shard_map/ppermute | solution.py:35
  23.3 1.1 %collective-permute-start.3 = (bf16[2,2,2,1,128,128]{5,4,3,2,1,0:T(8,128)(2,1)S(1)}, bf16[2,2,2,1,128,128]{5,4,3,2,1,0:T(8,128)(2,1)S(1)}, u32[]{:S(2)}, u32[]{:S(2)}) collective-permute-start(bf16[2,2,2,1,128,128]{5,4,3,2,1,0:T(8,128)(2,1)S(1)} %pad_maximum_fusion.2), channel_id=1, source_target_pairs={{0,2},{2,0},{4,6},{6,4},{8,10},{10,8},{12,14},{14,12},{16,18},{18,... | collective-permute-start | bytes 786440 | tf_op jit(solution)/shard_map/ppermute | solution.py:35
  24.4 1.8 %collective-permute-done.7 = bf16[2,2,1,2,128,128]{5,4,3,2,1,0:T(8,128)(2,1)S(1)} collective-permute-done((bf16[2,2,1,2,128,128]{5,4,3,2,1,0:T(8,128)(2,1)S(1)}, bf16[2,2,1,2,128,128]{5,4,3,2,1,0:T(8,128)(2,1)S(1)}, u32[]{:S(2)}, u32[]{:S(2)}) %collective-permute-start.7) | collective-permute-done | bytes 262176 | tf_op jit(solution)/shard_map/ppermute | solution.py:35
  26.2 0.1 pad_maximum_fusion.1
  26.3 0.5 convolution_bitcast_fusion.1
  26.8 0.0 copy-start.1
  26.8 0.0 copy-start.3
  26.8 2.9 %collective-permute-done.3 = bf16[2,2,2,1,128,128]{5,4,3,2,1,0:T(8,128)(2,1)S(1)} collective-permute-done((bf16[2,2,2,1,128,128]{5,4,3,2,1,0:T(8,128)(2,1)S(1)}, bf16[2,2,2,1,128,128]{5,4,3,2,1,0:T(8,128)(2,1)S(1)}, u32[]{:S(2)}, u32[]{:S(2)}) %collective-permute-start.3) | collective-permute-done | bytes 262176 | tf_op jit(solution)/shard_map/ppermute | solution.py:35
  29.7 0.1 pad_maximum_fusion
  29.8 0.5 convolution_bitcast_fusion.2
  30.3 0.1 collective-permute-start.8
  30.4 1.5 %collective-permute-done.8 = f32[2,128,256]{1,2,0:T(8,128)S(1)} collective-permute-done((f32[2,128,256]{1,2,0:T(8,128)S(1)}, f32[2,128,256]{1,2,0:T(8,128)S(1)}, u32[]{:S(2)}, u32[]{:S(2)}) %collective-permute-start.8) | collective-permute-done | bytes 262176 | tf_op jit(solution)/shard_map/ppermute | solution.py:96
  31.9 0.1 copy.23
  32.0 0.0 copy-done.1
  32.1 0.0 copy-done.3
  32.1 0.9 %multiply_convert_fusion = (bf16[256,256]{1,0:T(8,128)(2,1)S(1)}, f32[256,256]{1,0:T(8,128)S(1)}, f32[256,256]{1,0:T(8,128)}) fusion(bf16[256,256]{1,0:T(8,128)(2,1)S(1)} %copy-done.3, bf16[256,256]{1,0:T(8,128)(2,1)S(1)} %bitcast.87, bf16[256,256]{1,0:T(8,128)(2,1)S(1)} %copy-done.1), kind=kOutput, calls=%fused_computation.26 | convolution fusion | flops 34209792 | bytes 1048576 | tf_op jit(solution)/shard_map/dot_general | solution.py:148
  33.0 0.2 convolution_convert_fusion
  33.2 0.5 convolution_bitcast_fusion
  33.7 0.1 fusion.6
  33.8 1.1 %collective-permute-start.14 = (bf16[2,2,2,128,256]{4,3,2,1,0:T(8,128)(2,1)S(1)}, bf16[2,2,2,128,256]{4,3,2,1,0:T(8,128)(2,1)S(1)}, u32[]{:S(2)}, u32[]{:S(2)}) collective-permute-start(bf16[2,2,2,128,256]{4,3,2,1,0:T(8,128)(2,1)S(1)} %fusion.6), channel_id=1, source_target_pairs={{0,2},{2,0},{4,6},{6,4},{8,10},{10,8},{12,14},{14,12},{16,18},{18,... | collective-permute-start | bytes 1572872 | tf_op jit(solution)/shard_map/ppermute | solution.py:78
  34.9 0.2 fusion.20
  35.1 0.0 copy-start.2
  35.2 1.4 %collective-permute-start.9 = (f32[128,256]{1,0:T(8,128)S(1)}, f32[128,256]{1,0:T(8,128)S(1)}, u32[]{:S(2)}, u32[]{:S(2)}) collective-permute-start(f32[128,256]{1,0:T(8,128)S(1)} %constant_dynamic-slice_fusion), channel_id=1, source_target_pairs={{0,8},{2,10},{4,12},{6,14},{8,0},{10,2},{12,4},{14,6},{16,24},{18,... | collective-permute-start | bytes 393224 | tf_op jit(solution)/shard_map/ppermute | solution.py:96
  36.5 4.0 %collective-permute-done.9 = f32[128,256]{1,0:T(8,128)S(1)} collective-permute-done((f32[128,256]{1,0:T(8,128)S(1)}, f32[128,256]{1,0:T(8,128)S(1)}, u32[]{:S(2)}, u32[]{:S(2)}) %collective-permute-start.9) | collective-permute-done | bytes 131104 | tf_op jit(solution)/shard_map/ppermute | solution.py:96
  40.5 1.2 %collective-permute-start.10 = (f32[128,256]{1,0:T(8,128)S(1)}, f32[128,256]{1,0:T(8,128)S(1)}, u32[]{:S(2)}, u32[]{:S(2)}) collective-permute-start(f32[128,256]{1,0:T(8,128)S(1)} %fusion.30), channel_id=1, source_target_pairs={{0,16},{2,18},{4,20},{6,22},{8,24},{10,26},{12,28},{14,30},{16,0},... | collective-permute-start | bytes 393224 | tf_op jit(solution)/shard_map/ppermute | solution.py:96
  41.7 6.1 %collective-permute-done.14 = bf16[2,2,2,128,256]{4,3,2,1,0:T(8,128)(2,1)S(1)} collective-permute-done((bf16[2,2,2,128,256]{4,3,2,1,0:T(8,128)(2,1)S(1)}, bf16[2,2,2,128,256]{4,3,2,1,0:T(8,128)(2,1)S(1)}, u32[]{:S(2)}, u32[]{:S(2)}) %collective-permute-start.14) | collective-permute-done | bytes 524320 | tf_op jit(solution)/shard_map/ppermute | solution.py:78
  47.8 0.1 fusion
  48.0 1.6 %collective-permute-start.15 = (bf16[2,2,128,256]{3,2,1,0:T(8,128)(2,1)S(1)}, bf16[2,2,128,256]{3,2,1,0:T(8,128)(2,1)S(1)}, u32[]{:S(2)}, u32[]{:S(2)}) collective-permute-start(bf16[2,2,128,256]{3,2,1,0:T(8,128)(2,1)S(1)} %fusion.8), channel_id=1, source_target_pairs={{0,4},{2,6},{4,0},{6,2},{8,12},{10,14},{12,8},{14,10},{16,20},{18,... | collective-permute-start | bytes 786440 | tf_op jit(solution)/shard_map/ppermute | solution.py:78
  49.6 0.0 collective-permute-done.10
  49.6 1.1 %collective-permute-start.11 = (f32[128,256]{1,0:T(8,128)S(1)}, f32[128,256]{1,0:T(8,128)S(1)}, u32[]{:S(2)}, u32[]{:S(2)}) collective-permute-start(f32[128,256]{1,0:T(8,128)S(1)} %add.42), channel_id=1, source_target_pairs={{0,2},{2,0},{4,6},{6,4},{8,10},{10,8},{12,14},{14,12},{16,18},{18,... | collective-permute-start | bytes 393224 | tf_op jit(solution)/shard_map/ppermute | solution.py:96
  50.7 0.0 copy-done.2
  50.7 0.6 fusion.13
  51.4 3.3 %collective-permute-done.11 = f32[128,256]{1,0:T(8,128)S(1)} collective-permute-done((f32[128,256]{1,0:T(8,128)S(1)}, f32[128,256]{1,0:T(8,128)S(1)}, u32[]{:S(2)}, u32[]{:S(2)}) %collective-permute-start.11) | collective-permute-done | bytes 131104 | tf_op jit(solution)/shard_map/ppermute | solution.py:96
  54.6 0.7 %collective-permute-start.12 = (f32[128,256]{1,0:T(8,128)S(1)}, f32[128,256]{1,0:T(8,128)S(1)}, u32[]{:S(2)}, u32[]{:S(2)}) collective-permute-start(f32[128,256]{1,0:T(8,128)S(1)} %add.43), channel_id=1, source_target_pairs={{0,4},{2,6},{4,0},{6,2},{8,12},{10,14},{12,8},{14,10},{16,20},{18,... | collective-permute-start | bytes 393224 | tf_op jit(solution)/shard_map/ppermute | solution.py:96
  55.3 0.2 collective-permute-done.15
  55.6 0.1 fusion.7
  55.7 1.4 %collective-permute-start.16 = (bf16[2,128,256]{2,1,0:T(8,128)(2,1)S(1)}, bf16[2,128,256]{2,1,0:T(8,128)(2,1)S(1)}, u32[]{:S(2)}, u32[]{:S(2)}) collective-permute-start(bf16[2,128,256]{2,1,0:T(8,128)(2,1)S(1)} %fusion.10), channel_id=1, source_target_pairs={{0,8},{2,10},{4,12},{6,14},{8,0},{10,2},{12,4},{14,6},{16,24},{18,... | collective-permute-start | bytes 393224 | tf_op jit(solution)/shard_map/ppermute | solution.py:78
  57.1 2.6 %collective-permute-done.12 = f32[128,256]{1,0:T(8,128)S(1)} collective-permute-done((f32[128,256]{1,0:T(8,128)S(1)}, f32[128,256]{1,0:T(8,128)S(1)}, u32[]{:S(2)}, u32[]{:S(2)}) %collective-permute-start.12) | collective-permute-done | bytes 131104 | tf_op jit(solution)/shard_map/ppermute | solution.py:96
  59.7 0.1 collective-permute-start.13
  59.8 0.9 %collective-permute-done.16 = bf16[2,128,256]{2,1,0:T(8,128)(2,1)S(1)} collective-permute-done((bf16[2,128,256]{2,1,0:T(8,128)(2,1)S(1)}, bf16[2,128,256]{2,1,0:T(8,128)(2,1)S(1)}, u32[]{:S(2)}, u32[]{:S(2)}) %collective-permute-start.16) | collective-permute-done | bytes 131104 | tf_op jit(solution)/shard_map/ppermute | solution.py:78
  60.7 1.5 %collective-permute-start.17 = (bf16[128,256]{1,0:T(8,128)(2,1)S(1)}, bf16[128,256]{1,0:T(8,128)(2,1)S(1)}, u32[]{:S(2)}, u32[]{:S(2)}) collective-permute-start(bf16[128,256]{1,0:T(8,128)(2,1)S(1)} %fusion.14), channel_id=1, source_target_pairs={{0,16},{2,18},{4,20},{6,22},{8,24},{10,26},{12,28},{14,30},{16,0},... | collective-permute-start | bytes 196616 | tf_op jit(solution)/shard_map/ppermute | solution.py:78
  62.3 0.0 collective-permute-done.13
  62.3 0.7 %maximum_select_fusion = f32[2,128,256]{2,1,0:T(8,128)} fusion(f32[1,128,256]{2,1,0:T(8,128)S(1)} %collective-permute-done.13, f32[1,128,256]{2,1,0:T(8,128)S(1)} %add_bitcast_fusion, pred[]{:T(512)S(6)} %eq.19), kind=kLoop, calls=%fused_computation.25 | loop fusion | flops 196608 | bytes 524289 | tf_op jit(solution)/shard_map/jit(_where)/select_n | solution.py:106
  63.0 3.0 %collective-permute-done.17 = bf16[128,256]{1,0:T(8,128)(2,1)S(1)} collective-permute-done((bf16[128,256]{1,0:T(8,128)(2,1)S(1)}, bf16[128,256]{1,0:T(8,128)(2,1)S(1)}, u32[]{:S(2)}, u32[]{:S(2)}) %collective-permute-start.17) | collective-permute-done | bytes 65568 | tf_op jit(solution)/shard_map/ppermute | solution.py:78
  66.0 0.6 fusion.12
  (17 shorter events, 0.3 us)
Async XLA Ops:
  0.6 20.7 %copy-start = (bf16[2,1,16,128,128]{4,3,2,1,0:T(8,128)(2,1)S(1)}, bf16[2,1,16,128,128]{4,3,2,1,0:T(8,128)(2,1)}, u32[]{:S(2)}) copy-start(bf16[2,1,16,128,128]{4,3,2,1,0:T(8,128)(2,1)} %param.9) | copy-start | bytes 3145732
  1.5 10.5 %collective-permute-start = (bf16[1,1,1,1,128,128]{5,4,3,2,1,0:T(8,128)(2,1)S(1)}, bf16[1,1,1,1,128,128]{5,4,3,2,1,0:T(8,128)(2,1)S(1)}, u32[]{:S(2)}, u32[]{:S(2)}) collective-permute-start(bf16[1,1,1,1,128,128]{5,4,3,2,1,0:T(8,128)(2,1)S(1)} %get-tuple-element.5), channel_id=1, source_target_pairs={{0,16},{2,18},{4,20},{6,22},{8,24},{10,26},{12,28},{14,30},{16,0},... | collective-permute-start | bytes 98312 | tf_op jit(solution)/shard_map/ppermute | solution.py:35
  5.6 4.8 %collective-permute-start.4 = (bf16[1,1,1,1,128,128]{5,4,3,2,1,0:T(8,128)(2,1)S(1)}, bf16[1,1,1,1,128,128]{5,4,3,2,1,0:T(8,128)(2,1)S(1)}, u32[]{:S(2)}, u32[]{:S(2)}) collective-permute-start(bf16[1,1,1,1,128,128]{5,4,3,2,1,0:T(8,128)(2,1)S(1)} %get-tuple-element.6), channel_id=1, source_target_pairs={{0,16},{2,18},{4,20},{6,22},{8,24},{10,26},{12,28},{14,30},{16,0},... | collective-permute-start | bytes 98312 | tf_op jit(solution)/shard_map/ppermute | solution.py:35
  10.4 4.3 %collective-permute-start.5 = (bf16[2,1,1,1,128,128]{5,4,3,2,1,0:T(8,128)(2,1)S(1)}, bf16[2,1,1,1,128,128]{5,4,3,2,1,0:T(8,128)(2,1)S(1)}, u32[]{:S(2)}, u32[]{:S(2)}) collective-permute-start(bf16[2,1,1,1,128,128]{5,4,3,2,1,0:T(8,128)(2,1)S(1)} %pad_maximum_fusion.8), channel_id=1, source_target_pairs={{0,8},{2,10},{4,12},{6,14},{8,0},{10,2},{12,4},{14,6},{16,24},{18,... | collective-permute-start | bytes 196616 | tf_op jit(solution)/shard_map/ppermute | solution.py:35
  12.0 5.0 %collective-permute-start.1 = (bf16[2,1,1,1,128,128]{5,4,3,2,1,0:T(8,128)(2,1)S(1)}, bf16[2,1,1,1,128,128]{5,4,3,2,1,0:T(8,128)(2,1)S(1)}, u32[]{:S(2)}, u32[]{:S(2)}) collective-permute-start(bf16[2,1,1,1,128,128]{5,4,3,2,1,0:T(8,128)(2,1)S(1)} %pad_maximum_fusion.7), channel_id=1, source_target_pairs={{0,8},{2,10},{4,12},{6,14},{8,0},{10,2},{12,4},{14,6},{16,24},{18,... | collective-permute-start | bytes 196616 | tf_op jit(solution)/shard_map/ppermute | solution.py:35
  14.7 5.0 %collective-permute-start.6 = (bf16[2,2,1,1,128,128]{5,4,3,2,1,0:T(8,128)(2,1)S(1)}, bf16[2,2,1,1,128,128]{5,4,3,2,1,0:T(8,128)(2,1)S(1)}, u32[]{:S(2)}, u32[]{:S(2)}) collective-permute-start(bf16[2,2,1,1,128,128]{5,4,3,2,1,0:T(8,128)(2,1)S(1)} %pad_maximum_fusion.6), channel_id=1, source_target_pairs={{0,2},{2,0},{4,6},{6,4},{8,10},{10,8},{12,14},{14,12},{16,18},{18,... | collective-permute-start | bytes 393224 | tf_op jit(solution)/shard_map/ppermute | solution.py:35
  17.0 6.2 %collective-permute-start.2 = (bf16[2,2,1,1,128,128]{5,4,3,2,1,0:T(8,128)(2,1)S(1)}, bf16[2,2,1,1,128,128]{5,4,3,2,1,0:T(8,128)(2,1)S(1)}, u32[]{:S(2)}, u32[]{:S(2)}) collective-permute-start(bf16[2,2,1,1,128,128]{5,4,3,2,1,0:T(8,128)(2,1)S(1)} %pad_maximum_fusion.5), channel_id=1, source_target_pairs={{0,4},{2,6},{4,0},{6,2},{8,12},{10,14},{12,8},{14,10},{16,20},{18,... | collective-permute-start | bytes 393224 | tf_op jit(solution)/shard_map/ppermute | solution.py:35
  19.8 6.4 %collective-permute-start.7 = (bf16[2,2,1,2,128,128]{5,4,3,2,1,0:T(8,128)(2,1)S(1)}, bf16[2,2,1,2,128,128]{5,4,3,2,1,0:T(8,128)(2,1)S(1)}, u32[]{:S(2)}, u32[]{:S(2)}) collective-permute-start(bf16[2,2,1,2,128,128]{5,4,3,2,1,0:T(8,128)(2,1)S(1)} %pad_maximum_fusion.3), channel_id=1, source_target_pairs={{0,4},{2,6},{4,0},{6,2},{8,12},{10,14},{12,8},{14,10},{16,20},{18,... | collective-permute-start | bytes 786440 | tf_op jit(solution)/shard_map/ppermute | solution.py:35
  23.3 6.4 %collective-permute-start.3 = (bf16[2,2,2,1,128,128]{5,4,3,2,1,0:T(8,128)(2,1)S(1)}, bf16[2,2,2,1,128,128]{5,4,3,2,1,0:T(8,128)(2,1)S(1)}, u32[]{:S(2)}, u32[]{:S(2)}) collective-permute-start(bf16[2,2,2,1,128,128]{5,4,3,2,1,0:T(8,128)(2,1)S(1)} %pad_maximum_fusion.2), channel_id=1, source_target_pairs={{0,2},{2,0},{4,6},{6,4},{8,10},{10,8},{12,14},{14,12},{16,18},{18,... | collective-permute-start | bytes 786440 | tf_op jit(solution)/shard_map/ppermute | solution.py:35
  26.8 5.3 %copy-start.1 = (bf16[256,256]{1,0:T(8,128)(2,1)S(1)}, bf16[256,256]{1,0:T(8,128)(2,1)}, u32[]{:S(2)}) copy-start(bf16[256,256]{1,0:T(8,128)(2,1)} %param.8) | copy-start | bytes 393220
  26.8 5.3 %copy-start.3 = (bf16[256,256]{1,0:T(8,128)(2,1)S(1)}, bf16[256,256]{1,0:T(8,128)(2,1)}, u32[]{:S(2)}) copy-start(bf16[256,256]{1,0:T(8,128)(2,1)} %param.7) | copy-start | bytes 393220
  30.3 1.6 %collective-permute-start.8 = (f32[2,128,256]{1,2,0:T(8,128)S(1)}, f32[2,128,256]{1,2,0:T(8,128)S(1)}, u32[]{:S(2)}, u32[]{:S(2)}) collective-permute-start(f32[2,128,256]{1,2,0:T(8,128)S(1)} %pad_maximum_fusion.4), channel_id=1, source_target_pairs={{0,1},{1,0},{2,3},{3,2},{4,5},{5,4},{6,7},{7,6},{8,9},{9,8},{10,11... | collective-permute-start | bytes 786440 | tf_op jit(solution)/shard_map/ppermute | solution.py:96
  33.8 14.0 %collective-permute-start.14 = (bf16[2,2,2,128,256]{4,3,2,1,0:T(8,128)(2,1)S(1)}, bf16[2,2,2,128,256]{4,3,2,1,0:T(8,128)(2,1)S(1)}, u32[]{:S(2)}, u32[]{:S(2)}) collective-permute-start(bf16[2,2,2,128,256]{4,3,2,1,0:T(8,128)(2,1)S(1)} %fusion.6), channel_id=1, source_target_pairs={{0,2},{2,0},{4,6},{6,4},{8,10},{10,8},{12,14},{14,12},{16,18},{18,... | collective-permute-start | bytes 1572872 | tf_op jit(solution)/shard_map/ppermute | solution.py:78
  35.1 15.6 %copy-start.2 = (f32[256,256]{1,0:T(8,128)S(1)}, f32[256,256]{1,0:T(8,128)}, u32[]{:S(2)}) copy-start(f32[256,256]{1,0:T(8,128)} %get-tuple-element.7) | copy-start | bytes 786436
  35.2 5.3 %collective-permute-start.9 = (f32[128,256]{1,0:T(8,128)S(1)}, f32[128,256]{1,0:T(8,128)S(1)}, u32[]{:S(2)}, u32[]{:S(2)}) collective-permute-start(f32[128,256]{1,0:T(8,128)S(1)} %constant_dynamic-slice_fusion), channel_id=1, source_target_pairs={{0,8},{2,10},{4,12},{6,14},{8,0},{10,2},{12,4},{14,6},{16,24},{18,... | collective-permute-start | bytes 393224 | tf_op jit(solution)/shard_map/ppermute | solution.py:96
  40.5 9.1 %collective-permute-start.10 = (f32[128,256]{1,0:T(8,128)S(1)}, f32[128,256]{1,0:T(8,128)S(1)}, u32[]{:S(2)}, u32[]{:S(2)}) collective-permute-start(f32[128,256]{1,0:T(8,128)S(1)} %fusion.30), channel_id=1, source_target_pairs={{0,16},{2,18},{4,20},{6,22},{8,24},{10,26},{12,28},{14,30},{16,0},... | collective-permute-start | bytes 393224 | tf_op jit(solution)/shard_map/ppermute | solution.py:96
  48.0 7.6 %collective-permute-start.15 = (bf16[2,2,128,256]{3,2,1,0:T(8,128)(2,1)S(1)}, bf16[2,2,128,256]{3,2,1,0:T(8,128)(2,1)S(1)}, u32[]{:S(2)}, u32[]{:S(2)}) collective-permute-start(bf16[2,2,128,256]{3,2,1,0:T(8,128)(2,1)S(1)} %fusion.8), channel_id=1, source_target_pairs={{0,4},{2,6},{4,0},{6,2},{8,12},{10,14},{12,8},{14,10},{16,20},{18,... | collective-permute-start | bytes 786440 | tf_op jit(solution)/shard_map/ppermute | solution.py:78
  49.6 5.0 %collective-permute-start.11 = (f32[128,256]{1,0:T(8,128)S(1)}, f32[128,256]{1,0:T(8,128)S(1)}, u32[]{:S(2)}, u32[]{:S(2)}) collective-permute-start(f32[128,256]{1,0:T(8,128)S(1)} %add.42), channel_id=1, source_target_pairs={{0,2},{2,0},{4,6},{6,4},{8,10},{10,8},{12,14},{14,12},{16,18},{18,... | collective-permute-start | bytes 393224 | tf_op jit(solution)/shard_map/ppermute | solution.py:96
  54.6 5.0 %collective-permute-start.12 = (f32[128,256]{1,0:T(8,128)S(1)}, f32[128,256]{1,0:T(8,128)S(1)}, u32[]{:S(2)}, u32[]{:S(2)}) collective-permute-start(f32[128,256]{1,0:T(8,128)S(1)} %add.43), channel_id=1, source_target_pairs={{0,4},{2,6},{4,0},{6,2},{8,12},{10,14},{12,8},{14,10},{16,20},{18,... | collective-permute-start | bytes 393224 | tf_op jit(solution)/shard_map/ppermute | solution.py:96
  55.7 5.0 %collective-permute-start.16 = (bf16[2,128,256]{2,1,0:T(8,128)(2,1)S(1)}, bf16[2,128,256]{2,1,0:T(8,128)(2,1)S(1)}, u32[]{:S(2)}, u32[]{:S(2)}) collective-permute-start(bf16[2,128,256]{2,1,0:T(8,128)(2,1)S(1)} %fusion.10), channel_id=1, source_target_pairs={{0,8},{2,10},{4,12},{6,14},{8,0},{10,2},{12,4},{14,6},{16,24},{18,... | collective-permute-start | bytes 393224 | tf_op jit(solution)/shard_map/ppermute | solution.py:78
  59.7 2.6 %collective-permute-start.13 = (f32[1,128,256]{2,1,0:T(8,128)S(1)}, f32[1,128,256]{2,1,0:T(8,128)S(1)}, u32[]{:S(2)}, u32[]{:S(2)}) collective-permute-start(f32[1,128,256]{2,1,0:T(8,128)S(1)} %add_bitcast_fusion), channel_id=1, source_target_pairs={{0,1},{1,0},{2,3},{3,2},{4,5},{5,4},{6,7},{7,6},{8,9},{9,8},{10,11... | collective-permute-start | bytes 393224 | tf_op jit(solution)/shard_map/ppermute | solution.py:104
  60.7 5.2 %collective-permute-start.17 = (bf16[128,256]{1,0:T(8,128)(2,1)S(1)}, bf16[128,256]{1,0:T(8,128)(2,1)S(1)}, u32[]{:S(2)}, u32[]{:S(2)}) collective-permute-start(bf16[128,256]{1,0:T(8,128)(2,1)S(1)} %fusion.14), channel_id=1, source_target_pairs={{0,16},{2,18},{4,20},{6,22},{8,24},{10,26},{12,28},{14,30},{16,0},... | collective-permute-start | bytes 196616 | tf_op jit(solution)/shard_map/ppermute | solution.py:78

commit v4 on v3

--- a/solution.py
+++ b/solution.py
@@ -7,6 +7,8 @@
 SCATTER_PARTS = 1
 W_PACKED = False
 PIPE_FWD = False
+RADIX4_GATHER = True
+RADIX4_SCATTER = True
 
 
 def bit_count(n):
@@ -107,6 +109,58 @@
     return buf
 
 
+def bit_rounds(nb):
+    rounds = []
+    top = nb
+    while top > 0:
+        rounds.append(tuple(range(max(top - 2, 0), top)))
+        top -= 2
+    return rounds
+
+
+def radix_gather(x, n):
+    nb = bit_count(n)
+    held = x.reshape((1,) * nb + x.shape)
+    for bits in bit_rounds(nb):
+        if len(bits) == 1:
+            got = lax.ppermute(held, "rows", pairs_of(n, bits[0]))
+            held = jnp.concatenate([held, got], axis=nb - 1 - bits[0])
+            continue
+        low, high = bits
+        got_low = lax.ppermute(held, "rows", pairs_of(n, low))
+        got_high = lax.ppermute(held, "rows", pairs_of(n, high))
+        got_both = lax.ppermute(held, "rows", [(j, j ^ (1 << low) ^ (1 << high)) for j in range(n)])
+        first = jnp.concatenate([held, got_low], axis=nb - 1 - low)
+        second = jnp.concatenate([got_high, got_both], axis=nb - 1 - low)
+        held = jnp.concatenate([first, second], axis=nb - 1 - high)
+    return held
+
+
+def radix_scatter(rel, n, send_dtype):
+    nb = bit_count(n)
+    cur = rel
+    for bits in bit_rounds(nb)[::-1]:
+        lead = cur.ndim - 2
+        if len(bits) == 1:
+            ax = lead - 1
+            keep = lax.index_in_dim(cur, 0, ax, keepdims=False)
+            send = lax.index_in_dim(cur, 1, ax, keepdims=False)
+            got = lax.ppermute(send.astype(send_dtype), "rows", pairs_of(n, bits[0]))
+            cur = keep + got.astype(jnp.float32)
+            continue
+        low, high = bits
+        def part(h, l):
+            return lax.index_in_dim(lax.index_in_dim(cur, h, lead - 2, keepdims=False), l, lead - 2, keepdims=False)
+        keep = part(0, 0)
+        got_low = lax.ppermute(part(0, 1).astype(send_dtype), "rows", pairs_of(n, low))
+        got_high = lax.ppermute(part(1, 0).astype(send_dtype), "rows", pairs_of(n, high))
+        got_both = lax.ppermute(
+            part(1, 1).astype(send_dtype), "rows", [(j, j ^ (1 << low) ^ (1 << high)) for j in range(n)]
+        )
+        cur = keep + (got_low.astype(jnp.float32) + got_high.astype(jnp.float32) + got_both.astype(jnp.float32))
+    return cur
+
+
 def local(features, cotangent, weight, tile_vals, tile_cols, tile_count):
     n_rows = lax.axis_size("rows")
     n_rep = lax.axis_size("rep")
@@ -132,16 +186,24 @@
     )
     sorted_rel = sorted_rel.reshape((panel_tiles,) + (2,) * nb + (tile, tile))
 
-    down = list(range(nb - 1, -1, -1))
-    gather_orders = [down, down[:-2] + [down[-1], down[-2]]][:GATHER_PARTS] if nb >= 2 else [down]
-    width = feat_width // len(gather_orders)
-    partial_value = jnp.concatenate(
-        [
-            gather_contract(features[:, k * width:(k + 1) * width], sorted_rel, order, n_rows)
-            for k, order in enumerate(gather_orders)
-        ],
-        axis=-1,
-    )
+    if RADIX4_GATHER:
+        held = radix_gather(features, n_rows)
+        every = sorted_rel.reshape(panel_tiles, n_rows, tile, tile)
+        partial_value = jnp.einsum(
+            "tqab,qbf->taf", every, held.reshape(n_rows, block_rows, feat_width),
+            preferred_element_type=jnp.float32,
+        )
+    else:
+        down = list(range(nb - 1, -1, -1))
+        gather_orders = [down, down[:-2] + [down[-1], down[-2]]][:GATHER_PARTS] if nb >= 2 else [down]
+        width = feat_width // len(gather_orders)
+        partial_value = jnp.concatenate(
+            [
+                gather_contract(features[:, k * width:(k + 1) * width], sorted_rel, order, n_rows)
+                for k, order in enumerate(gather_orders)
+            ],
+            axis=-1,
+        )
     panel_sum = doubling_sum(partial_value, "rep", n_rep, rep_bits)
     aggregated = panel_sum.reshape(panel_tiles * tile, feat_width).astype(jnp.bfloat16)
 
@@ -169,6 +231,8 @@
     flat_rel = sorted_rel.reshape(panel_tiles, n_rows, tile, tile)
     up = list(range(nb))
     scatter_orders = ([up, [up[1], up[0]] + up[2:]] if nb >= 2 else [up])[:SCATTER_PARTS]
+    if RADIX4_SCATTER:
+        scatter_orders = [None]
     width = feat_width // len(scatter_orders)
     pieces = []
     for k, order in enumerate(scatter_orders):
@@ -179,6 +243,9 @@
             preferred_element_type=jnp.float32,
         )
         products = products.reshape((2,) * nb + (block_rows, width))
+        if order is None:
+            pieces.append(radix_scatter(products, n_rows, jnp.bfloat16))
+            continue
         extra = w_slice.reshape(-1, width) if (W_PACKED and k == 0) else None
         piece, extra = halving_scatter(products, order, n_rows, jnp.bfloat16, extra)
         if extra is not None:

time: 66.8 us -> 64 us (0.958)
  other arithmetic: 3.94 us -> 7.44 us
  waiting for transfers between devices: 34.8 us -> 31.3 us
  starting transfers between devices: 22.3 us -> 20.7 us
  local copies, waits for them, and re-layouts: 1.14 us -> 0.28 us
    ppermute x12, waiting for transfers between devices: 23.5 us -> 19 us  [the longest x2 12.2 us: radix_gather(): got_high = lax.ppermute(held, 'rows', pairs_of(n, high))]
    ppermute x12, starting transfers between devices: 17.8 us -> 16.5 us  [the longest x2 6.55 us: radix_gather(): lax.ppermute(held, 'rows', [(j, j ^ 1 << low ^ 1 << high) for j in range(...]
    another operation x0 -> x1, other arithmetic: none -> 1.07 us
    ppermute x5, waiting for transfers between devices: 11.3 us -> 12.4 us  [doubling_sum(): x = x + lax.ppermute(x, axis, pairs_of(n, b))]
    convert_element_type x1, other arithmetic: 0.64 us -> 1.61 us  [local(): output = (preact * sigmoid_part).astype(jnp.bfloat16)]
    add x3, other arithmetic: 0.05 us -> 0.95 us  [doubling_sum(): x = x + lax.ppermute(x, axis, pairs_of(n, b))]
    reshape x1 -> x0, local copies, waits for them, and re-layouts: 0.87 us -> none  [gather_contract(): held = x_part.reshape((1,) * nb + x_part.shape)]
    concatenate x9 -> x2, other arithmetic: 0.22 us -> 0.96 us  [radix_gather(): held = jnp.concatenate([first, second], axis=nb - 1 - high)]
  transfers between devices with their start and end apart: 18 -> 18, of which waited for: 14 -> 11; matrix products, arithmetic and copies ran while one was open for 7% -> 10% of each run, Pallas kernels for 0% -> 0%
where the time goes in v4:
time: 64 us; the launch traced here: 63.8 us
  waiting for transfers between devices  31.3 us (49%)
  starting transfers between devices  20.7 us (32%)
  other arithmetic  7.44 us (12%)
  matrix products  3.14 us (5%)
  between operations  0.82 us (1%)
    ppermute x5, waiting for transfers between devices, doubling_sum(): x = x + lax.ppermute(x, axis, pairs_of(n, b))  12.4 us
    ppermute x2, waiting for transfers between devices, radix_gather(): got_high = lax.ppermute(held, 'rows', pairs_of(n, high))  12.2 us
    ppermute x2, starting transfers between devices, radix_gather(): lax.ppermute(held, 'rows', [(j, j ^ 1 << low ^ 1 << high) for j in range(...  6.55 us
    ppermute x5, starting transfers between devices, doubling_sum(): x = x + lax.ppermute(x, axis, pairs_of(n, b))  4.19 us
    ppermute x2, starting transfers between devices, radix_scatter(): lax.ppermute(part(1, 0).astype(send_dtype), 'rows', pairs_of(n, high))  3.67 us
    ppermute x2, waiting for transfers between devices, radix_scatter(): lax.ppermute(part(1, 0).astype(send_dtype), 'rows', pairs_of(n, high))  2.02 us
    ppermute x2, starting transfers between devices, radix_scatter(): lax.ppermute(part(1, 1).astype(send_dtype), 'rows', [(j, j ^ 1 << low ^ 1...  1.79 us
    ppermute x2, starting transfers between devices, radix_scatter(): lax.ppermute(part(0, 1).astype(send_dtype), 'rows', pairs_of(n, low))  1.7 us
  transfers between devices with their start and end apart: 18, of which 11 were waited for; matrix products, arithmetic and copies ran while one was open for 10% of the time, Pallas kernels for 0%

profile of v4, /device:TPU:0, one launch (start us, length us, event | category | flops | bytes accessed | tf_op | source)
XLA Modules:
  0.0 63.8 jit_solution(16308986736100059764)
XLA Ops:
  0.6 0.0 copy-start
  0.6 0.0 copy-start.1
  0.7 5.1 %collective-permute-start.2 = (bf16[1,1,1,1,128,256]{5,4,3,2,1,0:T(8,128)(2,1)}, bf16[1,1,1,1,128,256]{5,4,3,2,1,0:T(8,128)(2,1)S(1)}, u32[]{:S(2)}, u32[]{:S(2)}) collective-permute-start(bf16[1,1,1,1,128,256]{5,4,3,2,1,0:T(8,128)(2,1)} %bitcast.74), channel_id=1, source_target_pairs={{0,24},{2,26},{4,28},{6,30},{8,16},{10,18},{12,20},{14,22},{16,8},... | collective-permute-start | bytes 196616 | tf_op jit(solution)/shard_map/ppermute | solution.py:132
  5.8 0.0 collective-permute-start.1
  5.8 0.6 %collective-permute-start = (bf16[1,1,1,1,128,256]{5,4,3,2,1,0:T(8,128)(2,1)}, bf16[1,1,1,1,128,256]{5,4,3,2,1,0:T(8,128)(2,1)S(1)}, u32[]{:S(2)}, u32[]{:S(2)}) collective-permute-start(bf16[1,1,1,1,128,256]{5,4,3,2,1,0:T(8,128)(2,1)} %bitcast.76), channel_id=1, source_target_pairs={{0,8},{2,10},{4,12},{6,14},{8,0},{10,2},{12,4},{14,6},{16,24},{18,... | collective-permute-start | bytes 196616 | tf_op jit(solution)/shard_map/ppermute | solution.py:130
  6.4 0.7 %broadcast_xor_fusion = s32[2,1,16]{2,1,0:T(1,128)S(1)} fusion(s32[2,1,16]{2,1,0:T(1,128)} %param.10, s32[]{:T(128)S(6)} %axis_index.27), kind=kLoop, calls=%fused_computation.38 | loop fusion | flops 32 | bytes 260 | tf_op jit(solution)/shard_map/xor | solution.py:182
  7.1 0.7 %iota_compare_fusion.1 = pred[2,16]{1,0:T(4,128)(4,1)S(1)} fusion(s32[2]{0:T(128)} %bitcast.80), kind=kLoop, calls=%fused_computation.36 | loop fusion | flops 32 | bytes 40 | tf_op jit(solution)/shard_map/lt | solution.py:181
  7.8 0.8 %collective-permute-done.2 = bf16[1,1,1,1,128,256]{5,4,3,2,1,0:T(8,128)(2,1)S(1)} collective-permute-done((bf16[1,1,1,1,128,256]{5,4,3,2,1,0:T(8,128)(2,1)}, bf16[1,1,1,1,128,256]{5,4,3,2,1,0:T(8,128)(2,1)S(1)}, u32[]{:S(2)}, u32[]{:S(2)}) %collective-permute-start.2) | collective-permute-done | bytes 65568 | tf_op jit(solution)/shard_map/ppermute | solution.py:132
  8.6 3.0 %collective-permute-done.1 = bf16[1,1,1,1,128,256]{5,4,3,2,1,0:T(8,128)(2,1)S(1)} collective-permute-done((bf16[1,1,1,1,128,256]{5,4,3,2,1,0:T(8,128)(2,1)}, bf16[1,1,1,1,128,256]{5,4,3,2,1,0:T(8,128)(2,1)S(1)}, u32[]{:S(2)}, u32[]{:S(2)}) %collective-permute-start.1) | collective-permute-done | bytes 65568 | tf_op jit(solution)/shard_map/ppermute | solution.py:131
  11.6 0.0 collective-permute-done
  11.6 0.9 %maximum_maximum_fusion.1 = bf16[2,2,1,1,128,256]{5,4,3,2,1,0:T(8,128)(2,1)S(1)} fusion(bf16[1,1,1,1,128,256]{5,4,3,2,1,0:T(8,128)(2,1)S(1)} %collective-permute-done.2, bf16[1,1,1,1,128,256]{5,4,3,2,1,0:T(8,128)(2,1)S(1)} %collective-permute-done.1, bf16[1,1,1,1,128,256]{5,4,3,2,1,0:T(8,128)(2,1)S(1)} %collective-permute-done, ...), kind=kLoop, calls=%fused_computation.17 | loop fusion | flops 393216 | bytes 524288 | tf_op jit(solution)/shard_map/concatenate | solution.py:135
  12.5 1.6 %collective-permute-start.4 = (bf16[2,2,1,1,128,256]{5,4,3,2,1,0:T(8,128)(2,1)S(1)}, bf16[2,2,1,1,128,256]{5,4,3,2,1,0:T(8,128)(2,1)S(1)}, u32[]{:S(2)}, u32[]{:S(2)}) collective-permute-start(bf16[2,2,1,1,128,256]{5,4,3,2,1,0:T(8,128)(2,1)S(1)} %maximum_maximum_fusion.1), channel_id=1, source_target_pairs={{0,4},{2,6},{4,0},{6,2},{8,12},{10,14},{12,8},{14,10},{16,20},{18,... | collective-permute-start | bytes 786440 | tf_op jit(solution)/shard_map/ppermute | solution.py:131
  14.0 1.4 %collective-permute-start.5 = (bf16[2,2,1,1,128,256]{5,4,3,2,1,0:T(8,128)(2,1)S(1)}, bf16[2,2,1,1,128,256]{5,4,3,2,1,0:T(8,128)(2,1)S(1)}, u32[]{:S(2)}, u32[]{:S(2)}) collective-permute-start(bf16[2,2,1,1,128,256]{5,4,3,2,1,0:T(8,128)(2,1)S(1)} %maximum_maximum_fusion.1), channel_id=1, source_target_pairs={{0,6},{2,4},{4,2},{6,0},{8,14},{10,12},{12,10},{14,8},{16,22},{18,... | collective-permute-start | bytes 786440 | tf_op jit(solution)/shard_map/ppermute | solution.py:132
  15.5 0.5 collective-permute-start.3
  16.0 0.0 copy-done
  16.0 0.7 %fusion.2 = bf16[2,16,128,128]{3,1,2,0:T(8,128)(2,1)S(1)} fusion(bf16[2,16,128,128]{3,2,1,0:T(8,128)(2,1)S(1)} %bitcast.67, s32[2,16]{1,0:T(2,128)S(1)} %bitcast.79, pred[2,16]{1,0:T(4,128)(4,1)S(1)} %iota_compare_fusion.1), kind=kOutput, calls=%fused_computation.8 | convolution fusion | flops 16778240 | bytes 2097312 | tf_op jit(solution)/shard_map/tsq,tsab->tqab/dot_general | solution.py:184
  16.8 9.2 %collective-permute-done.4 = bf16[2,2,1,1,128,256]{5,4,3,2,1,0:T(8,128)(2,1)S(1)} collective-permute-done((bf16[2,2,1,1,128,256]{5,4,3,2,1,0:T(8,128)(2,1)S(1)}, bf16[2,2,1,1,128,256]{5,4,3,2,1,0:T(8,128)(2,1)S(1)}, u32[]{:S(2)}, u32[]{:S(2)}) %collective-permute-start.4) | collective-permute-done | bytes 262176 | tf_op jit(solution)/shard_map/ppermute | solution.py:131
  26.0 0.0 collective-permute-done.5
  26.0 1.3 %collective-permute-done.3 = bf16[2,2,1,1,128,256]{5,4,3,2,1,0:T(8,128)(2,1)S(1)} collective-permute-done((bf16[2,2,1,1,128,256]{5,4,3,2,1,0:T(8,128)(2,1)S(1)}, bf16[2,2,1,1,128,256]{5,4,3,2,1,0:T(8,128)(2,1)S(1)}, u32[]{:S(2)}, u32[]{:S(2)}) %collective-permute-start.3) | collective-permute-done | bytes 262176 | tf_op jit(solution)/shard_map/ppermute | solution.py:130
  27.3 0.0 copy-done.1
  27.3 0.1 maximum_maximum_fusion
  27.4 0.0 copy-start.2
  27.4 0.0 copy-start.3
  27.4 0.4 convolution_bitcast_fusion.1
  27.9 0.1 collective-permute-start.6
  28.0 1.5 %collective-permute-done.6 = f32[2,128,256]{2,1,0:T(8,128)S(1)} collective-permute-done((f32[2,128,256]{2,1,0:T(8,128)S(1)}, f32[2,128,256]{2,1,0:T(8,128)S(1)}, u32[]{:S(2)}, u32[]{:S(2)}) %collective-permute-start.6) | collective-permute-done | bytes 262176 | tf_op jit(solution)/shard_map/ppermute | solution.py:98
  29.5 0.0 copy-done.2
  29.5 0.0 copy-done.3
  29.5 1.0 %multiply_convert_fusion = (bf16[256,256]{1,0:T(8,128)(2,1)S(1)}, f32[256,256]{1,0:T(8,128)}, f32[256,256]{1,0:T(8,128)}) fusion(bf16[256,256]{1,0:T(8,128)(2,1)S(1)} %copy-done.3, bf16[256,256]{1,0:T(8,128)(2,1)S(1)} %bitcast.71, bf16[256,256]{1,0:T(8,128)(2,1)S(1)} %copy-done.2), kind=kOutput, calls=%fused_computation.19 | convolution fusion | flops 34209792 | bytes 1048576 | tf_op jit(solution)/shard_map/dot_general | solution.py:210
  30.5 0.2 fusion.17
  30.7 0.2 convolution_convert_fusion
  31.0 0.5 convolution_bitcast_fusion
  31.5 0.1 fusion.4
  31.6 0.1 copy_bitcast_fusion
  31.7 0.2 collective-permute-start.7
  31.9 1.6 %collective-permute-start.12 = (bf16[2,2,128,256]{3,2,1,0:T(8,128)(2,1)S(1)}, bf16[2,2,128,256]{3,2,1,0:T(8,128)(2,1)S(1)}, u32[]{:S(2)}, u32[]{:S(2)}) collective-permute-start(bf16[2,2,128,256]{3,2,1,0:T(8,128)(2,1)S(1)} %fusion.6), channel_id=1, source_target_pairs={{0,2},{2,0},{4,6},{6,4},{8,10},{10,8},{12,14},{14,12},{16,18},{18,... | collective-permute-start | bytes 786440 | tf_op jit(solution)/shard_map/ppermute | solution.py:155
  33.6 1.6 %collective-permute-start.13 = (bf16[2,2,128,256]{3,2,1,0:T(8,128)(2,1)S(1)}, bf16[2,2,128,256]{3,2,1,0:T(8,128)(2,1)S(1)}, u32[]{:S(2)}, u32[]{:S(2)}) collective-permute-start(bf16[2,2,128,256]{3,2,1,0:T(8,128)(2,1)S(1)} %get-tuple-element.5), channel_id=1, source_target_pairs={{0,4},{2,6},{4,0},{6,2},{8,12},{10,14},{12,8},{14,10},{16,20},{18,... | collective-permute-start | bytes 786440 | tf_op jit(solution)/shard_map/ppermute | solution.py:156
  35.1 0.4 collective-permute-start.14
  35.5 1.8 %collective-permute-done.7 = f32[128,256]{1,0:T(8,128)S(1)} collective-permute-done((f32[128,256]{1,0:T(8,128)S(1)}, f32[128,256]{1,0:T(8,128)S(1)}, u32[]{:S(2)}, u32[]{:S(2)}) %collective-permute-start.7) | collective-permute-done | bytes 131104 | tf_op jit(solution)/shard_map/ppermute | solution.py:98
  37.3 0.5 collective-permute-start.8
  37.8 1.6 %fusion.9 = bf16[128,256]{1,0:T(8,128)(2,1)} fusion(f32[256,256]{1,0:T(8,128)} %get-tuple-element.11, s32[]{:T(128)S(6)} %select_n.16, f32[256,256]{1,0:T(8,128)} %get-tuple-element.12), kind=kLoop, calls=%fused_computation.26 | loop fusion | flops 65536 | bytes 327684 | tf_op jit(solution)/shard_map/convert_element_type | solution.py:212
  39.4 6.5 %collective-permute-done.8 = f32[128,256]{1,0:T(8,128)} collective-permute-done((f32[128,256]{1,0:T(8,128)S(1)}, f32[128,256]{1,0:T(8,128)}, u32[]{:S(2)}, u32[]{:S(2)}) %collective-permute-start.8) | collective-permute-done | bytes 131104 | tf_op jit(solution)/shard_map/ppermute | solution.py:98
  45.9 0.9 %add.48 = f32[128,256]{1,0:T(8,128)S(1)} add(f32[128,256]{1,0:T(8,128)S(1)} %fusion.26, f32[128,256]{1,0:T(8,128)} %collective-permute-done.8) | non-fusion elementwise | flops 32768 | bytes 393216 | tf_op jit(solution)/shard_map/add | solution.py:98
  46.8 1.8 %collective-permute-start.9 = (f32[128,256]{1,0:T(8,128)S(1)}, f32[128,256]{1,0:T(8,128)S(1)}, u32[]{:S(2)}, u32[]{:S(2)}) collective-permute-start(f32[128,256]{1,0:T(8,128)S(1)} %add.48), channel_id=1, source_target_pairs={{0,2},{2,0},{4,6},{6,4},{8,10},{10,8},{12,14},{14,12},{16,18},{18,... | collective-permute-start | bytes 393224 | tf_op jit(solution)/shard_map/ppermute | solution.py:98
  48.5 0.0 collective-permute-done.12
  48.5 0.0 collective-permute-done.13
  48.5 0.0 collective-permute-done.14
  48.6 1.1 %fusion.15 = (bf16[2,2,128,256]{3,2,1,0:T(8,128)(2,1)S(1)}, f32[2,2,128,256]{3,2,1,0:T(8,128)S(1)}) fusion(bf16[2,2,128,256]{3,2,1,0:T(8,128)(2,1)} %collective-permute-done.14, bf16[2,2,128,256]{3,2,1,0:T(8,128)(2,1)S(1)} %collective-permute-done.13, bf16[2,2,128,256]{3,2,1,0:T(8,128)(2,1)S(1)} %collective-permute-done.12, ...), kind=kLoop, calls=%fused_computation.39 | loop fusion | flops 917504 | bytes 2097152 | tf_op jit(solution)/shard_map/convert.2
  49.6 2.6 %collective-permute-done.9 = f32[128,256]{1,0:T(8,128)S(1)} collective-permute-done((f32[128,256]{1,0:T(8,128)S(1)}, f32[128,256]{1,0:T(8,128)S(1)}, u32[]{:S(2)}, u32[]{:S(2)}) %collective-permute-start.9) | collective-permute-done | bytes 131104 | tf_op jit(solution)/shard_map/ppermute | solution.py:98
  52.3 1.7 %collective-permute-start.10 = (f32[128,256]{1,0:T(8,128)S(1)}, f32[128,256]{1,0:T(8,128)S(1)}, u32[]{:S(2)}, u32[]{:S(2)}) collective-permute-start(f32[128,256]{1,0:T(8,128)S(1)} %add.49), channel_id=1, source_target_pairs={{0,4},{2,6},{4,0},{6,2},{8,12},{10,14},{12,8},{14,10},{16,20},{18,... | collective-permute-start | bytes 393224 | tf_op jit(solution)/shard_map/ppermute | solution.py:98
  54.0 0.1 collective-permute-start.15
  54.1 1.4 %collective-permute-start.17 = (bf16[128,256]{1,0:T(8,128)(2,1)S(1)}, bf16[128,256]{1,0:T(8,128)(2,1)S(1)}, u32[]{:S(2)}, u32[]{:S(2)}) collective-permute-start(bf16[128,256]{1,0:T(8,128)(2,1)S(1)} %get-tuple-element.8), channel_id=1, source_target_pairs={{0,24},{2,26},{4,28},{6,30},{8,16},{10,18},{12,20},{14,22},{16,8},... | collective-permute-start | bytes 196616 | tf_op jit(solution)/shard_map/ppermute | solution.py:157
  55.5 2.1 %collective-permute-start.16 = (bf16[128,256]{1,0:T(8,128)(2,1)S(1)}, bf16[128,256]{1,0:T(8,128)(2,1)S(1)}, u32[]{:S(2)}, u32[]{:S(2)}) collective-permute-start(bf16[128,256]{1,0:T(8,128)(2,1)S(1)} %get-tuple-element.9), channel_id=1, source_target_pairs={{0,16},{2,18},{4,20},{6,22},{8,24},{10,26},{12,28},{14,30},{16,0},... | collective-permute-start | bytes 196616 | tf_op jit(solution)/shard_map/ppermute | solution.py:156
  57.6 0.0 collective-permute-done.10
  57.6 0.1 collective-permute-start.11
  57.7 1.4 %collective-permute-done.15 = bf16[128,256]{1,0:T(8,128)(2,1)S(1)} collective-permute-done((bf16[128,256]{1,0:T(8,128)(2,1)S(1)}, bf16[128,256]{1,0:T(8,128)(2,1)S(1)}, u32[]{:S(2)}, u32[]{:S(2)}) %collective-permute-start.15) | collective-permute-done | bytes 65568 | tf_op jit(solution)/shard_map/ppermute | solution.py:155
  59.1 1.3 %collective-permute-done.17 = bf16[128,256]{1,0:T(8,128)(2,1)S(1)} collective-permute-done((bf16[128,256]{1,0:T(8,128)(2,1)S(1)}, bf16[128,256]{1,0:T(8,128)(2,1)S(1)}, u32[]{:S(2)}, u32[]{:S(2)}) %collective-permute-start.17) | collective-permute-done | bytes 65568 | tf_op jit(solution)/shard_map/ppermute | solution.py:157
  60.3 2.0 %collective-permute-done.16 = bf16[128,256]{1,0:T(8,128)(2,1)S(1)} collective-permute-done((bf16[128,256]{1,0:T(8,128)(2,1)S(1)}, bf16[128,256]{1,0:T(8,128)(2,1)S(1)}, u32[]{:S(2)}, u32[]{:S(2)}) %collective-permute-start.16) | collective-permute-done | bytes 65568 | tf_op jit(solution)/shard_map/ppermute | solution.py:156
  62.4 0.7 %fusion.8 = bf16[128,256]{1,0:T(8,128)(2,1)} fusion(f32[2,2,128,256]{3,2,1,0:T(8,128)S(1)} %get-tuple-element.4, bf16[128,256]{1,0:T(8,128)(2,1)S(1)} %collective-permute-done.17, bf16[128,256]{1,0:T(8,128)(2,1)S(1)} %collective-permute-done.16, bf16[128,256]{1,0:T(8,128)(2,1)S(1)} %collective-permute-done.15), kind=kLoop, calls=%fused_computation.24 | loop fusion | flops 229376 | bytes 393216 | tf_op jit(solution)/shard_map/convert_element_type | solution.py:254
  63.0 0.0 collective-permute-done.11
  63.0 0.7 %maximum_select_fusion = f32[2,128,256]{2,1,0:T(8,128)} fusion(f32[1,128,256]{2,1,0:T(8,128)S(1)} %collective-permute-done.11, f32[1,128,256]{2,1,0:T(8,128)S(1)} %add_bitcast_fusion, pred[]{:T(512)S(6)} %eq.19), kind=kLoop, calls=%fused_computation.18 | loop fusion | flops 196608 | bytes 524289 | tf_op jit(solution)/shard_map/jit(_where)/select_n | solution.py:108
  (8 shorter events, 0.2 us)
Async XLA Ops:
  0.6 15.4 %copy-start = (bf16[2,1,16,128,128]{4,3,2,1,0:T(8,128)(2,1)S(1)}, bf16[2,1,16,128,128]{4,3,2,1,0:T(8,128)(2,1)}, u32[]{:S(2)}) copy-start(bf16[2,1,16,128,128]{4,3,2,1,0:T(8,128)(2,1)} %param.9) | copy-start | bytes 3145732
  0.6 26.6 %copy-start.1 = (bf16[128,256]{1,0:T(8,128)(2,1)S(1)}, bf16[128,256]{1,0:T(8,128)(2,1)}, u32[]{:S(2)}) copy-start(bf16[128,256]{1,0:T(8,128)(2,1)} %param.6) | copy-start | bytes 196612
  0.7 7.9 %collective-permute-start.2 = (bf16[1,1,1,1,128,256]{5,4,3,2,1,0:T(8,128)(2,1)}, bf16[1,1,1,1,128,256]{5,4,3,2,1,0:T(8,128)(2,1)S(1)}, u32[]{:S(2)}, u32[]{:S(2)}) collective-permute-start(bf16[1,1,1,1,128,256]{5,4,3,2,1,0:T(8,128)(2,1)} %bitcast.74), channel_id=1, source_target_pairs={{0,24},{2,26},{4,28},{6,30},{8,16},{10,18},{12,20},{14,22},{16,8},... | collective-permute-start | bytes 196616 | tf_op jit(solution)/shard_map/ppermute | solution.py:132
  5.8 5.8 %collective-permute-start.1 = (bf16[1,1,1,1,128,256]{5,4,3,2,1,0:T(8,128)(2,1)}, bf16[1,1,1,1,128,256]{5,4,3,2,1,0:T(8,128)(2,1)S(1)}, u32[]{:S(2)}, u32[]{:S(2)}) collective-permute-start(bf16[1,1,1,1,128,256]{5,4,3,2,1,0:T(8,128)(2,1)} %bitcast.75), channel_id=1, source_target_pairs={{0,16},{2,18},{4,20},{6,22},{8,24},{10,26},{12,28},{14,30},{16,0},... | collective-permute-start | bytes 196616 | tf_op jit(solution)/shard_map/ppermute | solution.py:131
  5.8 5.8 %collective-permute-start = (bf16[1,1,1,1,128,256]{5,4,3,2,1,0:T(8,128)(2,1)}, bf16[1,1,1,1,128,256]{5,4,3,2,1,0:T(8,128)(2,1)S(1)}, u32[]{:S(2)}, u32[]{:S(2)}) collective-permute-start(bf16[1,1,1,1,128,256]{5,4,3,2,1,0:T(8,128)(2,1)} %bitcast.76), channel_id=1, source_target_pairs={{0,8},{2,10},{4,12},{6,14},{8,0},{10,2},{12,4},{14,6},{16,24},{18,... | collective-permute-start | bytes 196616 | tf_op jit(solution)/shard_map/ppermute | solution.py:130
  12.5 13.6 %collective-permute-start.4 = (bf16[2,2,1,1,128,256]{5,4,3,2,1,0:T(8,128)(2,1)S(1)}, bf16[2,2,1,1,128,256]{5,4,3,2,1,0:T(8,128)(2,1)S(1)}, u32[]{:S(2)}, u32[]{:S(2)}) collective-permute-start(bf16[2,2,1,1,128,256]{5,4,3,2,1,0:T(8,128)(2,1)S(1)} %maximum_maximum_fusion.1), channel_id=1, source_target_pairs={{0,4},{2,6},{4,0},{6,2},{8,12},{10,14},{12,8},{14,10},{16,20},{18,... | collective-permute-start | bytes 786440 | tf_op jit(solution)/shard_map/ppermute | solution.py:131
  14.0 12.0 %collective-permute-start.5 = (bf16[2,2,1,1,128,256]{5,4,3,2,1,0:T(8,128)(2,1)S(1)}, bf16[2,2,1,1,128,256]{5,4,3,2,1,0:T(8,128)(2,1)S(1)}, u32[]{:S(2)}, u32[]{:S(2)}) collective-permute-start(bf16[2,2,1,1,128,256]{5,4,3,2,1,0:T(8,128)(2,1)S(1)} %maximum_maximum_fusion.1), channel_id=1, source_target_pairs={{0,6},{2,4},{4,2},{6,0},{8,14},{10,12},{12,10},{14,8},{16,22},{18,... | collective-permute-start | bytes 786440 | tf_op jit(solution)/shard_map/ppermute | solution.py:132
  15.5 11.8 %collective-permute-start.3 = (bf16[2,2,1,1,128,256]{5,4,3,2,1,0:T(8,128)(2,1)S(1)}, bf16[2,2,1,1,128,256]{5,4,3,2,1,0:T(8,128)(2,1)S(1)}, u32[]{:S(2)}, u32[]{:S(2)}) collective-permute-start(bf16[2,2,1,1,128,256]{5,4,3,2,1,0:T(8,128)(2,1)S(1)} %maximum_maximum_fusion.1), channel_id=1, source_target_pairs={{0,2},{2,0},{4,6},{6,4},{8,10},{10,8},{12,14},{14,12},{16,18},{18,... | collective-permute-start | bytes 786440 | tf_op jit(solution)/shard_map/ppermute | solution.py:130
  27.4 2.1 %copy-start.2 = (bf16[256,256]{1,0:T(8,128)(2,1)S(1)}, bf16[256,256]{1,0:T(8,128)(2,1)}, u32[]{:S(2)}) copy-start(bf16[256,256]{1,0:T(8,128)(2,1)} %param.8) | copy-start | bytes 393220
  27.4 2.1 %copy-start.3 = (bf16[256,256]{1,0:T(8,128)(2,1)S(1)}, bf16[256,256]{1,0:T(8,128)(2,1)}, u32[]{:S(2)}) copy-start(bf16[256,256]{1,0:T(8,128)(2,1)} %param.7) | copy-start | bytes 393220
  27.9 1.6 %collective-permute-start.6 = (f32[2,128,256]{2,1,0:T(8,128)S(1)}, f32[2,128,256]{2,1,0:T(8,128)S(1)}, u32[]{:S(2)}, u32[]{:S(2)}) collective-permute-start(f32[2,128,256]{2,1,0:T(8,128)S(1)} %convolution_bitcast_fusion.1), channel_id=1, source_target_pairs={{0,1},{1,0},{2,3},{3,2},{4,5},{5,4},{6,7},{7,6},{8,9},{9,8},{10,11... | collective-permute-start | bytes 786440 | tf_op jit(solution)/shard_map/ppermute | solution.py:98
  31.7 5.6 %collective-permute-start.7 = (f32[128,256]{1,0:T(8,128)S(1)}, f32[128,256]{1,0:T(8,128)S(1)}, u32[]{:S(2)}, u32[]{:S(2)}) collective-permute-start(f32[128,256]{1,0:T(8,128)S(1)} %constant_dynamic-slice_fusion), channel_id=1, source_target_pairs={{0,8},{2,10},{4,12},{6,14},{8,0},{10,2},{12,4},{14,6},{16,24},{18,... | collective-permute-start | bytes 393224 | tf_op jit(solution)/shard_map/ppermute | solution.py:98
  31.9 16.7 %collective-permute-start.12 = (bf16[2,2,128,256]{3,2,1,0:T(8,128)(2,1)S(1)}, bf16[2,2,128,256]{3,2,1,0:T(8,128)(2,1)S(1)}, u32[]{:S(2)}, u32[]{:S(2)}) collective-permute-start(bf16[2,2,128,256]{3,2,1,0:T(8,128)(2,1)S(1)} %fusion.6), channel_id=1, source_target_pairs={{0,2},{2,0},{4,6},{6,4},{8,10},{10,8},{12,14},{14,12},{16,18},{18,... | collective-permute-start | bytes 786440 | tf_op jit(solution)/shard_map/ppermute | solution.py:155
  33.6 15.0 %collective-permute-start.13 = (bf16[2,2,128,256]{3,2,1,0:T(8,128)(2,1)S(1)}, bf16[2,2,128,256]{3,2,1,0:T(8,128)(2,1)S(1)}, u32[]{:S(2)}, u32[]{:S(2)}) collective-permute-start(bf16[2,2,128,256]{3,2,1,0:T(8,128)(2,1)S(1)} %get-tuple-element.5), channel_id=1, source_target_pairs={{0,4},{2,6},{4,0},{6,2},{8,12},{10,14},{12,8},{14,10},{16,20},{18,... | collective-permute-start | bytes 786440 | tf_op jit(solution)/shard_map/ppermute | solution.py:156
  35.1 13.4 %collective-permute-start.14 = (bf16[2,2,128,256]{3,2,1,0:T(8,128)(2,1)S(1)}, bf16[2,2,128,256]{3,2,1,0:T(8,128)(2,1)}, u32[]{:S(2)}, u32[]{:S(2)}) collective-permute-start(bf16[2,2,128,256]{3,2,1,0:T(8,128)(2,1)S(1)} %get-tuple-element.6), channel_id=1, source_target_pairs={{0,6},{2,4},{4,2},{6,0},{8,14},{10,12},{12,10},{14,8},{16,22},{18,... | collective-permute-start | bytes 786440 | tf_op jit(solution)/shard_map/ppermute | solution.py:157
  37.3 8.5 %collective-permute-start.8 = (f32[128,256]{1,0:T(8,128)S(1)}, f32[128,256]{1,0:T(8,128)}, u32[]{:S(2)}, u32[]{:S(2)}) collective-permute-start(f32[128,256]{1,0:T(8,128)S(1)} %fusion.26), channel_id=1, source_target_pairs={{0,16},{2,18},{4,20},{6,22},{8,24},{10,26},{12,28},{14,30},{16,0},... | collective-permute-start | bytes 393224 | tf_op jit(solution)/shard_map/ppermute | solution.py:98
  46.8 5.5 %collective-permute-start.9 = (f32[128,256]{1,0:T(8,128)S(1)}, f32[128,256]{1,0:T(8,128)S(1)}, u32[]{:S(2)}, u32[]{:S(2)}) collective-permute-start(f32[128,256]{1,0:T(8,128)S(1)} %add.48), channel_id=1, source_target_pairs={{0,2},{2,0},{4,6},{6,4},{8,10},{10,8},{12,14},{14,12},{16,18},{18,... | collective-permute-start | bytes 393224 | tf_op jit(solution)/shard_map/ppermute | solution.py:98
  52.3 5.3 %collective-permute-start.10 = (f32[128,256]{1,0:T(8,128)S(1)}, f32[128,256]{1,0:T(8,128)S(1)}, u32[]{:S(2)}, u32[]{:S(2)}) collective-permute-start(f32[128,256]{1,0:T(8,128)S(1)} %add.49), channel_id=1, source_target_pairs={{0,4},{2,6},{4,0},{6,2},{8,12},{10,14},{12,8},{14,10},{16,20},{18,... | collective-permute-start | bytes 393224 | tf_op jit(solution)/shard_map/ppermute | solution.py:98
  54.0 5.0 %collective-permute-start.15 = (bf16[128,256]{1,0:T(8,128)(2,1)S(1)}, bf16[128,256]{1,0:T(8,128)(2,1)S(1)}, u32[]{:S(2)}, u32[]{:S(2)}) collective-permute-start(bf16[128,256]{1,0:T(8,128)(2,1)S(1)} %get-tuple-element.7), channel_id=1, source_target_pairs={{0,8},{2,10},{4,12},{6,14},{8,0},{10,2},{12,4},{14,6},{16,24},{18,... | collective-permute-start | bytes 196616 | tf_op jit(solution)/shard_map/ppermute | solution.py:155
  54.1 6.2 %collective-permute-start.17 = (bf16[128,256]{1,0:T(8,128)(2,1)S(1)}, bf16[128,256]{1,0:T(8,128)(2,1)S(1)}, u32[]{:S(2)}, u32[]{:S(2)}) collective-permute-start(bf16[128,256]{1,0:T(8,128)(2,1)S(1)} %get-tuple-element.8), channel_id=1, source_target_pairs={{0,24},{2,26},{4,28},{6,30},{8,16},{10,18},{12,20},{14,22},{16,8},... | collective-permute-start | bytes 196616 | tf_op jit(solution)/shard_map/ppermute | solution.py:157
  55.5 6.9 %collective-permute-start.16 = (bf16[128,256]{1,0:T(8,128)(2,1)S(1)}, bf16[128,256]{1,0:T(8,128)(2,1)S(1)}, u32[]{:S(2)}, u32[]{:S(2)}) collective-permute-start(bf16[128,256]{1,0:T(8,128)(2,1)S(1)} %get-tuple-element.9), channel_id=1, source_target_pairs={{0,16},{2,18},{4,20},{6,22},{8,24},{10,26},{12,28},{14,30},{16,0},... | collective-permute-start | bytes 196616 | tf_op jit(solution)/shard_map/ppermute | solution.py:156
  57.6 5.4 %collective-permute-start.11 = (f32[1,128,256]{2,1,0:T(8,128)S(1)}, f32[1,128,256]{2,1,0:T(8,128)S(1)}, u32[]{:S(2)}, u32[]{:S(2)}) collective-permute-start(f32[1,128,256]{2,1,0:T(8,128)S(1)} %add_bitcast_fusion), channel_id=1, source_target_pairs={{0,1},{1,0},{2,3},{3,2},{4,5},{5,4},{6,7},{7,6},{8,9},{9,8},{10,11... | collective-permute-start | bytes 393224 | tf_op jit(solution)/shard_map/ppermute | solution.py:106

commit v5 on v4

--- a/solution.py
+++ b/solution.py
@@ -9,6 +9,8 @@
 PIPE_FWD = False
 RADIX4_GATHER = True
 RADIX4_SCATTER = True
+PAIRED_BACKWARD = True
+TIE_ROUNDS = False
 
 
 def bit_count(n):
@@ -161,6 +163,46 @@
     return cur
 
 
+def scatter_round(cur, bits, n, send_dtype):
+    lead = cur.ndim - 2
+    if len(bits) == 1:
+        keep = lax.index_in_dim(cur, 0, lead - 1, keepdims=False)
+        send = lax.index_in_dim(cur, 1, lead - 1, keepdims=False)
+        return keep + lax.ppermute(send.astype(send_dtype), "rows", pairs_of(n, bits[0])).astype(jnp.float32)
+    low, high = bits
+
+    def part(h, l):
+        return lax.index_in_dim(lax.index_in_dim(cur, h, lead - 2, keepdims=False), l, lead - 2, keepdims=False)
+
+    got_low = lax.ppermute(part(0, 1).astype(send_dtype), "rows", pairs_of(n, low))
+    got_high = lax.ppermute(part(1, 0).astype(send_dtype), "rows", pairs_of(n, high))
+    got_both = lax.ppermute(
+        part(1, 1).astype(send_dtype), "rows", [(j, j ^ (1 << low) ^ (1 << high)) for j in range(n)]
+    )
+    return part(0, 0) + (got_low.astype(jnp.float32) + got_high.astype(jnp.float32) + got_both.astype(jnp.float32))
+
+
+def sum_round(w, bits, n):
+    if len(bits) == 1:
+        return w + lax.ppermute(w, "rows", pairs_of(n, bits[0]))
+    low, high = bits
+    got_low = lax.ppermute(w, "rows", pairs_of(n, low))
+    got_high = lax.ppermute(w, "rows", pairs_of(n, high))
+    got_both = lax.ppermute(w, "rows", [(j, j ^ (1 << low) ^ (1 << high)) for j in range(n)])
+    return (w + got_low) + (got_high + got_both)
+
+
+def paired_backward(rel, w, n, send_dtype):
+    rounds = bit_rounds(bit_count(n))
+    cur = rel
+    for k, bits in enumerate(rounds[::-1]):
+        cur = scatter_round(cur, bits, n, send_dtype)
+        w = sum_round(w, rounds[k], n)
+        if TIE_ROUNDS:
+            cur, w = lax.optimization_barrier((cur, w))
+    return cur, w
+
+
 def local(features, cotangent, weight, tile_vals, tile_cols, tile_count):
     n_rows = lax.axis_size("rows")
     n_rep = lax.axis_size("rep")
@@ -223,7 +265,7 @@
 
     slice_rows = feat_width // n_rep
     w_slice = lax.dynamic_slice_in_dim(local_weight, me_rep * slice_rows, slice_rows, 0)
-    if not W_PACKED:
+    if not W_PACKED and not PAIRED_BACKWARD:
         w_order = list(range(2, nb)) + [0, 1] if nb >= 2 else list(range(nb))
         w_slice = doubling_sum(w_slice, "rows", n_rows, w_order)
 
@@ -243,6 +285,10 @@
             preferred_element_type=jnp.float32,
         )
         products = products.reshape((2,) * nb + (block_rows, width))
+        if order is None and PAIRED_BACKWARD:
+            piece, w_slice = paired_backward(products, w_slice, n_rows, jnp.bfloat16)
+            pieces.append(piece)
+            continue
         if order is None:
             pieces.append(radix_scatter(products, n_rows, jnp.bfloat16))
             continue

time: 64 us -> 62.1 us (0.970)
  starting transfers between devices: 20.7 us -> 25 us
  other arithmetic: 7.44 us -> 4.62 us
  waiting for transfers between devices: 31.3 us -> 28.8 us
  matrix products: 3.14 us -> 2.43 us
    ppermute x5 -> x1, waiting for transfers between devices: 12.4 us -> 1.52 us  [doubling_sum(): x = x + lax.ppermute(x, axis, pairs_of(n, b))]
    ppermute x6 -> x12, starting transfers between devices: 7.16 us -> 15.5 us  [the longest x2 4.19 us: scatter_round(): lax.ppermute(part(1, 1).astype(send_dtype), 'rows', [(j, j ^ 1 << low ^ 1...]
    ppermute x6 -> x12, waiting for transfers between devices: 4.68 us -> 13 us  [the longest x2 5.19 us: scatter_round(): lax.ppermute(part(1, 1).astype(send_dtype), 'rows', [(j, j ^ 1 << low ^ 1...]
    ppermute x5 -> x1, starting transfers between devices: 4.19 us -> 0.07 us  [doubling_sum(): x = x + lax.ppermute(x, axis, pairs_of(n, b))]
    convert_element_type x1, other arithmetic: 1.61 us -> 0.64 us  [local(): output = (preact * sigmoid_part).astype(jnp.bfloat16)]
    another operation x1, other arithmetic: 1.07 us -> 0.11 us
    add x3 -> x1, other arithmetic: 0.95 us -> 0.03 us  [sum_round(): return w + got_low + (got_high + got_both)]
    dot_general x1, matrix products: 0.98 us -> 0.27 us  [local(): preact = jnp.dot(aggregated, weight, preferred_element_type=jnp.float32)]
  transfers between devices with their start and end apart: 18 -> 20, of which waited for: 11 -> 12; matrix products, arithmetic and copies ran while one was open for 10% -> 7% of each run, Pallas kernels for 0% -> 0%
where the time goes in v5:
time: 62.1 us; the launch traced here: 61.9 us
  waiting for transfers between devices  28.8 us (46%)
  starting transfers between devices  25 us (40%)
  other arithmetic  4.62 us (7%)
  matrix products  2.43 us (4%)
  between operations  0.85 us (1%)
    ppermute x2, waiting for transfers between devices, radix_gather(): got_high = lax.ppermute(held, 'rows', pairs_of(n, high))  12.2 us
    ppermute x2, starting transfers between devices, radix_gather(): lax.ppermute(held, 'rows', [(j, j ^ 1 << low ^ 1 << high) for j in range(...  6.55 us
    ppermute x2, waiting for transfers between devices, scatter_round(): lax.ppermute(part(1, 1).astype(send_dtype), 'rows', [(j, j ^ 1 << low ^ 1...  5.19 us
    ppermute x2, waiting for transfers between devices, sum_round(): got_high = lax.ppermute(w, 'rows', pairs_of(n, high))  5.04 us
    ppermute x2, starting transfers between devices, scatter_round(): lax.ppermute(part(1, 1).astype(send_dtype), 'rows', [(j, j ^ 1 << low ^ 1...  4.19 us
    ppermute x2, starting transfers between devices, sum_round(): lax.ppermute(w, 'rows', [(j, j ^ 1 << low ^ 1 << high) for j in range(n)])  2.83 us
    ppermute x2, starting transfers between devices, sum_round(): got_low = lax.ppermute(w, 'rows', pairs_of(n, low))  2.53 us
    ppermute x2, starting transfers between devices, scatter_round(): lax.ppermute(part(1, 0).astype(send_dtype), 'rows', pairs_of(n, high))  2.46 us
  transfers between devices with their start and end apart: 20, of which 12 were waited for; matrix products, arithmetic and copies ran while one was open for 7% of the time, Pallas kernels for 0%

profile of v5, /device:TPU:0, one launch (start us, length us, event | category | flops | bytes accessed | tf_op | source)
XLA Modules:
  0.0 61.9 jit_solution(12278830976291450029)
XLA Ops:
  0.6 0.0 copy-start
  0.6 0.0 copy-start.1
  0.7 5.1 %collective-permute-start.2 = (bf16[1,1,1,1,128,256]{5,4,3,2,1,0:T(8,128)(2,1)}, bf16[1,1,1,1,128,256]{5,4,3,2,1,0:T(8,128)(2,1)S(1)}, u32[]{:S(2)}, u32[]{:S(2)}) collective-permute-start(bf16[1,1,1,1,128,256]{5,4,3,2,1,0:T(8,128)(2,1)} %bitcast.74), channel_id=1, source_target_pairs={{0,24},{2,26},{4,28},{6,30},{8,16},{10,18},{12,20},{14,22},{16,8},... | collective-permute-start | bytes 196616 | tf_op jit(solution)/shard_map/ppermute | solution.py:134
  5.8 0.0 collective-permute-start.1
  5.8 0.6 %collective-permute-start = (bf16[1,1,1,1,128,256]{5,4,3,2,1,0:T(8,128)(2,1)}, bf16[1,1,1,1,128,256]{5,4,3,2,1,0:T(8,128)(2,1)S(1)}, u32[]{:S(2)}, u32[]{:S(2)}) collective-permute-start(bf16[1,1,1,1,128,256]{5,4,3,2,1,0:T(8,128)(2,1)} %bitcast.76), channel_id=1, source_target_pairs={{0,8},{2,10},{4,12},{6,14},{8,0},{10,2},{12,4},{14,6},{16,24},{18,... | collective-permute-start | bytes 196616 | tf_op jit(solution)/shard_map/ppermute | solution.py:132
  6.4 0.7 %broadcast_xor_fusion = s32[2,1,16]{2,1,0:T(1,128)S(1)} fusion(s32[2,1,16]{2,1,0:T(1,128)} %param.10, s32[]{:T(128)S(6)} %axis_index.27), kind=kLoop, calls=%fused_computation.39 | loop fusion | flops 32 | bytes 260 | tf_op jit(solution)/shard_map/xor | solution.py:224
  7.1 0.7 %iota_compare_fusion.1 = pred[2,16]{1,0:T(4,128)(4,1)S(1)} fusion(s32[2]{0:T(128)} %bitcast.80), kind=kLoop, calls=%fused_computation.37 | loop fusion | flops 32 | bytes 40 | tf_op jit(solution)/shard_map/lt | solution.py:223
  7.8 0.8 %collective-permute-done.2 = bf16[1,1,1,1,128,256]{5,4,3,2,1,0:T(8,128)(2,1)S(1)} collective-permute-done((bf16[1,1,1,1,128,256]{5,4,3,2,1,0:T(8,128)(2,1)}, bf16[1,1,1,1,128,256]{5,4,3,2,1,0:T(8,128)(2,1)S(1)}, u32[]{:S(2)}, u32[]{:S(2)}) %collective-permute-start.2) | collective-permute-done | bytes 65568 | tf_op jit(solution)/shard_map/ppermute | solution.py:134
  8.6 3.0 %collective-permute-done.1 = bf16[1,1,1,1,128,256]{5,4,3,2,1,0:T(8,128)(2,1)S(1)} collective-permute-done((bf16[1,1,1,1,128,256]{5,4,3,2,1,0:T(8,128)(2,1)}, bf16[1,1,1,1,128,256]{5,4,3,2,1,0:T(8,128)(2,1)S(1)}, u32[]{:S(2)}, u32[]{:S(2)}) %collective-permute-start.1) | collective-permute-done | bytes 65568 | tf_op jit(solution)/shard_map/ppermute | solution.py:133
  11.6 0.0 collective-permute-done
  11.6 0.9 %maximum_maximum_fusion.1 = bf16[2,2,1,1,128,256]{5,4,3,2,1,0:T(8,128)(2,1)S(1)} fusion(bf16[1,1,1,1,128,256]{5,4,3,2,1,0:T(8,128)(2,1)S(1)} %collective-permute-done.2, bf16[1,1,1,1,128,256]{5,4,3,2,1,0:T(8,128)(2,1)S(1)} %collective-permute-done.1, bf16[1,1,1,1,128,256]{5,4,3,2,1,0:T(8,128)(2,1)S(1)} %collective-permute-done, ...), kind=kLoop, calls=%fused_computation.17 | loop fusion | flops 393216 | bytes 524288 | tf_op jit(solution)/shard_map/concatenate | solution.py:137
  12.5 1.6 %collective-permute-start.4 = (bf16[2,2,1,1,128,256]{5,4,3,2,1,0:T(8,128)(2,1)S(1)}, bf16[2,2,1,1,128,256]{5,4,3,2,1,0:T(8,128)(2,1)S(1)}, u32[]{:S(2)}, u32[]{:S(2)}) collective-permute-start(bf16[2,2,1,1,128,256]{5,4,3,2,1,0:T(8,128)(2,1)S(1)} %maximum_maximum_fusion.1), channel_id=1, source_target_pairs={{0,4},{2,6},{4,0},{6,2},{8,12},{10,14},{12,8},{14,10},{16,20},{18,... | collective-permute-start | bytes 786440 | tf_op jit(solution)/shard_map/ppermute | solution.py:133
  14.0 1.4 %collective-permute-start.5 = (bf16[2,2,1,1,128,256]{5,4,3,2,1,0:T(8,128)(2,1)S(1)}, bf16[2,2,1,1,128,256]{5,4,3,2,1,0:T(8,128)(2,1)S(1)}, u32[]{:S(2)}, u32[]{:S(2)}) collective-permute-start(bf16[2,2,1,1,128,256]{5,4,3,2,1,0:T(8,128)(2,1)S(1)} %maximum_maximum_fusion.1), channel_id=1, source_target_pairs={{0,6},{2,4},{4,2},{6,0},{8,14},{10,12},{12,10},{14,8},{16,22},{18,... | collective-permute-start | bytes 786440 | tf_op jit(solution)/shard_map/ppermute | solution.py:134
  15.5 0.5 collective-permute-start.3
  16.0 0.0 copy-done
  16.0 0.7 %fusion.2 = bf16[2,16,128,128]{3,1,2,0:T(8,128)(2,1)S(1)} fusion(bf16[2,16,128,128]{3,2,1,0:T(8,128)(2,1)S(1)} %bitcast.67, s32[2,16]{1,0:T(2,128)S(1)} %bitcast.79, pred[2,16]{1,0:T(4,128)(4,1)S(1)} %iota_compare_fusion.1), kind=kOutput, calls=%fused_computation.8 | convolution fusion | flops 16778240 | bytes 2097312 | tf_op jit(solution)/shard_map/tsq,tsab->tqab/dot_general | solution.py:226
  16.8 9.2 %collective-permute-done.4 = bf16[2,2,1,1,128,256]{5,4,3,2,1,0:T(8,128)(2,1)S(1)} collective-permute-done((bf16[2,2,1,1,128,256]{5,4,3,2,1,0:T(8,128)(2,1)S(1)}, bf16[2,2,1,1,128,256]{5,4,3,2,1,0:T(8,128)(2,1)S(1)}, u32[]{:S(2)}, u32[]{:S(2)}) %collective-permute-start.4) | collective-permute-done | bytes 262176 | tf_op jit(solution)/shard_map/ppermute | solution.py:133
  26.0 0.0 collective-permute-done.5
  26.0 1.3 %collective-permute-done.3 = bf16[2,2,1,1,128,256]{5,4,3,2,1,0:T(8,128)(2,1)S(1)} collective-permute-done((bf16[2,2,1,1,128,256]{5,4,3,2,1,0:T(8,128)(2,1)S(1)}, bf16[2,2,1,1,128,256]{5,4,3,2,1,0:T(8,128)(2,1)S(1)}, u32[]{:S(2)}, u32[]{:S(2)}) %collective-permute-start.3) | collective-permute-done | bytes 262176 | tf_op jit(solution)/shard_map/ppermute | solution.py:132
  27.3 0.0 copy-done.1
  27.3 0.1 maximum_maximum_fusion
  27.4 0.0 copy-start.2
  27.4 0.0 copy-start.3
  27.4 0.4 convolution_bitcast_fusion.1
  27.9 0.1 collective-permute-start.6
  28.0 1.5 %collective-permute-done.6 = f32[2,128,256]{2,1,0:T(8,128)S(1)} collective-permute-done((f32[2,128,256]{2,1,0:T(8,128)S(1)}, f32[2,128,256]{2,1,0:T(8,128)S(1)}, u32[]{:S(2)}, u32[]{:S(2)}) %collective-permute-start.6) | collective-permute-done | bytes 262176 | tf_op jit(solution)/shard_map/ppermute | solution.py:100
  29.5 0.0 copy-done.2
  29.5 0.0 copy-done.3
  29.5 0.3 multiply_convert_fusion
  29.8 0.2 fusion.17
  30.0 0.2 convolution_convert_fusion
  30.3 0.4 collective-permute-start.8
  30.7 2.2 %collective-permute-start.9 = (f32[128,256]{1,0:T(8,128)S(1)}, f32[128,256]{1,0:T(8,128)S(1)}, u32[]{:S(2)}, u32[]{:S(2)}) collective-permute-start(f32[128,256]{1,0:T(8,128)S(1)} %constant_dynamic-slice_fusion), channel_id=1, source_target_pairs={{0,24},{2,26},{4,28},{6,30},{8,16},{10,18},{12,20},{14,22},{16,8},... | collective-permute-start | bytes 393224 | tf_op jit(solution)/shard_map/ppermute | solution.py:191
  32.8 1.0 %collective-permute-start.7 = (f32[128,256]{1,0:T(8,128)S(1)}, f32[128,256]{1,0:T(8,128)S(1)}, u32[]{:S(2)}, u32[]{:S(2)}) collective-permute-start(f32[128,256]{1,0:T(8,128)S(1)} %constant_dynamic-slice_fusion), channel_id=1, source_target_pairs={{0,8},{2,10},{4,12},{6,14},{8,0},{10,2},{12,4},{14,6},{16,24},{18,... | collective-permute-start | bytes 393224 | tf_op jit(solution)/shard_map/ppermute | solution.py:189
  33.8 0.5 convolution_bitcast_fusion
  34.4 0.1 fusion.4
  34.4 0.1 copy_bitcast_fusion
  34.6 1.7 %collective-permute-start.14 = (bf16[2,2,128,256]{3,2,1,0:T(8,128)(2,1)S(1)}, bf16[2,2,128,256]{3,2,1,0:T(8,128)(2,1)S(1)}, u32[]{:S(2)}, u32[]{:S(2)}) collective-permute-start(bf16[2,2,128,256]{3,2,1,0:T(8,128)(2,1)S(1)} %fusion.6), channel_id=1, source_target_pairs={{0,2},{2,0},{4,6},{6,4},{8,10},{10,8},{12,14},{14,12},{16,18},{18,... | collective-permute-start | bytes 786440 | tf_op jit(solution)/shard_map/ppermute | solution.py:177
  36.3 1.5 %collective-permute-start.15 = (bf16[2,2,128,256]{3,2,1,0:T(8,128)(2,1)S(1)}, bf16[2,2,128,256]{3,2,1,0:T(8,128)(2,1)S(1)}, u32[]{:S(2)}, u32[]{:S(2)}) collective-permute-start(bf16[2,2,128,256]{3,2,1,0:T(8,128)(2,1)S(1)} %get-tuple-element.5), channel_id=1, source_target_pairs={{0,4},{2,6},{4,0},{6,2},{8,12},{10,14},{12,8},{14,10},{16,20},{18,... | collective-permute-start | bytes 786440 | tf_op jit(solution)/shard_map/ppermute | solution.py:178
  37.8 4.2 %collective-permute-done.8 = f32[128,256]{1,0:T(8,128)S(1)} collective-permute-done((f32[128,256]{1,0:T(8,128)S(1)}, f32[128,256]{1,0:T(8,128)S(1)}, u32[]{:S(2)}, u32[]{:S(2)}) %collective-permute-start.8) | collective-permute-done | bytes 131104 | tf_op jit(solution)/shard_map/ppermute | solution.py:190
  42.1 2.4 %collective-permute-start.16 = (bf16[2,2,128,256]{3,2,1,0:T(8,128)(2,1)S(1)}, bf16[2,2,128,256]{3,2,1,0:T(8,128)(2,1)S(1)}, u32[]{:S(2)}, u32[]{:S(2)}) collective-permute-start(bf16[2,2,128,256]{3,2,1,0:T(8,128)(2,1)S(1)} %get-tuple-element.6), channel_id=1, source_target_pairs={{0,6},{2,4},{4,2},{6,0},{8,14},{10,12},{12,10},{14,8},{16,22},{18,... | collective-permute-start | bytes 786440 | tf_op jit(solution)/shard_map/ppermute | solution.py:179
  44.5 0.6 %fusion.9 = bf16[128,256]{1,0:T(8,128)(2,1)} fusion(f32[256,256]{1,0:T(8,128)S(1)} %get-tuple-element.11, s32[]{:T(128)S(6)} %select_n.16, f32[256,256]{1,0:T(8,128)S(1)} %get-tuple-element.12), kind=kLoop, calls=%fused_computation.26 | loop fusion | flops 65536 | bytes 327684 | tf_op jit(solution)/shard_map/convert_element_type | solution.py:254
  45.1 0.0 collective-permute-done.9
  45.1 0.0 collective-permute-done.7
  45.2 0.7 %collective-permute-start.12 = (f32[128,256]{1,0:T(8,128)S(1)}, f32[128,256]{1,0:T(8,128)S(1)}, u32[]{:S(2)}, u32[]{:S(2)}) collective-permute-start(f32[128,256]{1,0:T(8,128)S(1)} %add_add_fusion), channel_id=1, source_target_pairs={{0,6},{2,4},{4,2},{6,0},{8,14},{10,12},{12,10},{14,8},{16,22},{18,... | collective-permute-start | bytes 393224 | tf_op jit(solution)/shard_map/ppermute | solution.py:191
  45.9 1.4 %collective-permute-start.11 = (f32[128,256]{1,0:T(8,128)S(1)}, f32[128,256]{1,0:T(8,128)S(1)}, u32[]{:S(2)}, u32[]{:S(2)}) collective-permute-start(f32[128,256]{1,0:T(8,128)S(1)} %add_add_fusion), channel_id=1, source_target_pairs={{0,4},{2,6},{4,0},{6,2},{8,12},{10,14},{12,8},{14,10},{16,20},{18,... | collective-permute-start | bytes 393224 | tf_op jit(solution)/shard_map/ppermute | solution.py:190
  47.3 0.0 collective-permute-done.14
  47.3 1.5 %collective-permute-start.10 = (f32[128,256]{1,0:T(8,128)S(1)}, f32[128,256]{1,0:T(8,128)S(1)}, u32[]{:S(2)}, u32[]{:S(2)}) collective-permute-start(f32[128,256]{1,0:T(8,128)S(1)} %add_add_fusion), channel_id=1, source_target_pairs={{0,2},{2,0},{4,6},{6,4},{8,10},{10,8},{12,14},{14,12},{16,18},{18,... | collective-permute-start | bytes 393224 | tf_op jit(solution)/shard_map/ppermute | solution.py:189
  48.8 0.0 collective-permute-done.15
  48.8 3.5 %collective-permute-done.16 = bf16[2,2,128,256]{3,2,1,0:T(8,128)(2,1)S(1)} collective-permute-done((bf16[2,2,128,256]{3,2,1,0:T(8,128)(2,1)S(1)}, bf16[2,2,128,256]{3,2,1,0:T(8,128)(2,1)S(1)}, u32[]{:S(2)}, u32[]{:S(2)}) %collective-permute-start.16) | collective-permute-done | bytes 262176 | tf_op jit(solution)/shard_map/ppermute | solution.py:179
  52.2 0.1 fusion.15
  52.4 0.1 collective-permute-start.17
  52.5 1.7 %collective-permute-start.19 = (bf16[128,256]{1,0:T(8,128)(2,1)S(1)}, bf16[128,256]{1,0:T(8,128)(2,1)S(1)}, u32[]{:S(2)}, u32[]{:S(2)}) collective-permute-start(bf16[128,256]{1,0:T(8,128)(2,1)S(1)} %get-tuple-element.8), channel_id=1, source_target_pairs={{0,24},{2,26},{4,28},{6,30},{8,16},{10,18},{12,20},{14,22},{16,8},... | collective-permute-start | bytes 196616 | tf_op jit(solution)/shard_map/ppermute | solution.py:179
  54.2 0.8 %collective-permute-done.12 = f32[128,256]{1,0:T(8,128)S(1)} collective-permute-done((f32[128,256]{1,0:T(8,128)S(1)}, f32[128,256]{1,0:T(8,128)S(1)}, u32[]{:S(2)}, u32[]{:S(2)}) %collective-permute-start.12) | collective-permute-done | bytes 131104 | tf_op jit(solution)/shard_map/ppermute | solution.py:191
  55.0 0.9 %collective-permute-start.18 = (bf16[128,256]{1,0:T(8,128)(2,1)S(1)}, bf16[128,256]{1,0:T(8,128)(2,1)S(1)}, u32[]{:S(2)}, u32[]{:S(2)}) collective-permute-start(bf16[128,256]{1,0:T(8,128)(2,1)S(1)} %get-tuple-element.9), channel_id=1, source_target_pairs={{0,16},{2,18},{4,20},{6,22},{8,24},{10,26},{12,28},{14,30},{16,0},... | collective-permute-start | bytes 196616 | tf_op jit(solution)/shard_map/ppermute | solution.py:178
  55.9 0.8 %collective-permute-done.11 = f32[128,256]{1,0:T(8,128)S(1)} collective-permute-done((f32[128,256]{1,0:T(8,128)S(1)}, f32[128,256]{1,0:T(8,128)S(1)}, u32[]{:S(2)}, u32[]{:S(2)}) %collective-permute-start.11) | collective-permute-done | bytes 131104 | tf_op jit(solution)/shard_map/ppermute | solution.py:190
  56.7 0.1 collective-permute-done.10
  56.9 0.1 collective-permute-start.13
  57.0 0.0 collective-permute-done.17
  57.0 1.7 %collective-permute-done.19 = bf16[128,256]{1,0:T(8,128)(2,1)S(1)} collective-permute-done((bf16[128,256]{1,0:T(8,128)(2,1)S(1)}, bf16[128,256]{1,0:T(8,128)(2,1)S(1)}, u32[]{:S(2)}, u32[]{:S(2)}) %collective-permute-start.19) | collective-permute-done | bytes 65568 | tf_op jit(solution)/shard_map/ppermute | solution.py:179
  58.7 1.9 %collective-permute-done.18 = bf16[128,256]{1,0:T(8,128)(2,1)S(1)} collective-permute-done((bf16[128,256]{1,0:T(8,128)(2,1)S(1)}, bf16[128,256]{1,0:T(8,128)(2,1)S(1)}, u32[]{:S(2)}, u32[]{:S(2)}) %collective-permute-start.18) | collective-permute-done | bytes 65568 | tf_op jit(solution)/shard_map/ppermute | solution.py:178
  60.6 0.7 %fusion.8 = bf16[128,256]{1,0:T(8,128)(2,1)} fusion(f32[2,2,128,256]{3,2,1,0:T(8,128)S(1)} %get-tuple-element.4, bf16[128,256]{1,0:T(8,128)(2,1)S(1)} %collective-permute-done.19, bf16[128,256]{1,0:T(8,128)(2,1)S(1)} %collective-permute-done.18, bf16[128,256]{1,0:T(8,128)(2,1)S(1)} %collective-permute-done.17), kind=kLoop, calls=%fused_computation.24 | loop fusion | flops 229376 | bytes 393216 | tf_op jit(solution)/shard_map/convert_element_type | solution.py:300
  61.2 0.0 collective-permute-done.13
  61.2 0.7 %maximum_select_fusion = f32[2,128,256]{2,1,0:T(8,128)} fusion(f32[1,128,256]{2,1,0:T(8,128)S(1)} %collective-permute-done.13, f32[1,128,256]{2,1,0:T(8,128)S(1)} %add_bitcast_fusion, pred[]{:T(512)S(6)} %eq.19), kind=kLoop, calls=%fused_computation.18 | loop fusion | flops 196608 | bytes 524289 | tf_op jit(solution)/shard_map/jit(_where)/select_n | solution.py:110
  (7 shorter events, 0.2 us)
Async XLA Ops:
  0.6 15.4 %copy-start = (bf16[2,1,16,128,128]{4,3,2,1,0:T(8,128)(2,1)S(1)}, bf16[2,1,16,128,128]{4,3,2,1,0:T(8,128)(2,1)}, u32[]{:S(2)}) copy-start(bf16[2,1,16,128,128]{4,3,2,1,0:T(8,128)(2,1)} %param.9) | copy-start | bytes 3145732
  0.6 26.6 %copy-start.1 = (bf16[128,256]{1,0:T(8,128)(2,1)S(1)}, bf16[128,256]{1,0:T(8,128)(2,1)}, u32[]{:S(2)}) copy-start(bf16[128,256]{1,0:T(8,128)(2,1)} %param.6) | copy-start | bytes 196612
  0.7 7.9 %collective-permute-start.2 = (bf16[1,1,1,1,128,256]{5,4,3,2,1,0:T(8,128)(2,1)}, bf16[1,1,1,1,128,256]{5,4,3,2,1,0:T(8,128)(2,1)S(1)}, u32[]{:S(2)}, u32[]{:S(2)}) collective-permute-start(bf16[1,1,1,1,128,256]{5,4,3,2,1,0:T(8,128)(2,1)} %bitcast.74), channel_id=1, source_target_pairs={{0,24},{2,26},{4,28},{6,30},{8,16},{10,18},{12,20},{14,22},{16,8},... | collective-permute-start | bytes 196616 | tf_op jit(solution)/shard_map/ppermute | solution.py:134
  5.8 5.8 %collective-permute-start.1 = (bf16[1,1,1,1,128,256]{5,4,3,2,1,0:T(8,128)(2,1)}, bf16[1,1,1,1,128,256]{5,4,3,2,1,0:T(8,128)(2,1)S(1)}, u32[]{:S(2)}, u32[]{:S(2)}) collective-permute-start(bf16[1,1,1,1,128,256]{5,4,3,2,1,0:T(8,128)(2,1)} %bitcast.75), channel_id=1, source_target_pairs={{0,16},{2,18},{4,20},{6,22},{8,24},{10,26},{12,28},{14,30},{16,0},... | collective-permute-start | bytes 196616 | tf_op jit(solution)/shard_map/ppermute | solution.py:133
  5.8 5.8 %collective-permute-start = (bf16[1,1,1,1,128,256]{5,4,3,2,1,0:T(8,128)(2,1)}, bf16[1,1,1,1,128,256]{5,4,3,2,1,0:T(8,128)(2,1)S(1)}, u32[]{:S(2)}, u32[]{:S(2)}) collective-permute-start(bf16[1,1,1,1,128,256]{5,4,3,2,1,0:T(8,128)(2,1)} %bitcast.76), channel_id=1, source_target_pairs={{0,8},{2,10},{4,12},{6,14},{8,0},{10,2},{12,4},{14,6},{16,24},{18,... | collective-permute-start | bytes 196616 | tf_op jit(solution)/shard_map/ppermute | solution.py:132
  12.5 13.6 %collective-permute-start.4 = (bf16[2,2,1,1,128,256]{5,4,3,2,1,0:T(8,128)(2,1)S(1)}, bf16[2,2,1,1,128,256]{5,4,3,2,1,0:T(8,128)(2,1)S(1)}, u32[]{:S(2)}, u32[]{:S(2)}) collective-permute-start(bf16[2,2,1,1,128,256]{5,4,3,2,1,0:T(8,128)(2,1)S(1)} %maximum_maximum_fusion.1), channel_id=1, source_target_pairs={{0,4},{2,6},{4,0},{6,2},{8,12},{10,14},{12,8},{14,10},{16,20},{18,... | collective-permute-start | bytes 786440 | tf_op jit(solution)/shard_map/ppermute | solution.py:133
  14.0 12.0 %collective-permute-start.5 = (bf16[2,2,1,1,128,256]{5,4,3,2,1,0:T(8,128)(2,1)S(1)}, bf16[2,2,1,1,128,256]{5,4,3,2,1,0:T(8,128)(2,1)S(1)}, u32[]{:S(2)}, u32[]{:S(2)}) collective-permute-start(bf16[2,2,1,1,128,256]{5,4,3,2,1,0:T(8,128)(2,1)S(1)} %maximum_maximum_fusion.1), channel_id=1, source_target_pairs={{0,6},{2,4},{4,2},{6,0},{8,14},{10,12},{12,10},{14,8},{16,22},{18,... | collective-permute-start | bytes 786440 | tf_op jit(solution)/shard_map/ppermute | solution.py:134
  15.5 11.8 %collective-permute-start.3 = (bf16[2,2,1,1,128,256]{5,4,3,2,1,0:T(8,128)(2,1)S(1)}, bf16[2,2,1,1,128,256]{5,4,3,2,1,0:T(8,128)(2,1)S(1)}, u32[]{:S(2)}, u32[]{:S(2)}) collective-permute-start(bf16[2,2,1,1,128,256]{5,4,3,2,1,0:T(8,128)(2,1)S(1)} %maximum_maximum_fusion.1), channel_id=1, source_target_pairs={{0,2},{2,0},{4,6},{6,4},{8,10},{10,8},{12,14},{14,12},{16,18},{18,... | collective-permute-start | bytes 786440 | tf_op jit(solution)/shard_map/ppermute | solution.py:132
  27.4 2.1 %copy-start.2 = (bf16[256,256]{1,0:T(8,128)(2,1)S(1)}, bf16[256,256]{1,0:T(8,128)(2,1)}, u32[]{:S(2)}) copy-start(bf16[256,256]{1,0:T(8,128)(2,1)} %param.8) | copy-start | bytes 393220
  27.4 2.1 %copy-start.3 = (bf16[256,256]{1,0:T(8,128)(2,1)S(1)}, bf16[256,256]{1,0:T(8,128)(2,1)}, u32[]{:S(2)}) copy-start(bf16[256,256]{1,0:T(8,128)(2,1)} %param.7) | copy-start | bytes 393220
  27.9 1.6 %collective-permute-start.6 = (f32[2,128,256]{2,1,0:T(8,128)S(1)}, f32[2,128,256]{2,1,0:T(8,128)S(1)}, u32[]{:S(2)}, u32[]{:S(2)}) collective-permute-start(f32[2,128,256]{2,1,0:T(8,128)S(1)} %convolution_bitcast_fusion.1), channel_id=1, source_target_pairs={{0,1},{1,0},{2,3},{3,2},{4,5},{5,4},{6,7},{7,6},{8,9},{9,8},{10,11... | collective-permute-start | bytes 786440 | tf_op jit(solution)/shard_map/ppermute | solution.py:100
  30.3 11.8 %collective-permute-start.8 = (f32[128,256]{1,0:T(8,128)S(1)}, f32[128,256]{1,0:T(8,128)S(1)}, u32[]{:S(2)}, u32[]{:S(2)}) collective-permute-start(f32[128,256]{1,0:T(8,128)S(1)} %constant_dynamic-slice_fusion), channel_id=1, source_target_pairs={{0,16},{2,18},{4,20},{6,22},{8,24},{10,26},{12,28},{14,30},{16,0},... | collective-permute-start | bytes 393224 | tf_op jit(solution)/shard_map/ppermute | solution.py:190
  30.7 14.5 %collective-permute-start.9 = (f32[128,256]{1,0:T(8,128)S(1)}, f32[128,256]{1,0:T(8,128)S(1)}, u32[]{:S(2)}, u32[]{:S(2)}) collective-permute-start(f32[128,256]{1,0:T(8,128)S(1)} %constant_dynamic-slice_fusion), channel_id=1, source_target_pairs={{0,24},{2,26},{4,28},{6,30},{8,16},{10,18},{12,20},{14,22},{16,8},... | collective-permute-start | bytes 393224 | tf_op jit(solution)/shard_map/ppermute | solution.py:191
  32.8 12.3 %collective-permute-start.7 = (f32[128,256]{1,0:T(8,128)S(1)}, f32[128,256]{1,0:T(8,128)S(1)}, u32[]{:S(2)}, u32[]{:S(2)}) collective-permute-start(f32[128,256]{1,0:T(8,128)S(1)} %constant_dynamic-slice_fusion), channel_id=1, source_target_pairs={{0,8},{2,10},{4,12},{6,14},{8,0},{10,2},{12,4},{14,6},{16,24},{18,... | collective-permute-start | bytes 393224 | tf_op jit(solution)/shard_map/ppermute | solution.py:189
  34.6 12.7 %collective-permute-start.14 = (bf16[2,2,128,256]{3,2,1,0:T(8,128)(2,1)S(1)}, bf16[2,2,128,256]{3,2,1,0:T(8,128)(2,1)S(1)}, u32[]{:S(2)}, u32[]{:S(2)}) collective-permute-start(bf16[2,2,128,256]{3,2,1,0:T(8,128)(2,1)S(1)} %fusion.6), channel_id=1, source_target_pairs={{0,2},{2,0},{4,6},{6,4},{8,10},{10,8},{12,14},{14,12},{16,18},{18,... | collective-permute-start | bytes 786440 | tf_op jit(solution)/shard_map/ppermute | solution.py:177
  36.3 12.5 %collective-permute-start.15 = (bf16[2,2,128,256]{3,2,1,0:T(8,128)(2,1)S(1)}, bf16[2,2,128,256]{3,2,1,0:T(8,128)(2,1)S(1)}, u32[]{:S(2)}, u32[]{:S(2)}) collective-permute-start(bf16[2,2,128,256]{3,2,1,0:T(8,128)(2,1)S(1)} %get-tuple-element.5), channel_id=1, source_target_pairs={{0,4},{2,6},{4,0},{6,2},{8,12},{10,14},{12,8},{14,10},{16,20},{18,... | collective-permute-start | bytes 786440 | tf_op jit(solution)/shard_map/ppermute | solution.py:178
  42.1 10.2 %collective-permute-start.16 = (bf16[2,2,128,256]{3,2,1,0:T(8,128)(2,1)S(1)}, bf16[2,2,128,256]{3,2,1,0:T(8,128)(2,1)S(1)}, u32[]{:S(2)}, u32[]{:S(2)}) collective-permute-start(bf16[2,2,128,256]{3,2,1,0:T(8,128)(2,1)S(1)} %get-tuple-element.6), channel_id=1, source_target_pairs={{0,6},{2,4},{4,2},{6,0},{8,14},{10,12},{12,10},{14,8},{16,22},{18,... | collective-permute-start | bytes 786440 | tf_op jit(solution)/shard_map/ppermute | solution.py:179
  45.2 9.8 %collective-permute-start.12 = (f32[128,256]{1,0:T(8,128)S(1)}, f32[128,256]{1,0:T(8,128)S(1)}, u32[]{:S(2)}, u32[]{:S(2)}) collective-permute-start(f32[128,256]{1,0:T(8,128)S(1)} %add_add_fusion), channel_id=1, source_target_pairs={{0,6},{2,4},{4,2},{6,0},{8,14},{10,12},{12,10},{14,8},{16,22},{18,... | collective-permute-start | bytes 393224 | tf_op jit(solution)/shard_map/ppermute | solution.py:191
  45.9 10.9 %collective-permute-start.11 = (f32[128,256]{1,0:T(8,128)S(1)}, f32[128,256]{1,0:T(8,128)S(1)}, u32[]{:S(2)}, u32[]{:S(2)}) collective-permute-start(f32[128,256]{1,0:T(8,128)S(1)} %add_add_fusion), channel_id=1, source_target_pairs={{0,4},{2,6},{4,0},{6,2},{8,12},{10,14},{12,8},{14,10},{16,20},{18,... | collective-permute-start | bytes 393224 | tf_op jit(solution)/shard_map/ppermute | solution.py:190
  47.3 9.6 %collective-permute-start.10 = (f32[128,256]{1,0:T(8,128)S(1)}, f32[128,256]{1,0:T(8,128)S(1)}, u32[]{:S(2)}, u32[]{:S(2)}) collective-permute-start(f32[128,256]{1,0:T(8,128)S(1)} %add_add_fusion), channel_id=1, source_target_pairs={{0,2},{2,0},{4,6},{6,4},{8,10},{10,8},{12,14},{14,12},{16,18},{18,... | collective-permute-start | bytes 393224 | tf_op jit(solution)/shard_map/ppermute | solution.py:189
  52.4 4.6 %collective-permute-start.17 = (bf16[128,256]{1,0:T(8,128)(2,1)S(1)}, bf16[128,256]{1,0:T(8,128)(2,1)S(1)}, u32[]{:S(2)}, u32[]{:S(2)}) collective-permute-start(bf16[128,256]{1,0:T(8,128)(2,1)S(1)} %get-tuple-element.7), channel_id=1, source_target_pairs={{0,8},{2,10},{4,12},{6,14},{8,0},{10,2},{12,4},{14,6},{16,24},{18,... | collective-permute-start | bytes 196616 | tf_op jit(solution)/shard_map/ppermute | solution.py:177
  52.5 6.2 %collective-permute-start.19 = (bf16[128,256]{1,0:T(8,128)(2,1)S(1)}, bf16[128,256]{1,0:T(8,128)(2,1)S(1)}, u32[]{:S(2)}, u32[]{:S(2)}) collective-permute-start(bf16[128,256]{1,0:T(8,128)(2,1)S(1)} %get-tuple-element.8), channel_id=1, source_target_pairs={{0,24},{2,26},{4,28},{6,30},{8,16},{10,18},{12,20},{14,22},{16,8},... | collective-permute-start | bytes 196616 | tf_op jit(solution)/shard_map/ppermute | solution.py:179
  55.0 5.6 %collective-permute-start.18 = (bf16[128,256]{1,0:T(8,128)(2,1)S(1)}, bf16[128,256]{1,0:T(8,128)(2,1)S(1)}, u32[]{:S(2)}, u32[]{:S(2)}) collective-permute-start(bf16[128,256]{1,0:T(8,128)(2,1)S(1)} %get-tuple-element.9), channel_id=1, source_target_pairs={{0,16},{2,18},{4,20},{6,22},{8,24},{10,26},{12,28},{14,30},{16,0},... | collective-permute-start | bytes 196616 | tf_op jit(solution)/shard_map/ppermute | solution.py:178
  56.9 4.3 %collective-permute-start.13 = (f32[1,128,256]{2,1,0:T(8,128)S(1)}, f32[1,128,256]{2,1,0:T(8,128)S(1)}, u32[]{:S(2)}, u32[]{:S(2)}) collective-permute-start(f32[1,128,256]{2,1,0:T(8,128)S(1)} %add_bitcast_fusion), channel_id=1, source_target_pairs={{0,1},{1,0},{2,3},{3,2},{4,5},{5,4},{6,7},{7,6},{8,9},{9,8},{10,11... | collective-permute-start | bytes 393224 | tf_op jit(solution)/shard_map/ppermute | solution.py:108

commit v6 on v1

v6 whole, which is shorter than its diff:
```python
import jax
import jax.numpy as jnp
from jax import lax
from jax.sharding import PartitionSpec as P


def bit_count(n):
    return n.bit_length() - 1


def pairs_of(n, mask):
    return [(j, j ^ mask) for j in range(n)]


def bit_rounds(nb):
    rounds = []
    top = nb
    while top > 0:
        rounds.append(tuple(range(max(top - 2, 0), top)))
        top -= 2
    return rounds


def radix_gather(x, n):
    nb = bit_count(n)
    held = x.reshape((1,) * nb + x.shape)
    for bits in bit_rounds(nb):
        if len(bits) == 1:
            got = lax.ppermute(held, "rows", pairs_of(n, 1 << bits[0]))
            held = jnp.concatenate([held, got], axis=nb - 1 - bits[0])
            continue
        low, high = bits
        got_low = lax.ppermute(held, "rows", pairs_of(n, 1 << low))
        got_high = lax.ppermute(held, "rows", pairs_of(n, 1 << high))
        got_both = lax.ppermute(held, "rows", pairs_of(n, (1 << low) | (1 << high)))
        first = jnp.concatenate([held, got_low], axis=nb - 1 - low)
        second = jnp.concatenate([got_high, got_both], axis=nb - 1 - low)
        held = jnp.concatenate([first, second], axis=nb - 1 - high)
    return held


def scatter_round(cur, bits, n, send_dtype):
    lead = cur.ndim - 2
    if len(bits) == 1:
        keep = lax.index_in_dim(cur, 0, lead - 1, keepdims=False)
        send = lax.index_in_dim(cur, 1, lead - 1, keepdims=False)
        return keep + lax.ppermute(send.astype(send_dtype), "rows", pairs_of(n, 1 << bits[0])).astype(jnp.float32)
    low, high = bits

    def part(h, l):
        return lax.index_in_dim(lax.index_in_dim(cur, h, lead - 2, keepdims=False), l, lead - 2, keepdims=False)

    got_low = lax.ppermute(part(0, 1).astype(send_dtype), "rows", pairs_of(n, 1 << low))
    got_high = lax.ppermute(part(1, 0).astype(send_dtype), "rows", pairs_of(n, 1 << high))
    got_both = lax.ppermute(part(1, 1).astype(send_dtype), "rows", pairs_of(n, (1 << low) | (1 << high)))
    return part(0, 0) + (got_low.astype(jnp.float32) + got_high.astype(jnp.float32) + got_both.astype(jnp.float32))


def sum_round(w, bits, n):
    if len(bits) == 1:
        return w + lax.ppermute(w, "rows", pairs_of(n, 1 << bits[0]))
    low, high = bits
    got_low = lax.ppermute(w, "rows", pairs_of(n, 1 << low))
    got_high = lax.ppermute(w, "rows", pairs_of(n, 1 << high))
    got_both = lax.ppermute(w, "rows", pairs_of(n, (1 << low) | (1 << high)))
    return (w + got_low) + (got_high + got_both)


def paired_backward(rel, w, n, send_dtype):
    rounds = bit_rounds(bit_count(n))
    cur = rel
    for k, bits in enumerate(rounds[::-1]):
        cur = scatter_round(cur, bits, n, send_dtype)
        w = sum_round(w, rounds[k], n)
    return cur, w


def rep_sum(x, n):
    for b in range(bit_count(n)):
        x = x + lax.ppermute(x, "rep", pairs_of(n, 1 << b))
    return x


def rep_gather(x, n):
    me = lax.axis_index("rep")
    buf = x[None]
    for b in range(bit_count(n)):
        got = lax.ppermute(buf, "rep", pairs_of(n, 1 << b))
        low = ((me >> b) & 1) == 0
        buf = jnp.where(low, jnp.concatenate([buf, got]), jnp.concatenate([got, buf]))
    return buf


def local(features, cotangent, weight, tile_vals, tile_cols, tile_count):
    n_rows = lax.axis_size("rows")
    n_rep = lax.axis_size("rep")
    tile = tile_vals.shape[-1]
    slots = tile_vals.shape[2]
    panel_tiles = tile_vals.shape[0]
    block_rows = features.shape[0]
    feat_width = features.shape[1]
    nb = bit_count(n_rows)
    me_rep = lax.axis_index("rep")
    me_rows = lax.axis_index("rows")

    values = tile_vals[:, 0]
    columns = tile_cols[:, 0]
    filled = tile_count[:, 0]

    is_live = jnp.arange(slots, dtype=jnp.int32)[None, :] < filled[:, None]
    relative = jnp.bitwise_xor(columns, me_rows)
    picks = (relative[:, :, None] == jnp.arange(n_rows, dtype=jnp.int32)[None, None, :]) & is_live[:, :, None]
    sorted_rel = jnp.einsum(
        "tsq,tsab->tqab", picks.astype(jnp.bfloat16), values, preferred_element_type=jnp.bfloat16
    )

    held = radix_gather(features, n_rows).reshape(n_rows, block_rows, feat_width)
    partial_value = jnp.einsum("tqab,qbf->taf", sorted_rel, held, preferred_element_type=jnp.float32)
    aggregated = rep_sum(partial_value, n_rep).reshape(panel_tiles * tile, feat_width).astype(jnp.bfloat16)

    preact = jnp.dot(aggregated, weight, preferred_element_type=jnp.float32)
    sigmoid_part = jax.nn.sigmoid(preact)
    output = (preact * sigmoid_part).astype(jnp.bfloat16)
    output = lax.dynamic_slice_in_dim(output, me_rep * block_rows, block_rows, 0)
    grad_pre = (
        cotangent.astype(jnp.float32) * sigmoid_part * (1.0 + preact * (1.0 - sigmoid_part))
    ).astype(jnp.bfloat16)
    pulled = lax.dot_general(
        grad_pre, weight, (((1,), (1,)), ((), ())), preferred_element_type=jnp.float32
    ).astype(jnp.bfloat16)
    local_weight = lax.dot_general(
        aggregated, grad_pre, (((0,), (0,)), ((), ())), preferred_element_type=jnp.float32
    )

    slice_rows = feat_width // n_rep
    w_slice = lax.dynamic_slice_in_dim(local_weight, me_rep * slice_rows, slice_rows, 0)

    pulled_tiles = pulled.reshape(panel_tiles, tile, feat_width)
    products = jnp.einsum("tqab,taf->qbf", sorted_rel, pulled_tiles, preferred_element_type=jnp.float32)
    products = products.reshape((2,) * nb + (block_rows, feat_width))
    summed, w_slice = paired_backward(products, w_slice, n_rows, jnp.bfloat16)
    feature_grad = summed.astype(jnp.bfloat16)
    weight_grad = rep_gather(w_slice, n_rep).reshape(feat_width, feat_width)
    return (output, weight_grad, feature_grad)


def solution(mesh):
    return jax.shard_map(
        local,
        mesh=mesh,
        in_specs=(
            P(("rows", "rep"), None),
            P("rows", None),
            P(),
            P("rows", "rep", None, None, None),
            P("rows", "rep", None),
            P("rows", "rep"),
        ),
        out_specs=(P(("rows", "rep"), None), P(), P(("rows", "rep"), None)),
        check_vma=False,
    )
```

time: 99 us -> 62.1 us (0.63)
  blocking collectives: 37.9 us -> 0 us
  starting transfers between devices: 11.3 us -> 25 us
  waiting for transfers between devices: 38.3 us -> 28.8 us
  local copies, waits for them, and re-layouts: 2.31 us -> 0.25 us
  matrix products: 4.22 us -> 2.43 us
    all_to_all x1 -> x0, blocking collectives: 37.9 us -> none  [local(): received = lax.all_to_all(packed, 'rows', 0, 0, tiled=True)]
    ppermute x12 -> x20, starting transfers between devices: 11.3 us -> 25 us  [the longest x2 6.55 us: radix_gather(): got_both = lax.ppermute(held, 'rows', pairs_of(n, 1 << low | 1 << high))]
    ppermute x12 -> x20, waiting for transfers between devices: 38.3 us -> 28.8 us  [the longest x2 12.2 us: radix_gather(): got_high = lax.ppermute(held, 'rows', pairs_of(n, 1 << high))]
    select_n x9 -> x1, other arithmetic: 3.57 us -> 0.72 us  [rep_gather(): jnp.where(low, jnp.concatenate([buf, got]), jnp.concatenate([got, buf]))]
    gather x1 -> x0, local copies, waits for them, and re-layouts: 1.6 us -> none  [local(): gathered = jnp.take(gathered, natural, axis=0)]
    convert_element_type x1 -> x3, other arithmetic: 0.02 us -> 1.34 us  [the longest x1 0.66 us: local(): feature_grad = summed.astype(jnp.bfloat16)]
    dot_general x2, matrix products: 2.23 us -> 0.97 us  [the longest x1 0.53 us: local(): jnp.einsum('tqab,taf->qbf', sorted_rel, pulled_tiles, preferred_element_t...]
  transfers between devices with their start and end apart: 12 -> 20, of which waited for: 11 -> 12; matrix products, arithmetic and copies ran while one was open for 2% -> 7% of each run, Pallas kernels for 0% -> 0%
where the time goes in v6:
time: 62.1 us; the launch traced here: 61.9 us
  waiting for transfers between devices  28.8 us (46%)
  starting transfers between devices  25 us (40%)
  other arithmetic  4.62 us (7%)
  matrix products  2.43 us (4%)
  between operations  0.85 us (1%)
    ppermute x2, waiting for transfers between devices, radix_gather(): got_high = lax.ppermute(held, 'rows', pairs_of(n, 1 << high))  12.2 us
    ppermute x2, starting transfers between devices, radix_gather(): got_both = lax.ppermute(held, 'rows', pairs_of(n, 1 << low | 1 << high))  6.55 us
    ppermute x2, waiting for transfers between devices, scatter_round(): lax.ppermute(part(1, 1).astype(send_dtype), 'rows', pairs_of(n, 1 << low...  5.19 us
    ppermute x2, waiting for transfers between devices, sum_round(): got_high = lax.ppermute(w, 'rows', pairs_of(n, 1 << high))  5.04 us
    ppermute x2, starting transfers between devices, scatter_round(): lax.ppermute(part(1, 1).astype(send_dtype), 'rows', pairs_of(n, 1 << low...  4.19 us
    ppermute x2, starting transfers between devices, sum_round(): got_both = lax.ppermute(w, 'rows', pairs_of(n, 1 << low | 1 << high))  2.83 us
    ppermute x2, starting transfers between devices, sum_round(): got_low = lax.ppermute(w, 'rows', pairs_of(n, 1 << low))  2.53 us
    ppermute x2, starting transfers between devices, scatter_round(): lax.ppermute(part(1, 0).astype(send_dtype), 'rows', pairs_of(n, 1 << high))  2.46 us
  transfers between devices with their start and end apart: 20, of which 12 were waited for; matrix products, arithmetic and copies ran while one was open for 7% of the time, Pallas kernels for 0%

profile of v6, /device:TPU:0, one launch (start us, length us, event | category | flops | bytes accessed | tf_op | source)
XLA Modules:
  0.0 61.9 jit_solution(12278830976291450029)
XLA Ops:
  0.6 0.0 copy-start
  0.6 0.0 copy-start.1
  0.7 5.1 %collective-permute-start.2 = (bf16[1,1,1,1,128,256]{5,4,3,2,1,0:T(8,128)(2,1)}, bf16[1,1,1,1,128,256]{5,4,3,2,1,0:T(8,128)(2,1)S(1)}, u32[]{:S(2)}, u32[]{:S(2)}) collective-permute-start(bf16[1,1,1,1,128,256]{5,4,3,2,1,0:T(8,128)(2,1)} %bitcast.74), channel_id=1, source_target_pairs={{0,24},{2,26},{4,28},{6,30},{8,16},{10,18},{12,20},{14,22},{16,8},... | collective-permute-start | bytes 196616 | tf_op jit(solution)/shard_map/ppermute | solution.py:35
  5.8 0.0 collective-permute-start.1
  5.8 0.6 %collective-permute-start = (bf16[1,1,1,1,128,256]{5,4,3,2,1,0:T(8,128)(2,1)}, bf16[1,1,1,1,128,256]{5,4,3,2,1,0:T(8,128)(2,1)S(1)}, u32[]{:S(2)}, u32[]{:S(2)}) collective-permute-start(bf16[1,1,1,1,128,256]{5,4,3,2,1,0:T(8,128)(2,1)} %bitcast.76), channel_id=1, source_target_pairs={{0,8},{2,10},{4,12},{6,14},{8,0},{10,2},{12,4},{14,6},{16,24},{18,... | collective-permute-start | bytes 196616 | tf_op jit(solution)/shard_map/ppermute | solution.py:33
  6.4 0.7 %broadcast_xor_fusion = s32[2,1,16]{2,1,0:T(1,128)S(1)} fusion(s32[2,1,16]{2,1,0:T(1,128)} %param.10, s32[]{:T(128)S(6)} %axis_index.27), kind=kLoop, calls=%fused_computation.39 | loop fusion | flops 32 | bytes 260 | tf_op jit(solution)/shard_map/xor | solution.py:111
  7.1 0.7 %iota_compare_fusion.1 = pred[2,16]{1,0:T(4,128)(4,1)S(1)} fusion(s32[2]{0:T(128)} %bitcast.80), kind=kLoop, calls=%fused_computation.37 | loop fusion | flops 32 | bytes 40 | tf_op jit(solution)/shard_map/lt | solution.py:110
  7.8 0.8 %collective-permute-done.2 = bf16[1,1,1,1,128,256]{5,4,3,2,1,0:T(8,128)(2,1)S(1)} collective-permute-done((bf16[1,1,1,1,128,256]{5,4,3,2,1,0:T(8,128)(2,1)}, bf16[1,1,1,1,128,256]{5,4,3,2,1,0:T(8,128)(2,1)S(1)}, u32[]{:S(2)}, u32[]{:S(2)}) %collective-permute-start.2) | collective-permute-done | bytes 65568 | tf_op jit(solution)/shard_map/ppermute | solution.py:35
  8.6 3.0 %collective-permute-done.1 = bf16[1,1,1,1,128,256]{5,4,3,2,1,0:T(8,128)(2,1)S(1)} collective-permute-done((bf16[1,1,1,1,128,256]{5,4,3,2,1,0:T(8,128)(2,1)}, bf16[1,1,1,1,128,256]{5,4,3,2,1,0:T(8,128)(2,1)S(1)}, u32[]{:S(2)}, u32[]{:S(2)}) %collective-permute-start.1) | collective-permute-done | bytes 65568 | tf_op jit(solution)/shard_map/ppermute | solution.py:34
  11.6 0.0 collective-permute-done
  11.6 0.9 %maximum_maximum_fusion.1 = bf16[2,2,1,1,128,256]{5,4,3,2,1,0:T(8,128)(2,1)S(1)} fusion(bf16[1,1,1,1,128,256]{5,4,3,2,1,0:T(8,128)(2,1)S(1)} %collective-permute-done.2, bf16[1,1,1,1,128,256]{5,4,3,2,1,0:T(8,128)(2,1)S(1)} %collective-permute-done.1, bf16[1,1,1,1,128,256]{5,4,3,2,1,0:T(8,128)(2,1)S(1)} %collective-permute-done, ...), kind=kLoop, calls=%fused_computation.17 | loop fusion | flops 393216 | bytes 524288 | tf_op jit(solution)/shard_map/concatenate | solution.py:38
  12.5 1.6 %collective-permute-start.4 = (bf16[2,2,1,1,128,256]{5,4,3,2,1,0:T(8,128)(2,1)S(1)}, bf16[2,2,1,1,128,256]{5,4,3,2,1,0:T(8,128)(2,1)S(1)}, u32[]{:S(2)}, u32[]{:S(2)}) collective-permute-start(bf16[2,2,1,1,128,256]{5,4,3,2,1,0:T(8,128)(2,1)S(1)} %maximum_maximum_fusion.1), channel_id=1, source_target_pairs={{0,4},{2,6},{4,0},{6,2},{8,12},{10,14},{12,8},{14,10},{16,20},{18,... | collective-permute-start | bytes 786440 | tf_op jit(solution)/shard_map/ppermute | solution.py:34
  14.0 1.4 %collective-permute-start.5 = (bf16[2,2,1,1,128,256]{5,4,3,2,1,0:T(8,128)(2,1)S(1)}, bf16[2,2,1,1,128,256]{5,4,3,2,1,0:T(8,128)(2,1)S(1)}, u32[]{:S(2)}, u32[]{:S(2)}) collective-permute-start(bf16[2,2,1,1,128,256]{5,4,3,2,1,0:T(8,128)(2,1)S(1)} %maximum_maximum_fusion.1), channel_id=1, source_target_pairs={{0,6},{2,4},{4,2},{6,0},{8,14},{10,12},{12,10},{14,8},{16,22},{18,... | collective-permute-start | bytes 786440 | tf_op jit(solution)/shard_map/ppermute | solution.py:35
  15.5 0.5 collective-permute-start.3
  16.0 0.0 copy-done
  16.0 0.7 %fusion.2 = bf16[2,16,128,128]{3,1,2,0:T(8,128)(2,1)S(1)} fusion(bf16[2,16,128,128]{3,2,1,0:T(8,128)(2,1)S(1)} %bitcast.67, s32[2,16]{1,0:T(2,128)S(1)} %bitcast.79, pred[2,16]{1,0:T(4,128)(4,1)S(1)} %iota_compare_fusion.1), kind=kOutput, calls=%fused_computation.8 | convolution fusion | flops 16778240 | bytes 2097312 | tf_op jit(solution)/shard_map/tsq,tsab->tqab/dot_general | solution.py:113
  16.8 9.2 %collective-permute-done.4 = bf16[2,2,1,1,128,256]{5,4,3,2,1,0:T(8,128)(2,1)S(1)} collective-permute-done((bf16[2,2,1,1,128,256]{5,4,3,2,1,0:T(8,128)(2,1)S(1)}, bf16[2,2,1,1,128,256]{5,4,3,2,1,0:T(8,128)(2,1)S(1)}, u32[]{:S(2)}, u32[]{:S(2)}) %collective-permute-start.4) | collective-permute-done | bytes 262176 | tf_op jit(solution)/shard_map/ppermute | solution.py:34
  26.0 0.0 collective-permute-done.5
  26.0 1.3 %collective-permute-done.3 = bf16[2,2,1,1,128,256]{5,4,3,2,1,0:T(8,128)(2,1)S(1)} collective-permute-done((bf16[2,2,1,1,128,256]{5,4,3,2,1,0:T(8,128)(2,1)S(1)}, bf16[2,2,1,1,128,256]{5,4,3,2,1,0:T(8,128)(2,1)S(1)}, u32[]{:S(2)}, u32[]{:S(2)}) %collective-permute-start.3) | collective-permute-done | bytes 262176 | tf_op jit(solution)/shard_map/ppermute | solution.py:33
  27.3 0.0 copy-done.1
  27.3 0.1 maximum_maximum_fusion
  27.4 0.0 copy-start.2
  27.4 0.0 copy-start.3
  27.4 0.4 convolution_bitcast_fusion.1
  27.9 0.1 collective-permute-start.6
  28.0 1.5 %collective-permute-done.6 = f32[2,128,256]{2,1,0:T(8,128)S(1)} collective-permute-done((f32[2,128,256]{2,1,0:T(8,128)S(1)}, f32[2,128,256]{2,1,0:T(8,128)S(1)}, u32[]{:S(2)}, u32[]{:S(2)}) %collective-permute-start.6) | collective-permute-done | bytes 262176 | tf_op jit(solution)/shard_map/ppermute | solution.py:80
  29.5 0.0 copy-done.2
  29.5 0.0 copy-done.3
  29.5 0.3 multiply_convert_fusion
  29.8 0.2 fusion.17
  30.0 0.2 convolution_convert_fusion
  30.3 0.4 collective-permute-start.8
  30.7 2.2 %collective-permute-start.9 = (f32[128,256]{1,0:T(8,128)S(1)}, f32[128,256]{1,0:T(8,128)S(1)}, u32[]{:S(2)}, u32[]{:S(2)}) collective-permute-start(f32[128,256]{1,0:T(8,128)S(1)} %constant_dynamic-slice_fusion), channel_id=1, source_target_pairs={{0,24},{2,26},{4,28},{6,30},{8,16},{10,18},{12,20},{14,22},{16,8},... | collective-permute-start | bytes 393224 | tf_op jit(solution)/shard_map/ppermute | solution.py:65
  32.8 1.0 %collective-permute-start.7 = (f32[128,256]{1,0:T(8,128)S(1)}, f32[128,256]{1,0:T(8,128)S(1)}, u32[]{:S(2)}, u32[]{:S(2)}) collective-permute-start(f32[128,256]{1,0:T(8,128)S(1)} %constant_dynamic-slice_fusion), channel_id=1, source_target_pairs={{0,8},{2,10},{4,12},{6,14},{8,0},{10,2},{12,4},{14,6},{16,24},{18,... | collective-permute-start | bytes 393224 | tf_op jit(solution)/shard_map/ppermute | solution.py:63
  33.8 0.5 convolution_bitcast_fusion
  34.4 0.1 fusion.4
  34.4 0.1 copy_bitcast_fusion
  34.6 1.7 %collective-permute-start.14 = (bf16[2,2,128,256]{3,2,1,0:T(8,128)(2,1)S(1)}, bf16[2,2,128,256]{3,2,1,0:T(8,128)(2,1)S(1)}, u32[]{:S(2)}, u32[]{:S(2)}) collective-permute-start(bf16[2,2,128,256]{3,2,1,0:T(8,128)(2,1)S(1)} %fusion.6), channel_id=1, source_target_pairs={{0,2},{2,0},{4,6},{6,4},{8,10},{10,8},{12,14},{14,12},{16,18},{18,... | collective-permute-start | bytes 786440 | tf_op jit(solution)/shard_map/ppermute | solution.py:53
  36.3 1.5 %collective-permute-start.15 = (bf16[2,2,128,256]{3,2,1,0:T(8,128)(2,1)S(1)}, bf16[2,2,128,256]{3,2,1,0:T(8,128)(2,1)S(1)}, u32[]{:S(2)}, u32[]{:S(2)}) collective-permute-start(bf16[2,2,128,256]{3,2,1,0:T(8,128)(2,1)S(1)} %get-tuple-element.5), channel_id=1, source_target_pairs={{0,4},{2,6},{4,0},{6,2},{8,12},{10,14},{12,8},{14,10},{16,20},{18,... | collective-permute-start | bytes 786440 | tf_op jit(solution)/shard_map/ppermute | solution.py:54
  37.8 4.2 %collective-permute-done.8 = f32[128,256]{1,0:T(8,128)S(1)} collective-permute-done((f32[128,256]{1,0:T(8,128)S(1)}, f32[128,256]{1,0:T(8,128)S(1)}, u32[]{:S(2)}, u32[]{:S(2)}) %collective-permute-start.8) | collective-permute-done | bytes 131104 | tf_op jit(solution)/shard_map/ppermute | solution.py:64
  42.1 2.4 %collective-permute-start.16 = (bf16[2,2,128,256]{3,2,1,0:T(8,128)(2,1)S(1)}, bf16[2,2,128,256]{3,2,1,0:T(8,128)(2,1)S(1)}, u32[]{:S(2)}, u32[]{:S(2)}) collective-permute-start(bf16[2,2,128,256]{3,2,1,0:T(8,128)(2,1)S(1)} %get-tuple-element.6), channel_id=1, source_target_pairs={{0,6},{2,4},{4,2},{6,0},{8,14},{10,12},{12,10},{14,8},{16,22},{18,... | collective-permute-start | bytes 786440 | tf_op jit(solution)/shard_map/ppermute | solution.py:55
  44.5 0.6 %fusion.9 = bf16[128,256]{1,0:T(8,128)(2,1)} fusion(f32[256,256]{1,0:T(8,128)S(1)} %get-tuple-element.11, s32[]{:T(128)S(6)} %select_n.16, f32[256,256]{1,0:T(8,128)S(1)} %get-tuple-element.12), kind=kLoop, calls=%fused_computation.26 | loop fusion | flops 65536 | bytes 327684 | tf_op jit(solution)/shard_map/convert_element_type | solution.py:123
  45.1 0.0 collective-permute-done.9
  45.1 0.0 collective-permute-done.7
  45.2 0.7 %collective-permute-start.12 = (f32[128,256]{1,0:T(8,128)S(1)}, f32[128,256]{1,0:T(8,128)S(1)}, u32[]{:S(2)}, u32[]{:S(2)}) collective-permute-start(f32[128,256]{1,0:T(8,128)S(1)} %add_add_fusion), channel_id=1, source_target_pairs={{0,6},{2,4},{4,2},{6,0},{8,14},{10,12},{12,10},{14,8},{16,22},{18,... | collective-permute-start | bytes 393224 | tf_op jit(solution)/shard_map/ppermute | solution.py:65
  45.9 1.4 %collective-permute-start.11 = (f32[128,256]{1,0:T(8,128)S(1)}, f32[128,256]{1,0:T(8,128)S(1)}, u32[]{:S(2)}, u32[]{:S(2)}) collective-permute-start(f32[128,256]{1,0:T(8,128)S(1)} %add_add_fusion), channel_id=1, source_target_pairs={{0,4},{2,6},{4,0},{6,2},{8,12},{10,14},{12,8},{14,10},{16,20},{18,... | collective-permute-start | bytes 393224 | tf_op jit(solution)/shard_map/ppermute | solution.py:64
  47.3 0.0 collective-permute-done.14
  47.3 1.5 %collective-permute-start.10 = (f32[128,256]{1,0:T(8,128)S(1)}, f32[128,256]{1,0:T(8,128)S(1)}, u32[]{:S(2)}, u32[]{:S(2)}) collective-permute-start(f32[128,256]{1,0:T(8,128)S(1)} %add_add_fusion), channel_id=1, source_target_pairs={{0,2},{2,0},{4,6},{6,4},{8,10},{10,8},{12,14},{14,12},{16,18},{18,... | collective-permute-start | bytes 393224 | tf_op jit(solution)/shard_map/ppermute | solution.py:63
  48.8 0.0 collective-permute-done.15
  48.8 3.5 %collective-permute-done.16 = bf16[2,2,128,256]{3,2,1,0:T(8,128)(2,1)S(1)} collective-permute-done((bf16[2,2,128,256]{3,2,1,0:T(8,128)(2,1)S(1)}, bf16[2,2,128,256]{3,2,1,0:T(8,128)(2,1)S(1)}, u32[]{:S(2)}, u32[]{:S(2)}) %collective-permute-start.16) | collective-permute-done | bytes 262176 | tf_op jit(solution)/shard_map/ppermute | solution.py:55
  52.2 0.1 fusion.15
  52.4 0.1 collective-permute-start.17
  52.5 1.7 %collective-permute-start.19 = (bf16[128,256]{1,0:T(8,128)(2,1)S(1)}, bf16[128,256]{1,0:T(8,128)(2,1)S(1)}, u32[]{:S(2)}, u32[]{:S(2)}) collective-permute-start(bf16[128,256]{1,0:T(8,128)(2,1)S(1)} %get-tuple-element.8), channel_id=1, source_target_pairs={{0,24},{2,26},{4,28},{6,30},{8,16},{10,18},{12,20},{14,22},{16,8},... | collective-permute-start | bytes 196616 | tf_op jit(solution)/shard_map/ppermute | solution.py:55
  54.2 0.8 %collective-permute-done.12 = f32[128,256]{1,0:T(8,128)S(1)} collective-permute-done((f32[128,256]{1,0:T(8,128)S(1)}, f32[128,256]{1,0:T(8,128)S(1)}, u32[]{:S(2)}, u32[]{:S(2)}) %collective-permute-start.12) | collective-permute-done | bytes 131104 | tf_op jit(solution)/shard_map/ppermute | solution.py:65
  55.0 0.9 %collective-permute-start.18 = (bf16[128,256]{1,0:T(8,128)(2,1)S(1)}, bf16[128,256]{1,0:T(8,128)(2,1)S(1)}, u32[]{:S(2)}, u32[]{:S(2)}) collective-permute-start(bf16[128,256]{1,0:T(8,128)(2,1)S(1)} %get-tuple-element.9), channel_id=1, source_target_pairs={{0,16},{2,18},{4,20},{6,22},{8,24},{10,26},{12,28},{14,30},{16,0},... | collective-permute-start | bytes 196616 | tf_op jit(solution)/shard_map/ppermute | solution.py:54
  55.9 0.8 %collective-permute-done.11 = f32[128,256]{1,0:T(8,128)S(1)} collective-permute-done((f32[128,256]{1,0:T(8,128)S(1)}, f32[128,256]{1,0:T(8,128)S(1)}, u32[]{:S(2)}, u32[]{:S(2)}) %collective-permute-start.11) | collective-permute-done | bytes 131104 | tf_op jit(solution)/shard_map/ppermute | solution.py:64
  56.7 0.1 collective-permute-done.10
  56.9 0.1 collective-permute-start.13
  57.0 0.0 collective-permute-done.17
  57.0 1.7 %collective-permute-done.19 = bf16[128,256]{1,0:T(8,128)(2,1)S(1)} collective-permute-done((bf16[128,256]{1,0:T(8,128)(2,1)S(1)}, bf16[128,256]{1,0:T(8,128)(2,1)S(1)}, u32[]{:S(2)}, u32[]{:S(2)}) %collective-permute-start.19) | collective-permute-done | bytes 65568 | tf_op jit(solution)/shard_map/ppermute | solution.py:55
  58.7 1.9 %collective-permute-done.18 = bf16[128,256]{1,0:T(8,128)(2,1)S(1)} collective-permute-done((bf16[128,256]{1,0:T(8,128)(2,1)S(1)}, bf16[128,256]{1,0:T(8,128)(2,1)S(1)}, u32[]{:S(2)}, u32[]{:S(2)}) %collective-permute-start.18) | collective-permute-done | bytes 65568 | tf_op jit(solution)/shard_map/ppermute | solution.py:54
  60.6 0.7 %fusion.8 = bf16[128,256]{1,0:T(8,128)(2,1)} fusion(f32[2,2,128,256]{3,2,1,0:T(8,128)S(1)} %get-tuple-element.4, bf16[128,256]{1,0:T(8,128)(2,1)S(1)} %collective-permute-done.19, bf16[128,256]{1,0:T(8,128)(2,1)S(1)} %collective-permute-done.18, bf16[128,256]{1,0:T(8,128)(2,1)S(1)} %collective-permute-done.17), kind=kLoop, calls=%fused_computation.24 | loop fusion | flops 229376 | bytes 393216 | tf_op jit(solution)/shard_map/convert_element_type | solution.py:142
  61.2 0.0 collective-permute-done.13
  61.2 0.7 %maximum_select_fusion = f32[2,128,256]{2,1,0:T(8,128)} fusion(f32[1,128,256]{2,1,0:T(8,128)S(1)} %collective-permute-done.13, f32[1,128,256]{2,1,0:T(8,128)S(1)} %add_bitcast_fusion, pred[]{:T(512)S(6)} %eq.19), kind=kLoop, calls=%fused_computation.18 | loop fusion | flops 196608 | bytes 524289 | tf_op jit(solution)/shard_map/jit(_where)/select_n | solution.py:90
  (7 shorter events, 0.2 us)
Async XLA Ops:
  0.6 15.4 %copy-start = (bf16[2,1,16,128,128]{4,3,2,1,0:T(8,128)(2,1)S(1)}, bf16[2,1,16,128,128]{4,3,2,1,0:T(8,128)(2,1)}, u32[]{:S(2)}) copy-start(bf16[2,1,16,128,128]{4,3,2,1,0:T(8,128)(2,1)} %param.9) | copy-start | bytes 3145732
  0.6 26.6 %copy-start.1 = (bf16[128,256]{1,0:T(8,128)(2,1)S(1)}, bf16[128,256]{1,0:T(8,128)(2,1)}, u32[]{:S(2)}) copy-start(bf16[128,256]{1,0:T(8,128)(2,1)} %param.6) | copy-start | bytes 196612
  0.7 7.9 %collective-permute-start.2 = (bf16[1,1,1,1,128,256]{5,4,3,2,1,0:T(8,128)(2,1)}, bf16[1,1,1,1,128,256]{5,4,3,2,1,0:T(8,128)(2,1)S(1)}, u32[]{:S(2)}, u32[]{:S(2)}) collective-permute-start(bf16[1,1,1,1,128,256]{5,4,3,2,1,0:T(8,128)(2,1)} %bitcast.74), channel_id=1, source_target_pairs={{0,24},{2,26},{4,28},{6,30},{8,16},{10,18},{12,20},{14,22},{16,8},... | collective-permute-start | bytes 196616 | tf_op jit(solution)/shard_map/ppermute | solution.py:35
  5.8 5.8 %collective-permute-start.1 = (bf16[1,1,1,1,128,256]{5,4,3,2,1,0:T(8,128)(2,1)}, bf16[1,1,1,1,128,256]{5,4,3,2,1,0:T(8,128)(2,1)S(1)}, u32[]{:S(2)}, u32[]{:S(2)}) collective-permute-start(bf16[1,1,1,1,128,256]{5,4,3,2,1,0:T(8,128)(2,1)} %bitcast.75), channel_id=1, source_target_pairs={{0,16},{2,18},{4,20},{6,22},{8,24},{10,26},{12,28},{14,30},{16,0},... | collective-permute-start | bytes 196616 | tf_op jit(solution)/shard_map/ppermute | solution.py:34
  5.8 5.8 %collective-permute-start = (bf16[1,1,1,1,128,256]{5,4,3,2,1,0:T(8,128)(2,1)}, bf16[1,1,1,1,128,256]{5,4,3,2,1,0:T(8,128)(2,1)S(1)}, u32[]{:S(2)}, u32[]{:S(2)}) collective-permute-start(bf16[1,1,1,1,128,256]{5,4,3,2,1,0:T(8,128)(2,1)} %bitcast.76), channel_id=1, source_target_pairs={{0,8},{2,10},{4,12},{6,14},{8,0},{10,2},{12,4},{14,6},{16,24},{18,... | collective-permute-start | bytes 196616 | tf_op jit(solution)/shard_map/ppermute | solution.py:33
  12.5 13.6 %collective-permute-start.4 = (bf16[2,2,1,1,128,256]{5,4,3,2,1,0:T(8,128)(2,1)S(1)}, bf16[2,2,1,1,128,256]{5,4,3,2,1,0:T(8,128)(2,1)S(1)}, u32[]{:S(2)}, u32[]{:S(2)}) collective-permute-start(bf16[2,2,1,1,128,256]{5,4,3,2,1,0:T(8,128)(2,1)S(1)} %maximum_maximum_fusion.1), channel_id=1, source_target_pairs={{0,4},{2,6},{4,0},{6,2},{8,12},{10,14},{12,8},{14,10},{16,20},{18,... | collective-permute-start | bytes 786440 | tf_op jit(solution)/shard_map/ppermute | solution.py:34
  14.0 12.0 %collective-permute-start.5 = (bf16[2,2,1,1,128,256]{5,4,3,2,1,0:T(8,128)(2,1)S(1)}, bf16[2,2,1,1,128,256]{5,4,3,2,1,0:T(8,128)(2,1)S(1)}, u32[]{:S(2)}, u32[]{:S(2)}) collective-permute-start(bf16[2,2,1,1,128,256]{5,4,3,2,1,0:T(8,128)(2,1)S(1)} %maximum_maximum_fusion.1), channel_id=1, source_target_pairs={{0,6},{2,4},{4,2},{6,0},{8,14},{10,12},{12,10},{14,8},{16,22},{18,... | collective-permute-start | bytes 786440 | tf_op jit(solution)/shard_map/ppermute | solution.py:35
  15.5 11.8 %collective-permute-start.3 = (bf16[2,2,1,1,128,256]{5,4,3,2,1,0:T(8,128)(2,1)S(1)}, bf16[2,2,1,1,128,256]{5,4,3,2,1,0:T(8,128)(2,1)S(1)}, u32[]{:S(2)}, u32[]{:S(2)}) collective-permute-start(bf16[2,2,1,1,128,256]{5,4,3,2,1,0:T(8,128)(2,1)S(1)} %maximum_maximum_fusion.1), channel_id=1, source_target_pairs={{0,2},{2,0},{4,6},{6,4},{8,10},{10,8},{12,14},{14,12},{16,18},{18,... | collective-permute-start | bytes 786440 | tf_op jit(solution)/shard_map/ppermute | solution.py:33
  27.4 2.1 %copy-start.2 = (bf16[256,256]{1,0:T(8,128)(2,1)S(1)}, bf16[256,256]{1,0:T(8,128)(2,1)}, u32[]{:S(2)}) copy-start(bf16[256,256]{1,0:T(8,128)(2,1)} %param.8) | copy-start | bytes 393220
  27.4 2.1 %copy-start.3 = (bf16[256,256]{1,0:T(8,128)(2,1)S(1)}, bf16[256,256]{1,0:T(8,128)(2,1)}, u32[]{:S(2)}) copy-start(bf16[256,256]{1,0:T(8,128)(2,1)} %param.7) | copy-start | bytes 393220
  27.9 1.6 %collective-permute-start.6 = (f32[2,128,256]{2,1,0:T(8,128)S(1)}, f32[2,128,256]{2,1,0:T(8,128)S(1)}, u32[]{:S(2)}, u32[]{:S(2)}) collective-permute-start(f32[2,128,256]{2,1,0:T(8,128)S(1)} %convolution_bitcast_fusion.1), channel_id=1, source_target_pairs={{0,1},{1,0},{2,3},{3,2},{4,5},{5,4},{6,7},{7,6},{8,9},{9,8},{10,11... | collective-permute-start | bytes 786440 | tf_op jit(solution)/shard_map/ppermute | solution.py:80
  30.3 11.8 %collective-permute-start.8 = (f32[128,256]{1,0:T(8,128)S(1)}, f32[128,256]{1,0:T(8,128)S(1)}, u32[]{:S(2)}, u32[]{:S(2)}) collective-permute-start(f32[128,256]{1,0:T(8,128)S(1)} %constant_dynamic-slice_fusion), channel_id=1, source_target_pairs={{0,16},{2,18},{4,20},{6,22},{8,24},{10,26},{12,28},{14,30},{16,0},... | collective-permute-start | bytes 393224 | tf_op jit(solution)/shard_map/ppermute | solution.py:64
  30.7 14.5 %collective-permute-start.9 = (f32[128,256]{1,0:T(8,128)S(1)}, f32[128,256]{1,0:T(8,128)S(1)}, u32[]{:S(2)}, u32[]{:S(2)}) collective-permute-start(f32[128,256]{1,0:T(8,128)S(1)} %constant_dynamic-slice_fusion), channel_id=1, source_target_pairs={{0,24},{2,26},{4,28},{6,30},{8,16},{10,18},{12,20},{14,22},{16,8},... | collective-permute-start | bytes 393224 | tf_op jit(solution)/shard_map/ppermute | solution.py:65
  32.8 12.3 %collective-permute-start.7 = (f32[128,256]{1,0:T(8,128)S(1)}, f32[128,256]{1,0:T(8,128)S(1)}, u32[]{:S(2)}, u32[]{:S(2)}) collective-permute-start(f32[128,256]{1,0:T(8,128)S(1)} %constant_dynamic-slice_fusion), channel_id=1, source_target_pairs={{0,8},{2,10},{4,12},{6,14},{8,0},{10,2},{12,4},{14,6},{16,24},{18,... | collective-permute-start | bytes 393224 | tf_op jit(solution)/shard_map/ppermute | solution.py:63
  34.6 12.7 %collective-permute-start.14 = (bf16[2,2,128,256]{3,2,1,0:T(8,128)(2,1)S(1)}, bf16[2,2,128,256]{3,2,1,0:T(8,128)(2,1)S(1)}, u32[]{:S(2)}, u32[]{:S(2)}) collective-permute-start(bf16[2,2,128,256]{3,2,1,0:T(8,128)(2,1)S(1)} %fusion.6), channel_id=1, source_target_pairs={{0,2},{2,0},{4,6},{6,4},{8,10},{10,8},{12,14},{14,12},{16,18},{18,... | collective-permute-start | bytes 786440 | tf_op jit(solution)/shard_map/ppermute | solution.py:53
  36.3 12.5 %collective-permute-start.15 = (bf16[2,2,128,256]{3,2,1,0:T(8,128)(2,1)S(1)}, bf16[2,2,128,256]{3,2,1,0:T(8,128)(2,1)S(1)}, u32[]{:S(2)}, u32[]{:S(2)}) collective-permute-start(bf16[2,2,128,256]{3,2,1,0:T(8,128)(2,1)S(1)} %get-tuple-element.5), channel_id=1, source_target_pairs={{0,4},{2,6},{4,0},{6,2},{8,12},{10,14},{12,8},{14,10},{16,20},{18,... | collective-permute-start | bytes 786440 | tf_op jit(solution)/shard_map/ppermute | solution.py:54
  42.1 10.2 %collective-permute-start.16 = (bf16[2,2,128,256]{3,2,1,0:T(8,128)(2,1)S(1)}, bf16[2,2,128,256]{3,2,1,0:T(8,128)(2,1)S(1)}, u32[]{:S(2)}, u32[]{:S(2)}) collective-permute-start(bf16[2,2,128,256]{3,2,1,0:T(8,128)(2,1)S(1)} %get-tuple-element.6), channel_id=1, source_target_pairs={{0,6},{2,4},{4,2},{6,0},{8,14},{10,12},{12,10},{14,8},{16,22},{18,... | collective-permute-start | bytes 786440 | tf_op jit(solution)/shard_map/ppermute | solution.py:55
  45.2 9.8 %collective-permute-start.12 = (f32[128,256]{1,0:T(8,128)S(1)}, f32[128,256]{1,0:T(8,128)S(1)}, u32[]{:S(2)}, u32[]{:S(2)}) collective-permute-start(f32[128,256]{1,0:T(8,128)S(1)} %add_add_fusion), channel_id=1, source_target_pairs={{0,6},{2,4},{4,2},{6,0},{8,14},{10,12},{12,10},{14,8},{16,22},{18,... | collective-permute-start | bytes 393224 | tf_op jit(solution)/shard_map/ppermute | solution.py:65
  45.9 10.9 %collective-permute-start.11 = (f32[128,256]{1,0:T(8,128)S(1)}, f32[128,256]{1,0:T(8,128)S(1)}, u32[]{:S(2)}, u32[]{:S(2)}) collective-permute-start(f32[128,256]{1,0:T(8,128)S(1)} %add_add_fusion), channel_id=1, source_target_pairs={{0,4},{2,6},{4,0},{6,2},{8,12},{10,14},{12,8},{14,10},{16,20},{18,... | collective-permute-start | bytes 393224 | tf_op jit(solution)/shard_map/ppermute | solution.py:64
  47.3 9.6 %collective-permute-start.10 = (f32[128,256]{1,0:T(8,128)S(1)}, f32[128,256]{1,0:T(8,128)S(1)}, u32[]{:S(2)}, u32[]{:S(2)}) collective-permute-start(f32[128,256]{1,0:T(8,128)S(1)} %add_add_fusion), channel_id=1, source_target_pairs={{0,2},{2,0},{4,6},{6,4},{8,10},{10,8},{12,14},{14,12},{16,18},{18,... | collective-permute-start | bytes 393224 | tf_op jit(solution)/shard_map/ppermute | solution.py:63
  52.4 4.6 %collective-permute-start.17 = (bf16[128,256]{1,0:T(8,128)(2,1)S(1)}, bf16[128,256]{1,0:T(8,128)(2,1)S(1)}, u32[]{:S(2)}, u32[]{:S(2)}) collective-permute-start(bf16[128,256]{1,0:T(8,128)(2,1)S(1)} %get-tuple-element.7), channel_id=1, source_target_pairs={{0,8},{2,10},{4,12},{6,14},{8,0},{10,2},{12,4},{14,6},{16,24},{18,... | collective-permute-start | bytes 196616 | tf_op jit(solution)/shard_map/ppermute | solution.py:53
  52.5 6.2 %collective-permute-start.19 = (bf16[128,256]{1,0:T(8,128)(2,1)S(1)}, bf16[128,256]{1,0:T(8,128)(2,1)S(1)}, u32[]{:S(2)}, u32[]{:S(2)}) collective-permute-start(bf16[128,256]{1,0:T(8,128)(2,1)S(1)} %get-tuple-element.8), channel_id=1, source_target_pairs={{0,24},{2,26},{4,28},{6,30},{8,16},{10,18},{12,20},{14,22},{16,8},... | collective-permute-start | bytes 196616 | tf_op jit(solution)/shard_map/ppermute | solution.py:55
  55.0 5.6 %collective-permute-start.18 = (bf16[128,256]{1,0:T(8,128)(2,1)S(1)}, bf16[128,256]{1,0:T(8,128)(2,1)S(1)}, u32[]{:S(2)}, u32[]{:S(2)}) collective-permute-start(bf16[128,256]{1,0:T(8,128)(2,1)S(1)} %get-tuple-element.9), channel_id=1, source_target_pairs={{0,16},{2,18},{4,20},{6,22},{8,24},{10,26},{12,28},{14,30},{16,0},... | collective-permute-start | bytes 196616 | tf_op jit(solution)/shard_map/ppermute | solution.py:54
  56.9 4.3 %collective-permute-start.13 = (f32[1,128,256]{2,1,0:T(8,128)S(1)}, f32[1,128,256]{2,1,0:T(8,128)S(1)}, u32[]{:S(2)}, u32[]{:S(2)}) collective-permute-start(f32[1,128,256]{2,1,0:T(8,128)S(1)} %add_bitcast_fusion), channel_id=1, source_target_pairs={{0,1},{1,0},{2,3},{3,2},{4,5},{5,4},{6,7},{7,6},{8,9},{9,8},{10,11... | collective-permute-start | bytes 393224 | tf_op jit(solution)/shard_map/ppermute | solution.py:88

commit v7 on v6

--- a/solution.py
+++ b/solution.py
@@ -67,11 +67,16 @@
 
 
 def paired_backward(rel, w, n, send_dtype):
-    rounds = bit_rounds(bit_count(n))
+    nb = bit_count(n)
     cur = rel
-    for k, bits in enumerate(rounds[::-1]):
-        cur = scatter_round(cur, bits, n, send_dtype)
-        w = sum_round(w, rounds[k], n)
+    if nb == 4:
+        pairs = [((0, 1), (3,)), ((2,), (2,)), ((3,), (0, 1))]
+    else:
+        rounds = bit_rounds(nb)
+        pairs = list(zip(rounds[::-1], rounds))
+    for fg_bits, w_bits in pairs:
+        cur = scatter_round(cur, fg_bits, n, send_dtype)
+        w = sum_round(w, w_bits, n)
     return cur, w
 
 

time: 62.1 us -> 60.2 us (0.969)
  starting transfers between devices: 25 us -> 20.5 us
  waiting for transfers between devices: 28.8 us -> 31.3 us
    ppermute x0 -> x4, waiting for transfers between devices: none -> 6.51 us  [the longest x2 4.85 us: sum_round(): return w + lax.ppermute(w, 'rows', pairs_of(n, 1 << bits[0]))]
    ppermute x2 -> x1, waiting for transfers between devices: 5.19 us -> 0.01 us  [scatter_round(): lax.ppermute(part(1, 1).astype(send_dtype), 'rows', pairs_of(n, 1 << low...]
    ppermute x2 -> x1, waiting for transfers between devices: 1.87 us -> 5.86 us  [scatter_round(): lax.ppermute(part(1, 0).astype(send_dtype), 'rows', pairs_of(n, 1 << high))]
    ppermute x0 -> x4, starting transfers between devices: none -> 3.93 us  [the longest x2 3.5 us: scatter_round(): lax.ppermute(send.astype(send_dtype), 'rows', pairs_of(n, 1 << bits[0]))]
    ppermute x2 -> x1, waiting for transfers between devices: 5.04 us -> 1.27 us  [sum_round(): got_high = lax.ppermute(w, 'rows', pairs_of(n, 1 << high))]
    ppermute x2 -> x1, starting transfers between devices: 4.19 us -> 0.48 us  [scatter_round(): lax.ppermute(part(1, 1).astype(send_dtype), 'rows', pairs_of(n, 1 << low...]
    ppermute x2 -> x1, starting transfers between devices: 2.53 us -> 0.8 us  [sum_round(): got_low = lax.ppermute(w, 'rows', pairs_of(n, 1 << low))]
    ppermute x2 -> x1, starting transfers between devices: 2.83 us -> 1.56 us  [sum_round(): got_both = lax.ppermute(w, 'rows', pairs_of(n, 1 << low | 1 << high))]
  transfers between devices with their start and end apart: 20 -> 18, of which waited for: 12 -> 12; matrix products, arithmetic and copies ran while one was open for 7% -> 6% of each run, Pallas kernels for 0% -> 0%
where the time goes in v7:
time: 60.2 us; the launch traced here: 60 us
  waiting for transfers between devices  31.3 us (52%)
  starting transfers between devices  20.5 us (34%)
  other arithmetic  4.62 us (8%)
  matrix products  2.43 us (4%)
  between operations  0.85 us (1%)
    ppermute x2, waiting for transfers between devices, radix_gather(): got_high = lax.ppermute(held, 'rows', pairs_of(n, 1 << high))  12.2 us
    ppermute x2, starting transfers between devices, radix_gather(): got_both = lax.ppermute(held, 'rows', pairs_of(n, 1 << low | 1 << high))  6.55 us
    ppermute x1, waiting for transfers between devices, scatter_round(): lax.ppermute(part(1, 0).astype(send_dtype), 'rows', pairs_of(n, 1 << high))  5.86 us
    ppermute x2, waiting for transfers between devices, sum_round(): return w + lax.ppermute(w, 'rows', pairs_of(n, 1 << bits[0]))  4.85 us
    ppermute x2, starting transfers between devices, scatter_round(): lax.ppermute(send.astype(send_dtype), 'rows', pairs_of(n, 1 << bits[0]))  3.5 us
    ppermute x2, waiting for transfers between devices, scatter_round(): lax.ppermute(send.astype(send_dtype), 'rows', pairs_of(n, 1 << bits[0]))  1.67 us
    ppermute x2, starting transfers between devices, radix_gather(): got_high = lax.ppermute(held, 'rows', pairs_of(n, 1 << high))  1.59 us
    ppermute x1, starting transfers between devices, sum_round(): got_both = lax.ppermute(w, 'rows', pairs_of(n, 1 << low | 1 << high))  1.56 us
  transfers between devices with their start and end apart: 18, of which 12 were waited for; matrix products, arithmetic and copies ran while one was open for 6% of the time, Pallas kernels for 0%

profile of v7, /device:TPU:0, one launch (start us, length us, event | category | flops | bytes accessed | tf_op | source)
XLA Modules:
  0.0 60.0 jit_solution(2765162643491267160)
XLA Ops:
  0.6 0.0 copy-start
  0.6 0.0 copy-start.1
  0.7 5.1 %collective-permute-start.2 = (bf16[1,1,1,1,128,256]{5,4,3,2,1,0:T(8,128)(2,1)}, bf16[1,1,1,1,128,256]{5,4,3,2,1,0:T(8,128)(2,1)S(1)}, u32[]{:S(2)}, u32[]{:S(2)}) collective-permute-start(bf16[1,1,1,1,128,256]{5,4,3,2,1,0:T(8,128)(2,1)} %bitcast.77), channel_id=1, source_target_pairs={{0,24},{2,26},{4,28},{6,30},{8,16},{10,18},{12,20},{14,22},{16,8},... | collective-permute-start | bytes 196616 | tf_op jit(solution)/shard_map/ppermute | solution.py:35
  5.8 0.0 collective-permute-start.1
  5.8 0.6 %collective-permute-start = (bf16[1,1,1,1,128,256]{5,4,3,2,1,0:T(8,128)(2,1)}, bf16[1,1,1,1,128,256]{5,4,3,2,1,0:T(8,128)(2,1)S(1)}, u32[]{:S(2)}, u32[]{:S(2)}) collective-permute-start(bf16[1,1,1,1,128,256]{5,4,3,2,1,0:T(8,128)(2,1)} %bitcast.79), channel_id=1, source_target_pairs={{0,8},{2,10},{4,12},{6,14},{8,0},{10,2},{12,4},{14,6},{16,24},{18,... | collective-permute-start | bytes 196616 | tf_op jit(solution)/shard_map/ppermute | solution.py:33
  6.4 0.7 %broadcast_xor_fusion = s32[2,1,16]{2,1,0:T(1,128)S(1)} fusion(s32[2,1,16]{2,1,0:T(1,128)} %param.10, s32[]{:T(128)S(6)} %axis_index.27), kind=kLoop, calls=%fused_computation.41 | loop fusion | flops 32 | bytes 260 | tf_op jit(solution)/shard_map/xor | solution.py:116
  7.1 0.7 %iota_compare_fusion.1 = pred[2,16]{1,0:T(4,128)(4,1)S(1)} fusion(s32[2]{0:T(128)} %bitcast.83), kind=kLoop, calls=%fused_computation.39 | loop fusion | flops 32 | bytes 40 | tf_op jit(solution)/shard_map/lt | solution.py:115
  7.8 0.8 %collective-permute-done.2 = bf16[1,1,1,1,128,256]{5,4,3,2,1,0:T(8,128)(2,1)S(1)} collective-permute-done((bf16[1,1,1,1,128,256]{5,4,3,2,1,0:T(8,128)(2,1)}, bf16[1,1,1,1,128,256]{5,4,3,2,1,0:T(8,128)(2,1)S(1)}, u32[]{:S(2)}, u32[]{:S(2)}) %collective-permute-start.2) | collective-permute-done | bytes 65568 | tf_op jit(solution)/shard_map/ppermute | solution.py:35
  8.6 3.0 %collective-permute-done.1 = bf16[1,1,1,1,128,256]{5,4,3,2,1,0:T(8,128)(2,1)S(1)} collective-permute-done((bf16[1,1,1,1,128,256]{5,4,3,2,1,0:T(8,128)(2,1)}, bf16[1,1,1,1,128,256]{5,4,3,2,1,0:T(8,128)(2,1)S(1)}, u32[]{:S(2)}, u32[]{:S(2)}) %collective-permute-start.1) | collective-permute-done | bytes 65568 | tf_op jit(solution)/shard_map/ppermute | solution.py:34
  11.6 0.0 collective-permute-done
  11.6 0.9 %maximum_maximum_fusion.1 = bf16[2,2,1,1,128,256]{5,4,3,2,1,0:T(8,128)(2,1)S(1)} fusion(bf16[1,1,1,1,128,256]{5,4,3,2,1,0:T(8,128)(2,1)S(1)} %collective-permute-done.2, bf16[1,1,1,1,128,256]{5,4,3,2,1,0:T(8,128)(2,1)S(1)} %collective-permute-done.1, bf16[1,1,1,1,128,256]{5,4,3,2,1,0:T(8,128)(2,1)S(1)} %collective-permute-done, ...), kind=kLoop, calls=%fused_computation.20 | loop fusion | flops 393216 | bytes 524288 | tf_op jit(solution)/shard_map/concatenate | solution.py:38
  12.5 1.6 %collective-permute-start.4 = (bf16[2,2,1,1,128,256]{5,4,3,2,1,0:T(8,128)(2,1)S(1)}, bf16[2,2,1,1,128,256]{5,4,3,2,1,0:T(8,128)(2,1)S(1)}, u32[]{:S(2)}, u32[]{:S(2)}) collective-permute-start(bf16[2,2,1,1,128,256]{5,4,3,2,1,0:T(8,128)(2,1)S(1)} %maximum_maximum_fusion.1), channel_id=1, source_target_pairs={{0,4},{2,6},{4,0},{6,2},{8,12},{10,14},{12,8},{14,10},{16,20},{18,... | collective-permute-start | bytes 786440 | tf_op jit(solution)/shard_map/ppermute | solution.py:34
  14.0 1.4 %collective-permute-start.5 = (bf16[2,2,1,1,128,256]{5,4,3,2,1,0:T(8,128)(2,1)S(1)}, bf16[2,2,1,1,128,256]{5,4,3,2,1,0:T(8,128)(2,1)S(1)}, u32[]{:S(2)}, u32[]{:S(2)}) collective-permute-start(bf16[2,2,1,1,128,256]{5,4,3,2,1,0:T(8,128)(2,1)S(1)} %maximum_maximum_fusion.1), channel_id=1, source_target_pairs={{0,6},{2,4},{4,2},{6,0},{8,14},{10,12},{12,10},{14,8},{16,22},{18,... | collective-permute-start | bytes 786440 | tf_op jit(solution)/shard_map/ppermute | solution.py:35
  15.5 0.5 collective-permute-start.3
  16.0 0.0 copy-done
  16.0 0.7 %fusion.2 = bf16[2,16,128,128]{3,1,2,0:T(8,128)(2,1)S(1)} fusion(bf16[2,16,128,128]{3,2,1,0:T(8,128)(2,1)S(1)} %bitcast.70, s32[2,16]{1,0:T(2,128)S(1)} %bitcast.82, pred[2,16]{1,0:T(4,128)(4,1)S(1)} %iota_compare_fusion.1), kind=kOutput, calls=%fused_computation.8 | convolution fusion | flops 16778240 | bytes 2097312 | tf_op jit(solution)/shard_map/tsq,tsab->tqab/dot_general | solution.py:118
  16.8 9.2 %collective-permute-done.4 = bf16[2,2,1,1,128,256]{5,4,3,2,1,0:T(8,128)(2,1)S(1)} collective-permute-done((bf16[2,2,1,1,128,256]{5,4,3,2,1,0:T(8,128)(2,1)S(1)}, bf16[2,2,1,1,128,256]{5,4,3,2,1,0:T(8,128)(2,1)S(1)}, u32[]{:S(2)}, u32[]{:S(2)}) %collective-permute-start.4) | collective-permute-done | bytes 262176 | tf_op jit(solution)/shard_map/ppermute | solution.py:34
  26.0 0.0 collective-permute-done.5
  26.0 1.3 %collective-permute-done.3 = bf16[2,2,1,1,128,256]{5,4,3,2,1,0:T(8,128)(2,1)S(1)} collective-permute-done((bf16[2,2,1,1,128,256]{5,4,3,2,1,0:T(8,128)(2,1)S(1)}, bf16[2,2,1,1,128,256]{5,4,3,2,1,0:T(8,128)(2,1)S(1)}, u32[]{:S(2)}, u32[]{:S(2)}) %collective-permute-start.3) | collective-permute-done | bytes 262176 | tf_op jit(solution)/shard_map/ppermute | solution.py:33
  27.3 0.0 copy-done.1
  27.3 0.1 maximum_maximum_fusion
  27.4 0.0 copy-start.2
  27.4 0.0 copy-start.3
  27.4 0.4 convolution_bitcast_fusion.1
  27.9 0.1 collective-permute-start.6
  28.0 1.5 %collective-permute-done.6 = f32[2,128,256]{2,1,0:T(8,128)S(1)} collective-permute-done((f32[2,128,256]{2,1,0:T(8,128)S(1)}, f32[2,128,256]{2,1,0:T(8,128)S(1)}, u32[]{:S(2)}, u32[]{:S(2)}) %collective-permute-start.6) | collective-permute-done | bytes 262176 | tf_op jit(solution)/shard_map/ppermute | solution.py:85
  29.5 0.0 copy-done.2
  29.5 0.0 copy-done.3
  29.5 0.3 multiply_convert_fusion
  29.8 0.2 fusion.18
  30.0 0.2 convolution_convert_fusion
  30.3 0.5 convolution_bitcast_fusion
  30.8 0.1 fusion.4
  30.9 0.1 copy_bitcast_fusion
  31.0 0.4 collective-permute-start.7
  31.4 1.6 %collective-permute-start.13 = (bf16[2,2,128,256]{3,2,1,0:T(8,128)(2,1)S(1)}, bf16[2,2,128,256]{3,2,1,0:T(8,128)(2,1)S(1)}, u32[]{:S(2)}, u32[]{:S(2)}) collective-permute-start(bf16[2,2,128,256]{3,2,1,0:T(8,128)(2,1)S(1)} %fusion.6), channel_id=1, source_target_pairs={{0,2},{2,0},{4,6},{6,4},{8,10},{10,8},{12,14},{14,12},{16,18},{18,... | collective-permute-start | bytes 786440 | tf_op jit(solution)/shard_map/ppermute | solution.py:53
  33.0 1.5 %collective-permute-start.14 = (bf16[2,2,128,256]{3,2,1,0:T(8,128)(2,1)S(1)}, bf16[2,2,128,256]{3,2,1,0:T(8,128)(2,1)S(1)}, u32[]{:S(2)}, u32[]{:S(2)}) collective-permute-start(bf16[2,2,128,256]{3,2,1,0:T(8,128)(2,1)S(1)} %get-tuple-element.3), channel_id=1, source_target_pairs={{0,4},{2,6},{4,0},{6,2},{8,12},{10,14},{12,8},{14,10},{16,20},{18,... | collective-permute-start | bytes 786440 | tf_op jit(solution)/shard_map/ppermute | solution.py:54
  34.5 0.5 collective-permute-start.15
  35.0 4.8 %collective-permute-done.7 = f32[128,256]{1,0:T(8,128)S(1)} collective-permute-done((f32[128,256]{1,0:T(8,128)S(1)}, f32[128,256]{1,0:T(8,128)S(1)}, u32[]{:S(2)}, u32[]{:S(2)}) %collective-permute-start.7) | collective-permute-done | bytes 131104 | tf_op jit(solution)/shard_map/ppermute | solution.py:61
  39.8 0.1 collective-permute-start.8
  39.9 0.8 %collective-permute-done.13 = bf16[2,2,128,256]{3,2,1,0:T(8,128)(2,1)S(1)} collective-permute-done((bf16[2,2,128,256]{3,2,1,0:T(8,128)(2,1)S(1)}, bf16[2,2,128,256]{3,2,1,0:T(8,128)(2,1)S(1)}, u32[]{:S(2)}, u32[]{:S(2)}) %collective-permute-start.13) | collective-permute-done | bytes 262176 | tf_op jit(solution)/shard_map/ppermute | solution.py:53
  40.7 5.9 %collective-permute-done.14 = bf16[2,2,128,256]{3,2,1,0:T(8,128)(2,1)S(1)} collective-permute-done((bf16[2,2,128,256]{3,2,1,0:T(8,128)(2,1)S(1)}, bf16[2,2,128,256]{3,2,1,0:T(8,128)(2,1)S(1)}, u32[]{:S(2)}, u32[]{:S(2)}) %collective-permute-start.14) | collective-permute-done | bytes 262176 | tf_op jit(solution)/shard_map/ppermute | solution.py:54
  46.5 0.0 collective-permute-done.15
  46.5 0.1 fusion.5
  46.7 1.8 %collective-permute-start.16 = (bf16[2,128,256]{2,1,0:T(8,128)(2,1)S(1)}, bf16[2,128,256]{2,1,0:T(8,128)(2,1)S(1)}, u32[]{:S(2)}, u32[]{:S(2)}) collective-permute-start(bf16[2,128,256]{2,1,0:T(8,128)(2,1)S(1)} %fusion.8), channel_id=1, source_target_pairs={{0,8},{2,10},{4,12},{6,14},{8,0},{10,2},{12,4},{14,6},{16,24},{18,... | collective-permute-start | bytes 393224 | tf_op jit(solution)/shard_map/ppermute | solution.py:47
  48.4 0.6 %fusion.11 = bf16[128,256]{1,0:T(8,128)(2,1)} fusion(f32[256,256]{1,0:T(8,128)S(1)} %get-tuple-element.6, s32[]{:T(128)S(6)} %select_n.16, f32[256,256]{1,0:T(8,128)S(1)} %get-tuple-element.7), kind=kLoop, calls=%fused_computation.31 | loop fusion | flops 65536 | bytes 327684 | tf_op jit(solution)/shard_map/convert_element_type | solution.py:128
  49.1 0.0 collective-permute-done.8
  49.1 1.6 %collective-permute-start.11 = (f32[128,256]{1,0:T(8,128)S(1)}, f32[128,256]{1,0:T(8,128)S(1)}, u32[]{:S(2)}, u32[]{:S(2)}) collective-permute-start(f32[128,256]{1,0:T(8,128)S(1)} %add.48), channel_id=1, source_target_pairs={{0,6},{2,4},{4,2},{6,0},{8,14},{10,12},{12,10},{14,8},{16,22},{18,... | collective-permute-start | bytes 393224 | tf_op jit(solution)/shard_map/ppermute | solution.py:65
  50.6 1.2 %collective-permute-start.10 = (f32[128,256]{1,0:T(8,128)S(1)}, f32[128,256]{1,0:T(8,128)S(1)}, u32[]{:S(2)}, u32[]{:S(2)}) collective-permute-start(f32[128,256]{1,0:T(8,128)S(1)} %add.48), channel_id=1, source_target_pairs={{0,4},{2,6},{4,0},{6,2},{8,12},{10,14},{12,8},{14,10},{16,20},{18,... | collective-permute-start | bytes 393224 | tf_op jit(solution)/shard_map/ppermute | solution.py:64
  51.8 0.8 %collective-permute-start.9 = (f32[128,256]{1,0:T(8,128)S(1)}, f32[128,256]{1,0:T(8,128)S(1)}, u32[]{:S(2)}, u32[]{:S(2)}) collective-permute-start(f32[128,256]{1,0:T(8,128)S(1)} %add.48), channel_id=1, source_target_pairs={{0,2},{2,0},{4,6},{6,4},{8,10},{10,8},{12,14},{14,12},{16,18},{18,... | collective-permute-start | bytes 393224 | tf_op jit(solution)/shard_map/ppermute | solution.py:63
  52.6 0.0 collective-permute-done.16
  52.7 1.7 %collective-permute-start.17 = (bf16[128,256]{1,0:T(8,128)(2,1)S(1)}, bf16[128,256]{1,0:T(8,128)(2,1)S(1)}, u32[]{:S(2)}, u32[]{:S(2)}) collective-permute-start(bf16[128,256]{1,0:T(8,128)(2,1)S(1)} %fusion.12), channel_id=1, source_target_pairs={{0,16},{2,18},{4,20},{6,22},{8,24},{10,26},{12,28},{14,30},{16,0},... | collective-permute-start | bytes 196616 | tf_op jit(solution)/shard_map/ppermute | solution.py:47
  54.4 1.1 %collective-permute-done.11 = f32[128,256]{1,0:T(8,128)S(1)} collective-permute-done((f32[128,256]{1,0:T(8,128)S(1)}, f32[128,256]{1,0:T(8,128)S(1)}, u32[]{:S(2)}, u32[]{:S(2)}) %collective-permute-start.11) | collective-permute-done | bytes 131104 | tf_op jit(solution)/shard_map/ppermute | solution.py:65
  55.5 1.3 %collective-permute-done.10 = f32[128,256]{1,0:T(8,128)S(1)} collective-permute-done((f32[128,256]{1,0:T(8,128)S(1)}, f32[128,256]{1,0:T(8,128)S(1)}, u32[]{:S(2)}, u32[]{:S(2)}) %collective-permute-start.10) | collective-permute-done | bytes 131104 | tf_op jit(solution)/shard_map/ppermute | solution.py:64
  56.7 0.1 collective-permute-done.9
  56.9 0.1 collective-permute-start.12
  57.0 1.7 %collective-permute-done.17 = bf16[128,256]{1,0:T(8,128)(2,1)S(1)} collective-permute-done((bf16[128,256]{1,0:T(8,128)(2,1)S(1)}, bf16[128,256]{1,0:T(8,128)(2,1)S(1)}, u32[]{:S(2)}, u32[]{:S(2)}) %collective-permute-start.17) | collective-permute-done | bytes 65568 | tf_op jit(solution)/shard_map/ppermute | solution.py:47
  58.6 0.6 %fusion.10 = bf16[128,256]{1,0:T(8,128)(2,1)} fusion(f32[2,128,256]{2,1,0:T(8,128)S(1)} %fusion.7, bf16[128,256]{1,0:T(8,128)(2,1)S(1)} %collective-permute-done.17), kind=kLoop, calls=%fused_computation.29 | loop fusion | flops 98304 | bytes 262144 | tf_op jit(solution)/shard_map/convert_element_type | solution.py:147
  59.3 0.0 collective-permute-done.12
  59.3 0.7 %maximum_select_fusion = f32[2,128,256]{2,1,0:T(8,128)} fusion(f32[1,128,256]{2,1,0:T(8,128)S(1)} %collective-permute-done.12, f32[1,128,256]{2,1,0:T(8,128)S(1)} %add_bitcast_fusion, pred[]{:T(512)S(6)} %eq.19), kind=kLoop, calls=%fused_computation.21 | loop fusion | flops 196608 | bytes 524289 | tf_op jit(solution)/shard_map/jit(_where)/select_n | solution.py:95
  (10 shorter events, 0.2 us)
Async XLA Ops:
  0.6 15.4 %copy-start = (bf16[2,1,16,128,128]{4,3,2,1,0:T(8,128)(2,1)S(1)}, bf16[2,1,16,128,128]{4,3,2,1,0:T(8,128)(2,1)}, u32[]{:S(2)}) copy-start(bf16[2,1,16,128,128]{4,3,2,1,0:T(8,128)(2,1)} %param.9) | copy-start | bytes 3145732
  0.6 26.6 %copy-start.1 = (bf16[128,256]{1,0:T(8,128)(2,1)S(1)}, bf16[128,256]{1,0:T(8,128)(2,1)}, u32[]{:S(2)}) copy-start(bf16[128,256]{1,0:T(8,128)(2,1)} %param.6) | copy-start | bytes 196612
  0.7 7.9 %collective-permute-start.2 = (bf16[1,1,1,1,128,256]{5,4,3,2,1,0:T(8,128)(2,1)}, bf16[1,1,1,1,128,256]{5,4,3,2,1,0:T(8,128)(2,1)S(1)}, u32[]{:S(2)}, u32[]{:S(2)}) collective-permute-start(bf16[1,1,1,1,128,256]{5,4,3,2,1,0:T(8,128)(2,1)} %bitcast.77), channel_id=1, source_target_pairs={{0,24},{2,26},{4,28},{6,30},{8,16},{10,18},{12,20},{14,22},{16,8},... | collective-permute-start | bytes 196616 | tf_op jit(solution)/shard_map/ppermute | solution.py:35
  5.8 5.8 %collective-permute-start.1 = (bf16[1,1,1,1,128,256]{5,4,3,2,1,0:T(8,128)(2,1)}, bf16[1,1,1,1,128,256]{5,4,3,2,1,0:T(8,128)(2,1)S(1)}, u32[]{:S(2)}, u32[]{:S(2)}) collective-permute-start(bf16[1,1,1,1,128,256]{5,4,3,2,1,0:T(8,128)(2,1)} %bitcast.78), channel_id=1, source_target_pairs={{0,16},{2,18},{4,20},{6,22},{8,24},{10,26},{12,28},{14,30},{16,0},... | collective-permute-start | bytes 196616 | tf_op jit(solution)/shard_map/ppermute | solution.py:34
  5.8 5.8 %collective-permute-start = (bf16[1,1,1,1,128,256]{5,4,3,2,1,0:T(8,128)(2,1)}, bf16[1,1,1,1,128,256]{5,4,3,2,1,0:T(8,128)(2,1)S(1)}, u32[]{:S(2)}, u32[]{:S(2)}) collective-permute-start(bf16[1,1,1,1,128,256]{5,4,3,2,1,0:T(8,128)(2,1)} %bitcast.79), channel_id=1, source_target_pairs={{0,8},{2,10},{4,12},{6,14},{8,0},{10,2},{12,4},{14,6},{16,24},{18,... | collective-permute-start | bytes 196616 | tf_op jit(solution)/shard_map/ppermute | solution.py:33
  12.5 13.6 %collective-permute-start.4 = (bf16[2,2,1,1,128,256]{5,4,3,2,1,0:T(8,128)(2,1)S(1)}, bf16[2,2,1,1,128,256]{5,4,3,2,1,0:T(8,128)(2,1)S(1)}, u32[]{:S(2)}, u32[]{:S(2)}) collective-permute-start(bf16[2,2,1,1,128,256]{5,4,3,2,1,0:T(8,128)(2,1)S(1)} %maximum_maximum_fusion.1), channel_id=1, source_target_pairs={{0,4},{2,6},{4,0},{6,2},{8,12},{10,14},{12,8},{14,10},{16,20},{18,... | collective-permute-start | bytes 786440 | tf_op jit(solution)/shard_map/ppermute | solution.py:34
  14.0 12.0 %collective-permute-start.5 = (bf16[2,2,1,1,128,256]{5,4,3,2,1,0:T(8,128)(2,1)S(1)}, bf16[2,2,1,1,128,256]{5,4,3,2,1,0:T(8,128)(2,1)S(1)}, u32[]{:S(2)}, u32[]{:S(2)}) collective-permute-start(bf16[2,2,1,1,128,256]{5,4,3,2,1,0:T(8,128)(2,1)S(1)} %maximum_maximum_fusion.1), channel_id=1, source_target_pairs={{0,6},{2,4},{4,2},{6,0},{8,14},{10,12},{12,10},{14,8},{16,22},{18,... | collective-permute-start | bytes 786440 | tf_op jit(solution)/shard_map/ppermute | solution.py:35
  15.5 11.8 %collective-permute-start.3 = (bf16[2,2,1,1,128,256]{5,4,3,2,1,0:T(8,128)(2,1)S(1)}, bf16[2,2,1,1,128,256]{5,4,3,2,1,0:T(8,128)(2,1)S(1)}, u32[]{:S(2)}, u32[]{:S(2)}) collective-permute-start(bf16[2,2,1,1,128,256]{5,4,3,2,1,0:T(8,128)(2,1)S(1)} %maximum_maximum_fusion.1), channel_id=1, source_target_pairs={{0,2},{2,0},{4,6},{6,4},{8,10},{10,8},{12,14},{14,12},{16,18},{18,... | collective-permute-start | bytes 786440 | tf_op jit(solution)/shard_map/ppermute | solution.py:33
  27.4 2.1 %copy-start.2 = (bf16[256,256]{1,0:T(8,128)(2,1)S(1)}, bf16[256,256]{1,0:T(8,128)(2,1)}, u32[]{:S(2)}) copy-start(bf16[256,256]{1,0:T(8,128)(2,1)} %param.8) | copy-start | bytes 393220
  27.4 2.1 %copy-start.3 = (bf16[256,256]{1,0:T(8,128)(2,1)S(1)}, bf16[256,256]{1,0:T(8,128)(2,1)}, u32[]{:S(2)}) copy-start(bf16[256,256]{1,0:T(8,128)(2,1)} %param.7) | copy-start | bytes 393220
  27.9 1.6 %collective-permute-start.6 = (f32[2,128,256]{2,1,0:T(8,128)S(1)}, f32[2,128,256]{2,1,0:T(8,128)S(1)}, u32[]{:S(2)}, u32[]{:S(2)}) collective-permute-start(f32[2,128,256]{2,1,0:T(8,128)S(1)} %convolution_bitcast_fusion.1), channel_id=1, source_target_pairs={{0,1},{1,0},{2,3},{3,2},{4,5},{5,4},{6,7},{7,6},{8,9},{9,8},{10,11... | collective-permute-start | bytes 786440 | tf_op jit(solution)/shard_map/ppermute | solution.py:85
  31.0 8.8 %collective-permute-start.7 = (f32[128,256]{1,0:T(8,128)S(1)}, f32[128,256]{1,0:T(8,128)S(1)}, u32[]{:S(2)}, u32[]{:S(2)}) collective-permute-start(f32[128,256]{1,0:T(8,128)S(1)} %constant_dynamic-slice_fusion), channel_id=1, source_target_pairs={{0,16},{2,18},{4,20},{6,22},{8,24},{10,26},{12,28},{14,30},{16,0},... | collective-permute-start | bytes 393224 | tf_op jit(solution)/shard_map/ppermute | solution.py:61
  31.4 9.3 %collective-permute-start.13 = (bf16[2,2,128,256]{3,2,1,0:T(8,128)(2,1)S(1)}, bf16[2,2,128,256]{3,2,1,0:T(8,128)(2,1)S(1)}, u32[]{:S(2)}, u32[]{:S(2)}) collective-permute-start(bf16[2,2,128,256]{3,2,1,0:T(8,128)(2,1)S(1)} %fusion.6), channel_id=1, source_target_pairs={{0,2},{2,0},{4,6},{6,4},{8,10},{10,8},{12,14},{14,12},{16,18},{18,... | collective-permute-start | bytes 786440 | tf_op jit(solution)/shard_map/ppermute | solution.py:53
  33.0 13.6 %collective-permute-start.14 = (bf16[2,2,128,256]{3,2,1,0:T(8,128)(2,1)S(1)}, bf16[2,2,128,256]{3,2,1,0:T(8,128)(2,1)S(1)}, u32[]{:S(2)}, u32[]{:S(2)}) collective-permute-start(bf16[2,2,128,256]{3,2,1,0:T(8,128)(2,1)S(1)} %get-tuple-element.3), channel_id=1, source_target_pairs={{0,4},{2,6},{4,0},{6,2},{8,12},{10,14},{12,8},{14,10},{16,20},{18,... | collective-permute-start | bytes 786440 | tf_op jit(solution)/shard_map/ppermute | solution.py:54
  34.5 12.0 %collective-permute-start.15 = (bf16[2,2,128,256]{3,2,1,0:T(8,128)(2,1)S(1)}, bf16[2,2,128,256]{3,2,1,0:T(8,128)(2,1)S(1)}, u32[]{:S(2)}, u32[]{:S(2)}) collective-permute-start(bf16[2,2,128,256]{3,2,1,0:T(8,128)(2,1)S(1)} %get-tuple-element.4), channel_id=1, source_target_pairs={{0,6},{2,4},{4,2},{6,0},{8,14},{10,12},{12,10},{14,8},{16,22},{18,... | collective-permute-start | bytes 786440 | tf_op jit(solution)/shard_map/ppermute | solution.py:55
  39.8 9.2 %collective-permute-start.8 = (f32[128,256]{1,0:T(8,128)S(1)}, f32[128,256]{1,0:T(8,128)S(1)}, u32[]{:S(2)}, u32[]{:S(2)}) collective-permute-start(f32[128,256]{1,0:T(8,128)S(1)} %fusion.27), channel_id=1, source_target_pairs={{0,8},{2,10},{4,12},{6,14},{8,0},{10,2},{12,4},{14,6},{16,24},{18,... | collective-permute-start | bytes 393224 | tf_op jit(solution)/shard_map/ppermute | solution.py:61
  46.7 6.0 %collective-permute-start.16 = (bf16[2,128,256]{2,1,0:T(8,128)(2,1)S(1)}, bf16[2,128,256]{2,1,0:T(8,128)(2,1)S(1)}, u32[]{:S(2)}, u32[]{:S(2)}) collective-permute-start(bf16[2,128,256]{2,1,0:T(8,128)(2,1)S(1)} %fusion.8), channel_id=1, source_target_pairs={{0,8},{2,10},{4,12},{6,14},{8,0},{10,2},{12,4},{14,6},{16,24},{18,... | collective-permute-start | bytes 393224 | tf_op jit(solution)/shard_map/ppermute | solution.py:47
  49.1 6.4 %collective-permute-start.11 = (f32[128,256]{1,0:T(8,128)S(1)}, f32[128,256]{1,0:T(8,128)S(1)}, u32[]{:S(2)}, u32[]{:S(2)}) collective-permute-start(f32[128,256]{1,0:T(8,128)S(1)} %add.48), channel_id=1, source_target_pairs={{0,6},{2,4},{4,2},{6,0},{8,14},{10,12},{12,10},{14,8},{16,22},{18,... | collective-permute-start | bytes 393224 | tf_op jit(solution)/shard_map/ppermute | solution.py:65
  50.6 6.1 %collective-permute-start.10 = (f32[128,256]{1,0:T(8,128)S(1)}, f32[128,256]{1,0:T(8,128)S(1)}, u32[]{:S(2)}, u32[]{:S(2)}) collective-permute-start(f32[128,256]{1,0:T(8,128)S(1)} %add.48), channel_id=1, source_target_pairs={{0,4},{2,6},{4,0},{6,2},{8,12},{10,14},{12,8},{14,10},{16,20},{18,... | collective-permute-start | bytes 393224 | tf_op jit(solution)/shard_map/ppermute | solution.py:64
  51.8 5.0 %collective-permute-start.9 = (f32[128,256]{1,0:T(8,128)S(1)}, f32[128,256]{1,0:T(8,128)S(1)}, u32[]{:S(2)}, u32[]{:S(2)}) collective-permute-start(f32[128,256]{1,0:T(8,128)S(1)} %add.48), channel_id=1, source_target_pairs={{0,2},{2,0},{4,6},{6,4},{8,10},{10,8},{12,14},{14,12},{16,18},{18,... | collective-permute-start | bytes 393224 | tf_op jit(solution)/shard_map/ppermute | solution.py:63
  52.7 5.9 %collective-permute-start.17 = (bf16[128,256]{1,0:T(8,128)(2,1)S(1)}, bf16[128,256]{1,0:T(8,128)(2,1)S(1)}, u32[]{:S(2)}, u32[]{:S(2)}) collective-permute-start(bf16[128,256]{1,0:T(8,128)(2,1)S(1)} %fusion.12), channel_id=1, source_target_pairs={{0,16},{2,18},{4,20},{6,22},{8,24},{10,26},{12,28},{14,30},{16,0},... | collective-permute-start | bytes 196616 | tf_op jit(solution)/shard_map/ppermute | solution.py:47
  56.9 2.4 %collective-permute-start.12 = (f32[1,128,256]{2,1,0:T(8,128)S(1)}, f32[1,128,256]{2,1,0:T(8,128)S(1)}, u32[]{:S(2)}, u32[]{:S(2)}) collective-permute-start(f32[1,128,256]{2,1,0:T(8,128)S(1)} %add_bitcast_fusion), channel_id=1, source_target_pairs={{0,1},{1,0},{2,3},{3,2},{4,5},{5,4},{6,7},{7,6},{8,9},{9,8},{10,11... | collective-permute-start | bytes 393224 | tf_op jit(solution)/shard_map/ppermute | solution.py:93

commit v8 on v7

--- a/solution.py
+++ b/solution.py
@@ -70,13 +70,15 @@
     nb = bit_count(n)
     cur = rel
     if nb == 4:
-        pairs = [((0, 1), (3,)), ((2,), (2,)), ((3,), (0, 1))]
+        pairs = [((0, 1), (3,)), ((2,), (2,)), ((3,), (0,)), (None, (1,))]
     else:
         rounds = bit_rounds(nb)
         pairs = list(zip(rounds[::-1], rounds))
     for fg_bits, w_bits in pairs:
-        cur = scatter_round(cur, fg_bits, n, send_dtype)
-        w = sum_round(w, w_bits, n)
+        if fg_bits:
+            cur = scatter_round(cur, fg_bits, n, send_dtype)
+        if w_bits:
+            w = sum_round(w, w_bits, n)
     return cur, w
 
 

time: 60.2 us -> 58.9 us (0.978)
  waiting for transfers between devices: 31.3 us -> 30.1 us
    ppermute x2 -> x4, waiting for transfers between devices: 4.85 us -> 12.4 us  [sum_round(): return w + lax.ppermute(w, 'rows', pairs_of(n, 1 << bits[0]))]
    ppermute x1, waiting for transfers between devices: 5.86 us -> 0.01 us  [scatter_round(): lax.ppermute(part(1, 0).astype(send_dtype), 'rows', pairs_of(n, 1 << high))]
    ppermute x3 -> x0, starting transfers between devices: 3.55 us -> none  [the longest x1 1.56 us: sum_round(): got_both = lax.ppermute(w, 'rows', pairs_of(n, 1 << low | 1 << high))]
    ppermute x2 -> x4, starting transfers between devices: 0.43 us -> 3.57 us  [sum_round(): return w + lax.ppermute(w, 'rows', pairs_of(n, 1 << bits[0]))]
    ppermute x3 -> x0, waiting for transfers between devices: 2.41 us -> none  [the longest x1 1.27 us: sum_round(): got_high = lax.ppermute(w, 'rows', pairs_of(n, 1 << high))]
    ppermute x1, waiting for transfers between devices: 0.76 us -> 0.01 us  [scatter_round(): lax.ppermute(part(0, 1).astype(send_dtype), 'rows', pairs_of(n, 1 << low))]
  transfers between devices with their start and end apart: 18 -> 17, of which waited for: 12 -> 11; matrix products, arithmetic and copies ran while one was open for 6% -> 6% of each run, Pallas kernels for 0% -> 0%
where the time goes in v8:
time: 58.9 us; the launch traced here: 58.7 us
  waiting for transfers between devices  30.1 us (51%)
  starting transfers between devices  20.4 us (35%)
  other arithmetic  4.62 us (8%)
  matrix products  2.43 us (4%)
  between operations  0.85 us (1%)
    ppermute x4, waiting for transfers between devices, sum_round(): return w + lax.ppermute(w, 'rows', pairs_of(n, 1 << bits[0]))  12.4 us
    ppermute x2, waiting for transfers between devices, radix_gather(): got_high = lax.ppermute(held, 'rows', pairs_of(n, 1 << high))  12.2 us
    ppermute x2, starting transfers between devices, radix_gather(): got_both = lax.ppermute(held, 'rows', pairs_of(n, 1 << low | 1 << high))  6.55 us
    ppermute x2, starting transfers between devices, scatter_round(): lax.ppermute(send.astype(send_dtype), 'rows', pairs_of(n, 1 << bits[0]))  3.79 us
    ppermute x4, starting transfers between devices, sum_round(): return w + lax.ppermute(w, 'rows', pairs_of(n, 1 << bits[0]))  3.57 us
    ppermute x2, waiting for transfers between devices, scatter_round(): lax.ppermute(send.astype(send_dtype), 'rows', pairs_of(n, 1 << bits[0]))  1.93 us
    ppermute x2, starting transfers between devices, radix_gather(): got_high = lax.ppermute(held, 'rows', pairs_of(n, 1 << high))  1.59 us
    ppermute x1, starting transfers between devices, scatter_round(): lax.ppermute(part(1, 0).astype(send_dtype), 'rows', pairs_of(n, 1 << high))  1.58 us
  transfers between devices with their start and end apart: 17, of which 11 were waited for; matrix products, arithmetic and copies ran while one was open for 6% of the time, Pallas kernels for 0%

profile of v8, /device:TPU:0, one launch (start us, length us, event | category | flops | bytes accessed | tf_op | source)
XLA Modules:
  0.0 58.7 jit_solution(2986458337935727876)
XLA Ops:
  0.6 0.0 copy-start
  0.6 0.0 copy-start.1
  0.7 5.1 %collective-permute-start.2 = (bf16[1,1,1,1,128,256]{5,4,3,2,1,0:T(8,128)(2,1)}, bf16[1,1,1,1,128,256]{5,4,3,2,1,0:T(8,128)(2,1)S(1)}, u32[]{:S(2)}, u32[]{:S(2)}) collective-permute-start(bf16[1,1,1,1,128,256]{5,4,3,2,1,0:T(8,128)(2,1)} %bitcast.77), channel_id=1, source_target_pairs={{0,24},{2,26},{4,28},{6,30},{8,16},{10,18},{12,20},{14,22},{16,8},... | collective-permute-start | bytes 196616 | tf_op jit(solution)/shard_map/ppermute | solution.py:35
  5.8 0.0 collective-permute-start.1
  5.8 0.6 %collective-permute-start = (bf16[1,1,1,1,128,256]{5,4,3,2,1,0:T(8,128)(2,1)}, bf16[1,1,1,1,128,256]{5,4,3,2,1,0:T(8,128)(2,1)S(1)}, u32[]{:S(2)}, u32[]{:S(2)}) collective-permute-start(bf16[1,1,1,1,128,256]{5,4,3,2,1,0:T(8,128)(2,1)} %bitcast.79), channel_id=1, source_target_pairs={{0,8},{2,10},{4,12},{6,14},{8,0},{10,2},{12,4},{14,6},{16,24},{18,... | collective-permute-start | bytes 196616 | tf_op jit(solution)/shard_map/ppermute | solution.py:33
  6.4 0.7 %broadcast_xor_fusion = s32[2,1,16]{2,1,0:T(1,128)S(1)} fusion(s32[2,1,16]{2,1,0:T(1,128)} %param.10, s32[]{:T(128)S(6)} %axis_index.27), kind=kLoop, calls=%fused_computation.41 | loop fusion | flops 32 | bytes 260 | tf_op jit(solution)/shard_map/xor | solution.py:118
  7.1 0.7 %iota_compare_fusion.1 = pred[2,16]{1,0:T(4,128)(4,1)S(1)} fusion(s32[2]{0:T(128)} %bitcast.83), kind=kLoop, calls=%fused_computation.39 | loop fusion | flops 32 | bytes 40 | tf_op jit(solution)/shard_map/lt | solution.py:117
  7.8 0.8 %collective-permute-done.2 = bf16[1,1,1,1,128,256]{5,4,3,2,1,0:T(8,128)(2,1)S(1)} collective-permute-done((bf16[1,1,1,1,128,256]{5,4,3,2,1,0:T(8,128)(2,1)}, bf16[1,1,1,1,128,256]{5,4,3,2,1,0:T(8,128)(2,1)S(1)}, u32[]{:S(2)}, u32[]{:S(2)}) %collective-permute-start.2) | collective-permute-done | bytes 65568 | tf_op jit(solution)/shard_map/ppermute | solution.py:35
  8.6 3.0 %collective-permute-done.1 = bf16[1,1,1,1,128,256]{5,4,3,2,1,0:T(8,128)(2,1)S(1)} collective-permute-done((bf16[1,1,1,1,128,256]{5,4,3,2,1,0:T(8,128)(2,1)}, bf16[1,1,1,1,128,256]{5,4,3,2,1,0:T(8,128)(2,1)S(1)}, u32[]{:S(2)}, u32[]{:S(2)}) %collective-permute-start.1) | collective-permute-done | bytes 65568 | tf_op jit(solution)/shard_map/ppermute | solution.py:34
  11.6 0.0 collective-permute-done
  11.6 0.9 %maximum_maximum_fusion.1 = bf16[2,2,1,1,128,256]{5,4,3,2,1,0:T(8,128)(2,1)S(1)} fusion(bf16[1,1,1,1,128,256]{5,4,3,2,1,0:T(8,128)(2,1)S(1)} %collective-permute-done.2, bf16[1,1,1,1,128,256]{5,4,3,2,1,0:T(8,128)(2,1)S(1)} %collective-permute-done.1, bf16[1,1,1,1,128,256]{5,4,3,2,1,0:T(8,128)(2,1)S(1)} %collective-permute-done, ...), kind=kLoop, calls=%fused_computation.20 | loop fusion | flops 393216 | bytes 524288 | tf_op jit(solution)/shard_map/concatenate | solution.py:38
  12.5 1.6 %collective-permute-start.4 = (bf16[2,2,1,1,128,256]{5,4,3,2,1,0:T(8,128)(2,1)S(1)}, bf16[2,2,1,1,128,256]{5,4,3,2,1,0:T(8,128)(2,1)S(1)}, u32[]{:S(2)}, u32[]{:S(2)}) collective-permute-start(bf16[2,2,1,1,128,256]{5,4,3,2,1,0:T(8,128)(2,1)S(1)} %maximum_maximum_fusion.1), channel_id=1, source_target_pairs={{0,4},{2,6},{4,0},{6,2},{8,12},{10,14},{12,8},{14,10},{16,20},{18,... | collective-permute-start | bytes 786440 | tf_op jit(solution)/shard_map/ppermute | solution.py:34
  14.0 1.4 %collective-permute-start.5 = (bf16[2,2,1,1,128,256]{5,4,3,2,1,0:T(8,128)(2,1)S(1)}, bf16[2,2,1,1,128,256]{5,4,3,2,1,0:T(8,128)(2,1)S(1)}, u32[]{:S(2)}, u32[]{:S(2)}) collective-permute-start(bf16[2,2,1,1,128,256]{5,4,3,2,1,0:T(8,128)(2,1)S(1)} %maximum_maximum_fusion.1), channel_id=1, source_target_pairs={{0,6},{2,4},{4,2},{6,0},{8,14},{10,12},{12,10},{14,8},{16,22},{18,... | collective-permute-start | bytes 786440 | tf_op jit(solution)/shard_map/ppermute | solution.py:35
  15.5 0.5 collective-permute-start.3
  16.0 0.0 copy-done
  16.0 0.7 %fusion.2 = bf16[2,16,128,128]{3,1,2,0:T(8,128)(2,1)S(1)} fusion(bf16[2,16,128,128]{3,2,1,0:T(8,128)(2,1)S(1)} %bitcast.70, s32[2,16]{1,0:T(2,128)S(1)} %bitcast.82, pred[2,16]{1,0:T(4,128)(4,1)S(1)} %iota_compare_fusion.1), kind=kOutput, calls=%fused_computation.8 | convolution fusion | flops 16778240 | bytes 2097312 | tf_op jit(solution)/shard_map/tsq,tsab->tqab/dot_general | solution.py:120
  16.8 9.2 %collective-permute-done.4 = bf16[2,2,1,1,128,256]{5,4,3,2,1,0:T(8,128)(2,1)S(1)} collective-permute-done((bf16[2,2,1,1,128,256]{5,4,3,2,1,0:T(8,128)(2,1)S(1)}, bf16[2,2,1,1,128,256]{5,4,3,2,1,0:T(8,128)(2,1)S(1)}, u32[]{:S(2)}, u32[]{:S(2)}) %collective-permute-start.4) | collective-permute-done | bytes 262176 | tf_op jit(solution)/shard_map/ppermute | solution.py:34
  26.0 0.0 collective-permute-done.5
  26.0 1.3 %collective-permute-done.3 = bf16[2,2,1,1,128,256]{5,4,3,2,1,0:T(8,128)(2,1)S(1)} collective-permute-done((bf16[2,2,1,1,128,256]{5,4,3,2,1,0:T(8,128)(2,1)S(1)}, bf16[2,2,1,1,128,256]{5,4,3,2,1,0:T(8,128)(2,1)S(1)}, u32[]{:S(2)}, u32[]{:S(2)}) %collective-permute-start.3) | collective-permute-done | bytes 262176 | tf_op jit(solution)/shard_map/ppermute | solution.py:33
  27.3 0.0 copy-done.1
  27.3 0.1 maximum_maximum_fusion
  27.4 0.0 copy-start.2
  27.4 0.0 copy-start.3
  27.4 0.4 convolution_bitcast_fusion.1
  27.9 0.1 collective-permute-start.6
  28.0 1.5 %collective-permute-done.6 = f32[2,128,256]{2,1,0:T(8,128)S(1)} collective-permute-done((f32[2,128,256]{2,1,0:T(8,128)S(1)}, f32[2,128,256]{2,1,0:T(8,128)S(1)}, u32[]{:S(2)}, u32[]{:S(2)}) %collective-permute-start.6) | collective-permute-done | bytes 262176 | tf_op jit(solution)/shard_map/ppermute | solution.py:87
  29.5 0.0 copy-done.2
  29.5 0.0 copy-done.3
  29.5 0.3 multiply_convert_fusion
  29.8 0.2 fusion.18
  30.0 0.2 convolution_convert_fusion
  30.3 0.5 convolution_bitcast_fusion
  30.8 0.1 fusion.4
  30.9 0.1 copy_bitcast_fusion
  31.0 0.4 collective-permute-start.7
  31.4 1.6 %collective-permute-start.12 = (bf16[2,2,128,256]{3,2,1,0:T(8,128)(2,1)S(1)}, bf16[2,2,128,256]{3,2,1,0:T(8,128)(2,1)S(1)}, u32[]{:S(2)}, u32[]{:S(2)}) collective-permute-start(bf16[2,2,128,256]{3,2,1,0:T(8,128)(2,1)S(1)} %fusion.6), channel_id=1, source_target_pairs={{0,2},{2,0},{4,6},{6,4},{8,10},{10,8},{12,14},{14,12},{16,18},{18,... | collective-permute-start | bytes 786440 | tf_op jit(solution)/shard_map/ppermute | solution.py:53
  33.0 1.6 %collective-permute-start.13 = (bf16[2,2,128,256]{3,2,1,0:T(8,128)(2,1)S(1)}, bf16[2,2,128,256]{3,2,1,0:T(8,128)(2,1)S(1)}, u32[]{:S(2)}, u32[]{:S(2)}) collective-permute-start(bf16[2,2,128,256]{3,2,1,0:T(8,128)(2,1)S(1)} %get-tuple-element.3), channel_id=1, source_target_pairs={{0,4},{2,6},{4,0},{6,2},{8,12},{10,14},{12,8},{14,10},{16,20},{18,... | collective-permute-start | bytes 786440 | tf_op jit(solution)/shard_map/ppermute | solution.py:54
  34.5 0.5 collective-permute-start.14
  35.0 4.8 %collective-permute-done.7 = f32[128,256]{1,0:T(8,128)S(1)} collective-permute-done((f32[128,256]{1,0:T(8,128)S(1)}, f32[128,256]{1,0:T(8,128)S(1)}, u32[]{:S(2)}, u32[]{:S(2)}) %collective-permute-start.7) | collective-permute-done | bytes 131104 | tf_op jit(solution)/shard_map/ppermute | solution.py:61
  39.8 0.1 collective-permute-start.8
  39.9 5.4 %collective-permute-done.8 = f32[128,256]{1,0:T(8,128)S(1)} collective-permute-done((f32[128,256]{1,0:T(8,128)S(1)}, f32[128,256]{1,0:T(8,128)S(1)}, u32[]{:S(2)}, u32[]{:S(2)}) %collective-permute-start.8) | collective-permute-done | bytes 131104 | tf_op jit(solution)/shard_map/ppermute | solution.py:61
  45.3 1.6 %collective-permute-start.9 = (f32[128,256]{1,0:T(8,128)S(1)}, f32[128,256]{1,0:T(8,128)S(1)}, u32[]{:S(2)}, u32[]{:S(2)}) collective-permute-start(f32[128,256]{1,0:T(8,128)S(1)} %add.45), channel_id=1, source_target_pairs={{0,2},{2,0},{4,6},{6,4},{8,10},{10,8},{12,14},{14,12},{16,18},{18,... | collective-permute-start | bytes 393224 | tf_op jit(solution)/shard_map/ppermute | solution.py:61
  46.9 0.0 collective-permute-done.12
  46.9 0.0 collective-permute-done.13
  46.9 0.0 collective-permute-done.14
  46.9 0.1 fusion.5
  47.0 1.4 %collective-permute-start.15 = (bf16[2,128,256]{2,1,0:T(8,128)(2,1)S(1)}, bf16[2,128,256]{2,1,0:T(8,128)(2,1)S(1)}, u32[]{:S(2)}, u32[]{:S(2)}) collective-permute-start(bf16[2,128,256]{2,1,0:T(8,128)(2,1)S(1)} %fusion.8), channel_id=1, source_target_pairs={{0,8},{2,10},{4,12},{6,14},{8,0},{10,2},{12,4},{14,6},{16,24},{18,... | collective-permute-start | bytes 393224 | tf_op jit(solution)/shard_map/ppermute | solution.py:47
  48.5 0.6 %fusion.11 = bf16[128,256]{1,0:T(8,128)(2,1)} fusion(f32[256,256]{1,0:T(8,128)S(1)} %get-tuple-element.6, s32[]{:T(128)S(6)} %select_n.16, f32[256,256]{1,0:T(8,128)S(1)} %get-tuple-element.7), kind=kLoop, calls=%fused_computation.31 | loop fusion | flops 65536 | bytes 327684 | tf_op jit(solution)/shard_map/convert_element_type | solution.py:130
  49.1 1.3 %collective-permute-done.9 = f32[128,256]{1,0:T(8,128)S(1)} collective-permute-done((f32[128,256]{1,0:T(8,128)S(1)}, f32[128,256]{1,0:T(8,128)S(1)}, u32[]{:S(2)}, u32[]{:S(2)}) %collective-permute-start.9) | collective-permute-done | bytes 131104 | tf_op jit(solution)/shard_map/ppermute | solution.py:61
  50.4 1.6 %collective-permute-start.10 = (f32[128,256]{1,0:T(8,128)S(1)}, f32[128,256]{1,0:T(8,128)S(1)}, u32[]{:S(2)}, u32[]{:S(2)}) collective-permute-start(f32[128,256]{1,0:T(8,128)S(1)} %add.46), channel_id=1, source_target_pairs={{0,4},{2,6},{4,0},{6,2},{8,12},{10,14},{12,8},{14,10},{16,20},{18,... | collective-permute-start | bytes 393224 | tf_op jit(solution)/shard_map/ppermute | solution.py:61
  52.0 0.1 collective-permute-done.15
  52.1 2.4 %collective-permute-start.16 = (bf16[128,256]{1,0:T(8,128)(2,1)S(1)}, bf16[128,256]{1,0:T(8,128)(2,1)S(1)}, u32[]{:S(2)}, u32[]{:S(2)}) collective-permute-start(bf16[128,256]{1,0:T(8,128)(2,1)S(1)} %fusion.12), channel_id=1, source_target_pairs={{0,16},{2,18},{4,20},{6,22},{8,24},{10,26},{12,28},{14,30},{16,0},... | collective-permute-start | bytes 196616 | tf_op jit(solution)/shard_map/ppermute | solution.py:47
  54.5 0.9 %collective-permute-done.10 = f32[128,256]{1,0:T(8,128)S(1)} collective-permute-done((f32[128,256]{1,0:T(8,128)S(1)}, f32[128,256]{1,0:T(8,128)S(1)}, u32[]{:S(2)}, u32[]{:S(2)}) %collective-permute-start.10) | collective-permute-done | bytes 131104 | tf_op jit(solution)/shard_map/ppermute | solution.py:61
  55.4 0.1 collective-permute-start.11
  55.5 1.8 %collective-permute-done.16 = bf16[128,256]{1,0:T(8,128)(2,1)S(1)} collective-permute-done((bf16[128,256]{1,0:T(8,128)(2,1)S(1)}, bf16[128,256]{1,0:T(8,128)(2,1)S(1)}, u32[]{:S(2)}, u32[]{:S(2)}) %collective-permute-start.16) | collective-permute-done | bytes 65568 | tf_op jit(solution)/shard_map/ppermute | solution.py:47
  57.4 0.6 %fusion.10 = bf16[128,256]{1,0:T(8,128)(2,1)} fusion(f32[2,128,256]{2,1,0:T(8,128)S(1)} %fusion.7, bf16[128,256]{1,0:T(8,128)(2,1)S(1)} %collective-permute-done.16), kind=kLoop, calls=%fused_computation.29 | loop fusion | flops 98304 | bytes 262144 | tf_op jit(solution)/shard_map/convert_element_type | solution.py:149
  58.0 0.0 collective-permute-done.11
  58.0 0.7 %maximum_select_fusion = f32[2,128,256]{2,1,0:T(8,128)} fusion(f32[1,128,256]{2,1,0:T(8,128)S(1)} %collective-permute-done.11, f32[1,128,256]{2,1,0:T(8,128)S(1)} %add_bitcast_fusion, pred[]{:T(512)S(6)} %eq.19), kind=kLoop, calls=%fused_computation.21 | loop fusion | flops 196608 | bytes 524289 | tf_op jit(solution)/shard_map/jit(_where)/select_n | solution.py:97
  (11 shorter events, 0.2 us)
Async XLA Ops:
  0.6 15.4 %copy-start = (bf16[2,1,16,128,128]{4,3,2,1,0:T(8,128)(2,1)S(1)}, bf16[2,1,16,128,128]{4,3,2,1,0:T(8,128)(2,1)}, u32[]{:S(2)}) copy-start(bf16[2,1,16,128,128]{4,3,2,1,0:T(8,128)(2,1)} %param.9) | copy-start | bytes 3145732
  0.6 26.6 %copy-start.1 = (bf16[128,256]{1,0:T(8,128)(2,1)S(1)}, bf16[128,256]{1,0:T(8,128)(2,1)}, u32[]{:S(2)}) copy-start(bf16[128,256]{1,0:T(8,128)(2,1)} %param.6) | copy-start | bytes 196612
  0.7 7.9 %collective-permute-start.2 = (bf16[1,1,1,1,128,256]{5,4,3,2,1,0:T(8,128)(2,1)}, bf16[1,1,1,1,128,256]{5,4,3,2,1,0:T(8,128)(2,1)S(1)}, u32[]{:S(2)}, u32[]{:S(2)}) collective-permute-start(bf16[1,1,1,1,128,256]{5,4,3,2,1,0:T(8,128)(2,1)} %bitcast.77), channel_id=1, source_target_pairs={{0,24},{2,26},{4,28},{6,30},{8,16},{10,18},{12,20},{14,22},{16,8},... | collective-permute-start | bytes 196616 | tf_op jit(solution)/shard_map/ppermute | solution.py:35
  5.8 5.8 %collective-permute-start.1 = (bf16[1,1,1,1,128,256]{5,4,3,2,1,0:T(8,128)(2,1)}, bf16[1,1,1,1,128,256]{5,4,3,2,1,0:T(8,128)(2,1)S(1)}, u32[]{:S(2)}, u32[]{:S(2)}) collective-permute-start(bf16[1,1,1,1,128,256]{5,4,3,2,1,0:T(8,128)(2,1)} %bitcast.78), channel_id=1, source_target_pairs={{0,16},{2,18},{4,20},{6,22},{8,24},{10,26},{12,28},{14,30},{16,0},... | collective-permute-start | bytes 196616 | tf_op jit(solution)/shard_map/ppermute | solution.py:34
  5.8 5.8 %collective-permute-start = (bf16[1,1,1,1,128,256]{5,4,3,2,1,0:T(8,128)(2,1)}, bf16[1,1,1,1,128,256]{5,4,3,2,1,0:T(8,128)(2,1)S(1)}, u32[]{:S(2)}, u32[]{:S(2)}) collective-permute-start(bf16[1,1,1,1,128,256]{5,4,3,2,1,0:T(8,128)(2,1)} %bitcast.79), channel_id=1, source_target_pairs={{0,8},{2,10},{4,12},{6,14},{8,0},{10,2},{12,4},{14,6},{16,24},{18,... | collective-permute-start | bytes 196616 | tf_op jit(solution)/shard_map/ppermute | solution.py:33
  12.5 13.6 %collective-permute-start.4 = (bf16[2,2,1,1,128,256]{5,4,3,2,1,0:T(8,128)(2,1)S(1)}, bf16[2,2,1,1,128,256]{5,4,3,2,1,0:T(8,128)(2,1)S(1)}, u32[]{:S(2)}, u32[]{:S(2)}) collective-permute-start(bf16[2,2,1,1,128,256]{5,4,3,2,1,0:T(8,128)(2,1)S(1)} %maximum_maximum_fusion.1), channel_id=1, source_target_pairs={{0,4},{2,6},{4,0},{6,2},{8,12},{10,14},{12,8},{14,10},{16,20},{18,... | collective-permute-start | bytes 786440 | tf_op jit(solution)/shard_map/ppermute | solution.py:34
  14.0 12.0 %collective-permute-start.5 = (bf16[2,2,1,1,128,256]{5,4,3,2,1,0:T(8,128)(2,1)S(1)}, bf16[2,2,1,1,128,256]{5,4,3,2,1,0:T(8,128)(2,1)S(1)}, u32[]{:S(2)}, u32[]{:S(2)}) collective-permute-start(bf16[2,2,1,1,128,256]{5,4,3,2,1,0:T(8,128)(2,1)S(1)} %maximum_maximum_fusion.1), channel_id=1, source_target_pairs={{0,6},{2,4},{4,2},{6,0},{8,14},{10,12},{12,10},{14,8},{16,22},{18,... | collective-permute-start | bytes 786440 | tf_op jit(solution)/shard_map/ppermute | solution.py:35
  15.5 11.8 %collective-permute-start.3 = (bf16[2,2,1,1,128,256]{5,4,3,2,1,0:T(8,128)(2,1)S(1)}, bf16[2,2,1,1,128,256]{5,4,3,2,1,0:T(8,128)(2,1)S(1)}, u32[]{:S(2)}, u32[]{:S(2)}) collective-permute-start(bf16[2,2,1,1,128,256]{5,4,3,2,1,0:T(8,128)(2,1)S(1)} %maximum_maximum_fusion.1), channel_id=1, source_target_pairs={{0,2},{2,0},{4,6},{6,4},{8,10},{10,8},{12,14},{14,12},{16,18},{18,... | collective-permute-start | bytes 786440 | tf_op jit(solution)/shard_map/ppermute | solution.py:33
  27.4 2.1 %copy-start.2 = (bf16[256,256]{1,0:T(8,128)(2,1)S(1)}, bf16[256,256]{1,0:T(8,128)(2,1)}, u32[]{:S(2)}) copy-start(bf16[256,256]{1,0:T(8,128)(2,1)} %param.8) | copy-start | bytes 393220
  27.4 2.1 %copy-start.3 = (bf16[256,256]{1,0:T(8,128)(2,1)S(1)}, bf16[256,256]{1,0:T(8,128)(2,1)}, u32[]{:S(2)}) copy-start(bf16[256,256]{1,0:T(8,128)(2,1)} %param.7) | copy-start | bytes 393220
  27.9 1.6 %collective-permute-start.6 = (f32[2,128,256]{2,1,0:T(8,128)S(1)}, f32[2,128,256]{2,1,0:T(8,128)S(1)}, u32[]{:S(2)}, u32[]{:S(2)}) collective-permute-start(f32[2,128,256]{2,1,0:T(8,128)S(1)} %convolution_bitcast_fusion.1), channel_id=1, source_target_pairs={{0,1},{1,0},{2,3},{3,2},{4,5},{5,4},{6,7},{7,6},{8,9},{9,8},{10,11... | collective-permute-start | bytes 786440 | tf_op jit(solution)/shard_map/ppermute | solution.py:87
  31.0 8.8 %collective-permute-start.7 = (f32[128,256]{1,0:T(8,128)S(1)}, f32[128,256]{1,0:T(8,128)S(1)}, u32[]{:S(2)}, u32[]{:S(2)}) collective-permute-start(f32[128,256]{1,0:T(8,128)S(1)} %constant_dynamic-slice_fusion), channel_id=1, source_target_pairs={{0,16},{2,18},{4,20},{6,22},{8,24},{10,26},{12,28},{14,30},{16,0},... | collective-permute-start | bytes 393224 | tf_op jit(solution)/shard_map/ppermute | solution.py:61
  31.4 15.5 %collective-permute-start.12 = (bf16[2,2,128,256]{3,2,1,0:T(8,128)(2,1)S(1)}, bf16[2,2,128,256]{3,2,1,0:T(8,128)(2,1)S(1)}, u32[]{:S(2)}, u32[]{:S(2)}) collective-permute-start(bf16[2,2,128,256]{3,2,1,0:T(8,128)(2,1)S(1)} %fusion.6), channel_id=1, source_target_pairs={{0,2},{2,0},{4,6},{6,4},{8,10},{10,8},{12,14},{14,12},{16,18},{18,... | collective-permute-start | bytes 786440 | tf_op jit(solution)/shard_map/ppermute | solution.py:53
  33.0 13.9 %collective-permute-start.13 = (bf16[2,2,128,256]{3,2,1,0:T(8,128)(2,1)S(1)}, bf16[2,2,128,256]{3,2,1,0:T(8,128)(2,1)S(1)}, u32[]{:S(2)}, u32[]{:S(2)}) collective-permute-start(bf16[2,2,128,256]{3,2,1,0:T(8,128)(2,1)S(1)} %get-tuple-element.3), channel_id=1, source_target_pairs={{0,4},{2,6},{4,0},{6,2},{8,12},{10,14},{12,8},{14,10},{16,20},{18,... | collective-permute-start | bytes 786440 | tf_op jit(solution)/shard_map/ppermute | solution.py:54
  34.5 12.4 %collective-permute-start.14 = (bf16[2,2,128,256]{3,2,1,0:T(8,128)(2,1)S(1)}, bf16[2,2,128,256]{3,2,1,0:T(8,128)(2,1)S(1)}, u32[]{:S(2)}, u32[]{:S(2)}) collective-permute-start(bf16[2,2,128,256]{3,2,1,0:T(8,128)(2,1)S(1)} %get-tuple-element.4), channel_id=1, source_target_pairs={{0,6},{2,4},{4,2},{6,0},{8,14},{10,12},{12,10},{14,8},{16,22},{18,... | collective-permute-start | bytes 786440 | tf_op jit(solution)/shard_map/ppermute | solution.py:55
  39.8 5.5 %collective-permute-start.8 = (f32[128,256]{1,0:T(8,128)S(1)}, f32[128,256]{1,0:T(8,128)S(1)}, u32[]{:S(2)}, u32[]{:S(2)}) collective-permute-start(f32[128,256]{1,0:T(8,128)S(1)} %fusion.27), channel_id=1, source_target_pairs={{0,8},{2,10},{4,12},{6,14},{8,0},{10,2},{12,4},{14,6},{16,24},{18,... | collective-permute-start | bytes 393224 | tf_op jit(solution)/shard_map/ppermute | solution.py:61
  45.3 5.0 %collective-permute-start.9 = (f32[128,256]{1,0:T(8,128)S(1)}, f32[128,256]{1,0:T(8,128)S(1)}, u32[]{:S(2)}, u32[]{:S(2)}) collective-permute-start(f32[128,256]{1,0:T(8,128)S(1)} %add.45), channel_id=1, source_target_pairs={{0,2},{2,0},{4,6},{6,4},{8,10},{10,8},{12,14},{14,12},{16,18},{18,... | collective-permute-start | bytes 393224 | tf_op jit(solution)/shard_map/ppermute | solution.py:61
  47.0 5.0 %collective-permute-start.15 = (bf16[2,128,256]{2,1,0:T(8,128)(2,1)S(1)}, bf16[2,128,256]{2,1,0:T(8,128)(2,1)S(1)}, u32[]{:S(2)}, u32[]{:S(2)}) collective-permute-start(bf16[2,128,256]{2,1,0:T(8,128)(2,1)S(1)} %fusion.8), channel_id=1, source_target_pairs={{0,8},{2,10},{4,12},{6,14},{8,0},{10,2},{12,4},{14,6},{16,24},{18,... | collective-permute-start | bytes 393224 | tf_op jit(solution)/shard_map/ppermute | solution.py:47
  50.4 5.0 %collective-permute-start.10 = (f32[128,256]{1,0:T(8,128)S(1)}, f32[128,256]{1,0:T(8,128)S(1)}, u32[]{:S(2)}, u32[]{:S(2)}) collective-permute-start(f32[128,256]{1,0:T(8,128)S(1)} %add.46), channel_id=1, source_target_pairs={{0,4},{2,6},{4,0},{6,2},{8,12},{10,14},{12,8},{14,10},{16,20},{18,... | collective-permute-start | bytes 393224 | tf_op jit(solution)/shard_map/ppermute | solution.py:61
  52.1 5.2 %collective-permute-start.16 = (bf16[128,256]{1,0:T(8,128)(2,1)S(1)}, bf16[128,256]{1,0:T(8,128)(2,1)S(1)}, u32[]{:S(2)}, u32[]{:S(2)}) collective-permute-start(bf16[128,256]{1,0:T(8,128)(2,1)S(1)} %fusion.12), channel_id=1, source_target_pairs={{0,16},{2,18},{4,20},{6,22},{8,24},{10,26},{12,28},{14,30},{16,0},... | collective-permute-start | bytes 196616 | tf_op jit(solution)/shard_map/ppermute | solution.py:47
  55.4 2.6 %collective-permute-start.11 = (f32[1,128,256]{2,1,0:T(8,128)S(1)}, f32[1,128,256]{2,1,0:T(8,128)S(1)}, u32[]{:S(2)}, u32[]{:S(2)}) collective-permute-start(f32[1,128,256]{2,1,0:T(8,128)S(1)} %add_bitcast_fusion), channel_id=1, source_target_pairs={{0,1},{1,0},{2,3},{3,2},{4,5},{5,4},{6,7},{7,6},{8,9},{9,8},{10,11... | collective-permute-start | bytes 393224 | tf_op jit(solution)/shard_map/ppermute | solution.py:95
